TPU v7x, 128 devices: a whole 4x4x4 slice. The times are simulated.
128 devices in a mesh: fsdp: 32 (over y, z, core), seq: 4 (over x).
Axes of the slice: x: 4, y: 4, z: 4, core: 2. Of those that a mesh axis runs over, the one named last changes fastest.
Arguments:
- draft_tokens: bfloat16 [32768, 2048], P('fsdp'), may hold values from -6 to 6
- draft_gate: bfloat16 [2048, 4096], P('fsdp', 'seq'), may hold values from -0.125 to 0.125
- draft_up: bfloat16 [2048, 4096], P('fsdp', 'seq'), may hold values from -0.125 to 0.125
- draft_head: float32 [4096], P('seq'), may hold values from -0.75 to 0.75
- verifier_rows: bfloat16 [32768, 8192], P(('fsdp', 'seq')), may hold values from -6 to 6
- norm_gain: float32 [8192], replicated, may hold values from 0.5 to 1.5
- key_weight: bfloat16 [8192, 512], P('fsdp'), may hold values from -0.06629126 to 0.06629126
- value_weight: bfloat16 [8192, 512], P('fsdp'), may hold values from -0.0625 to 0.0625
- pool_query: float32 [4, 4, 128], replicated, may hold values from -32 to 32
- flags: int32 [1024], P(('fsdp', 'seq')), may hold values from 0 to 1, as said below
- owner: int32 [1024], P(('fsdp', 'seq')), may hold values from 0 to 3
Outputs:
- draft_score: float32 [1024], P(('fsdp', 'seq'))
- verdict: bfloat16 [1024, 512], P(('fsdp', 'seq'))
Inputs may be any that keep to these rules, and one draw needn't show every extreme that they name: `flags`: on the 8 segments of one device, at most 4 flagged segments share an owner lane, and on every device exactly 4 flagged segments share one lane.
All inputs are finite; a program needn't handle non-finite values.
Results may differ from a plain program's by a relative error of at most 0.009.
Values may be sent and summed in bfloat16 or wider, within the bound.
No kernel may reach another device: no remote copies, remote signals or barrier semaphores. Data moves between devices by JAX's collectives and lax.ppermute only.
A program may use at most 128 MiB of HBM per device.

v0:
```python
import math

import jax
import jax.numpy as jnp
from jax import lax
from jax.sharding import PartitionSpec as P

KVH = 4
HD = 128
SEGL = 32


eps = 1e-05


def normalize_rows(rows, norm_gain):
    values = rows.astype(jnp.float32)
    scale = lax.rsqrt(jnp.mean(values * values, axis=-1, keepdims=True) + eps)
    return (values * scale * norm_gain).astype(jnp.bfloat16)


def segment_pool(seg_keys, seg_values, queries, head_size):
    scores = jnp.einsum(
        "sthd,shd->sth", seg_keys, queries, precision=lax.Precision.HIGHEST
    ) / math.sqrt(head_size)
    scores = scores - jnp.max(scores, axis=1, keepdims=True)
    weights = jnp.exp(scores)
    weights = weights / jnp.sum(weights, axis=1, keepdims=True)
    summary_key = jnp.einsum("sth,sthd->shd", weights, seg_keys, precision=lax.Precision.HIGHEST)
    summary_value = jnp.einsum(
        "sth,sthd->shd", weights, seg_values, precision=lax.Precision.HIGHEST
    )
    return (summary_key, summary_value)


def cross_pool(query_keys, key_all, value_all, live_all, head_size):
    scores = jnp.einsum(
        "jhd,ihd->jhi", query_keys, key_all, precision=lax.Precision.HIGHEST
    ) / math.sqrt(head_size)
    scores = jnp.where(live_all[None, None, :], scores, -1e30)
    highest = jnp.max(scores, axis=2, keepdims=True)
    weights = jnp.where(live_all[None, None, :], jnp.exp(scores - highest), 0.0)
    total = jnp.sum(weights, axis=2, keepdims=True)
    return jnp.einsum("jhi,ihd->jhd", weights, value_all, precision=lax.Precision.HIGHEST) / total


def project_pair(row_block, pieces):
    return (
        jnp.dot(row_block, pieces[0], preferred_element_type=jnp.float32),
        jnp.dot(row_block, pieces[1], preferred_element_type=jnp.float32),
    )


def local(
    draft_tokens,
    draft_gate,
    draft_up,
    draft_head,
    verifier_rows,
    norm_gain,
    key_weight,
    value_weight,
    pool_query,
    flags,
    owner,
):
    seg_count = flags.shape[0]
    gate, upward = project_pair(
        draft_tokens,
        (
            lax.all_gather(draft_gate, "fsdp", axis=0, tiled=True),
            lax.all_gather(draft_up, "fsdp", axis=0, tiled=True),
        ),
    )
    partial_scores = jnp.sum(jax.nn.silu(gate) * upward * draft_head[None, :], axis=1)
    own_scores = lax.psum_scatter(partial_scores, "seq", scatter_dimension=0, tiled=True)
    draft_score = jnp.mean(own_scores.reshape(seg_count, SEGL), axis=1)
    normed = normalize_rows(verifier_rows, norm_gain)
    seg_keys, seg_values = project_pair(
        normed,
        (
            lax.all_gather(key_weight, "fsdp", axis=0, tiled=True),
            lax.all_gather(value_weight, "fsdp", axis=0, tiled=True),
        ),
    )
    lane_pick = (
        owner[:, None] == jnp.arange(pool_query.shape[0], dtype=jnp.int32)[None, :]
    ).astype(jnp.float32)
    queries = jnp.einsum("sc,chd->shd", lane_pick, pool_query, precision=lax.Precision.HIGHEST)
    summary_key, summary_value = segment_pool(
        seg_keys.reshape(seg_count, SEGL, KVH, HD),
        seg_values.reshape(seg_count, SEGL, KVH, HD),
        queries,
        HD,
    )
    live_own = flags.astype(jnp.float32)
    key_all, value_all, live_all = (
        lax.all_gather(summary_key.reshape(seg_count, KVH * HD), "seq", axis=0, tiled=True),
        lax.all_gather(summary_value.reshape(seg_count, KVH * HD), "seq", axis=0, tiled=True),
        lax.all_gather(live_own, "seq", axis=0, tiled=True),
    )
    pooled = cross_pool(
        summary_key,
        key_all.reshape(-1, KVH, HD),
        value_all.reshape(-1, KVH, HD),
        live_all > 0.5,
        HD,
    )
    own_pooled = pooled.reshape(seg_count, KVH * HD)
    verdict = jnp.where(
        flags[:, None] == 1, jax.nn.sigmoid(draft_score)[:, None] * own_pooled, 0.0
    ).astype(jnp.bfloat16)
    return (draft_score, verdict)


def solution(mesh):
    return jax.shard_map(
        local,
        mesh=mesh,
        in_specs=(
            P("fsdp", None),
            P("fsdp", "seq"),
            P("fsdp", "seq"),
            P("seq"),
            P(("fsdp", "seq"), None),
            P(),
            P("fsdp", None),
            P("fsdp", None),
            P(),
            P(("fsdp", "seq")),
            P(("fsdp", "seq")),
        ),
        out_specs=(P(("fsdp", "seq")), P(("fsdp", "seq"), None)),
        check_vma=False,
    )
```

profile of v0, /device:TPU:0, one launch (start us, length us, event | category | flops | bytes accessed | tf_op | source)
XLA Modules:
  0.0 243.5 jit_solution(6076633560900266448)
XLA Ops:
  7.2 0.7 all-gather.5.cloned.1.call-update
  8.0 0.7 all-gather.7.cloned.1.call-update
  8.7 0.7 all-gather.9.cloned.1.call-update
  10.0 1.3 fusion.44
  12.6 0.9 convolution_bitcast_fusion.1
  13.5 0.7 broadcast_compare_fusion.1
  14.1 0.7 convert_dynamic-update-slice_fusion
  14.9 3.1 %fusion.1 = f32[256]{0:T(256)S(1)} fusion(bf16[256,8192]{1,0:T(8,128)(2,1)} %param.15), kind=kLoop, calls=%fused_computation.3 | loop fusion | flops 6291200 | bytes 4195328 | tf_op jit(solution)/shard_map/reduce_sum | solution.py:18
  18.0 41.0 %all-gather.5.cloned.1.call-done = bf16[2048,1024]{1,0:T(8,128)(2,1)} async-done(((bf16[64,1024]{1,0:T(8,128)(2,1)}), bf16[2048,1024]{1,0:T(8,128)(2,1)}) %all-gather.5.cloned.1.call-update) | async-done | bytes 4194320 | tf_op jit(solution)/shard_map/all_gather | solution.py:71
  59.0 10.0 %fusion.47 = f32[1024,1024]{0,1:T(8,128)} fusion(bf16[1024,2048]{1,0:T(8,128)(2,1)} %param.11, bf16[2048,1024]{1,0:T(8,128)(2,1)} %all-gather.5.cloned.1.call-done), kind=kOutput, calls=%fused_computation.63 | convolution fusion | flops 4294967296 | bytes 12582912 | tf_op jit(solution)/shard_map/dot_general | solution.py:49
  69.0 37.8 %all-gather.7.cloned.1.call-done = bf16[2048,1024]{1,0:T(8,128)(2,1)} async-done(((bf16[64,1024]{1,0:T(8,128)(2,1)}), bf16[2048,1024]{1,0:T(8,128)(2,1)}) %all-gather.7.cloned.1.call-update) | async-done | bytes 4194320 | tf_op jit(solution)/shard_map/all_gather | solution.py:72
  106.7 10.1 %multiply_reduce_fusion = f32[1024]{0:T(1024)S(1)} fusion(f32[1024,1024]{0,1:T(8,128)} %fusion.47, bf16[1024,2048]{1,0:T(8,128)(2,1)} %param.11, bf16[2048,1024]{1,0:T(8,128)(2,1)} %all-gather.7.cloned.1.call-done, f32[1024]{0:T(1024)S(1)} %copy-done.2), kind=kOutput, calls=%fused_computation.6 | convolution fusion | flops 4302306304 | bytes 12591104 | tf_op jit(solution)/shard_map/dot_general | solution.py:50
  116.9 10.7 %all-reduce.2 = (f32[1024]{0:T(1024)S(1)}, f32[32]{0:T(128)S(1)}) all-reduce(f32[1024]{0:T(1024)S(1)} %multiply_reduce_fusion, f32[32]{0:T(128)S(1)} %convert_dynamic-update-slice_fusion), channel_id=2, replica_groups=mesh['fsdp'=32,'seq'=4] {'seq'}, use_global_device_ids=true, to_apply=%region_1.2.clone | all-reduce | flops 1056 | bytes 8448
  128.4 32.8 %all-gather.9.cloned.1.call-done = bf16[8192,512]{1,0:T(8,128)(2,1)} async-done(((bf16[256,512]{1,0:T(8,128)(2,1)}), bf16[8192,512]{1,0:T(8,128)(2,1)}) %all-gather.9.cloned.1.call-update) | async-done | bytes 8388624 | tf_op jit(solution)/shard_map/all_gather | solution.py:82
  161.2 7.0 %fusion.6 = f32[256,512]{1,0:T(8,128)S(1)} fusion(bf16[8192,512]{1,0:T(8,128)(2,1)} %all-gather.9.cloned.1.call-done, bf16[256,8192]{1,0:T(8,128)(2,1)} %param.15, f32[8192]{0:T(1024)S(1)} %copy-done.1, f32[256]{0:T(256)S(1)} %add_rsqrt_fusion), kind=kOutput, calls=%fused_computation.8 | convolution fusion | flops 2155872256 | bytes 13140992 | tf_op jit(solution)/shard_map/dot_general | solution.py:49
  168.4 0.9 fusion.21
  169.3 0.7 fusion.45
  170.1 0.5 fusion.19
  170.6 12.2 %all_gather.27 = f32[32,512]{1,0:T(8,128)S(1)} all-gather(f32[8,512]{1,0:T(8,128)S(1)} %bitcast.83), channel_id=1, replica_groups=mesh['fsdp'=32,'seq'=4] {'seq'}, dimensions={0}, use_global_device_ids=true | all-gather | bytes 81920 | tf_op jit(solution)/shard_map/all_gather | solution.py:98
  182.8 32.9 %all-gather.11.cloned.1.call-done = bf16[8192,512]{1,0:T(8,128)(2,1)} async-done(((bf16[256,512]{1,0:T(8,128)(2,1)}), bf16[8192,512]{1,0:T(8,128)(2,1)}) %all-gather.11.cloned.1.call-update) | async-done | bytes 8388624 | tf_op jit(solution)/shard_map/all_gather | solution.py:83
  215.7 7.0 %fusion.4 = f32[256,512]{1,0:T(8,128)S(1)} fusion(bf16[8192,512]{1,0:T(8,128)(2,1)} %all-gather.11.cloned.1.call-done, bf16[256,8192]{1,0:T(8,128)(2,1)} %param.15, f32[8192]{0:T(1024)S(1)} %copy-done.1, f32[256]{0:T(256)S(1)} %add_rsqrt_fusion), kind=kOutput, calls=%fused_computation.7 | convolution fusion | flops 2155872256 | bytes 13140992 | tf_op jit(solution)/shard_map/dot_general | solution.py:50
  222.9 0.5 fusion.17
  223.5 12.2 %all_gather.25 = f32[32,512]{1,0:T(8,128)S(1)} all-gather(f32[8,512]{1,0:T(8,128)S(1)} %bitcast.82), channel_id=1, replica_groups=mesh['fsdp'=32,'seq'=4] {'seq'}, dimensions={0}, use_global_device_ids=true | all-gather | bytes 81920 | tf_op jit(solution)/shard_map/all_gather | solution.py:99
  236.1 0.9 fusion.16
  (25 shorter events, 2.4 us)
Async XLA Ops:
  7.2 5.4 %copy-start = (f32[4,4,128]{2,1,0:T(4,128)S(1)}, f32[4,4,128]{2,1,0:T(4,128)}, u32[]{:S(2)}) copy-start(f32[4,4,128]{2,1,0:T(4,128)} %param.19) | copy-start | bytes 24580
  7.2 51.8 %all-gather.5.cloned.1.call-start = ((), (), s32[]{:S(2)}) async-start(), calls=%async_computation | async-start | bytes 4325376 | tf_op jit(solution)/shard_map/all_gather | solution.py:71
  7.9 98.8 %all-gather.7.cloned.1.call-start = ((), (), s32[]{:S(2)}) async-start(), calls=%async_computation.1 | async-start | bytes 4325376 | tf_op jit(solution)/shard_map/all_gather | solution.py:72
  8.7 152.5 %all-gather.9.cloned.1.call-start = ((), (), s32[]{:S(2)}) async-start(), calls=%async_computation.2 | async-start | bytes 8650752 | tf_op jit(solution)/shard_map/all_gather | solution.py:82
  9.4 206.3 %all-gather.11.cloned.1.call-start = ((), (), s32[]{:S(2)}) async-start(), calls=%async_computation.3 | async-start | bytes 8650752 | tf_op jit(solution)/shard_map/all_gather | solution.py:83
  18.0 88.7 %copy-start.2 = (f32[1024]{0:T(1024)S(1)}, f32[1024]{0:T(1024)}, u32[]{:S(2)}) copy-start(f32[1024]{0:T(1024)} %param.14) | copy-start | bytes 12292
  69.0 92.2 %copy-start.1 = (f32[8192]{0:T(1024)S(1)}, f32[8192]{0:T(1024)}, u32[]{:S(2)}) copy-start(f32[8192]{0:T(1024)} %param.16) | copy-start | bytes 98308
Sparse Core Ops, SparseCore 0:
  10.2 48.6 all-gather.4
  61.2 45.4 all-gather.6
  109.0 52.1 all-gather.8
  163.3 52.3 all-gather.10
where the time goes:
time: 244 us; the launch traced here: 243 us
  waiting for transfers between devices  147 us (60%)
  matrix products  38.2 us (16%)
  blocking collectives  35 us (14%)
  between operations  15.2 us (6%)
  other arithmetic  6.1 us (2%)
    all_gather x1, waiting for transfers between devices, local(): lax.all_gather(draft_gate, 'fsdp', axis=0, tiled=True)  41 us
    all_gather x1, waiting for transfers between devices, local(): lax.all_gather(draft_up, 'fsdp', axis=0, tiled=True)  37.8 us
    all_gather x1, waiting for transfers between devices, local(): lax.all_gather(value_weight, 'fsdp', axis=0, tiled=True)  32.9 us
    all_gather x1, waiting for transfers between devices, local(): lax.all_gather(key_weight, 'fsdp', axis=0, tiled=True)  32.8 us
    dot_general x2, matrix products, project_pair(): jnp.dot(row_block, pieces[1], preferred_element_type=jnp.float32)  17.2 us
    dot_general x2, matrix products, project_pair(): jnp.dot(row_block, pieces[0], preferred_element_type=jnp.float32)  17 us
    all_gather x1, blocking collectives, local(): lax.all_gather(summary_value.reshape(seg_count, KVH * HD), 'seq', axis=0,...  12.2 us
    all_gather x1, blocking collectives, local(): lax.all_gather(summary_key.reshape(seg_count, KVH * HD), 'seq', axis=0, t...  12.2 us
  transfers between devices with their start and end apart: 4, of which 4 were waited for; matrix products, arithmetic and copies ran while one was open for 15% of the time, Pallas kernels for 0%

commit v1 on v0

--- a/solution.py
+++ b/solution.py
@@ -44,13 +44,6 @@
     return jnp.einsum("jhi,ihd->jhd", weights, value_all, precision=lax.Precision.HIGHEST) / total
 
 
-def project_pair(row_block, pieces):
-    return (
-        jnp.dot(row_block, pieces[0], preferred_element_type=jnp.float32),
-        jnp.dot(row_block, pieces[1], preferred_element_type=jnp.float32),
-    )
-
-
 def local(
     draft_tokens,
     draft_gate,
@@ -65,24 +58,27 @@
     owner,
 ):
     seg_count = flags.shape[0]
-    gate, upward = project_pair(
-        draft_tokens,
-        (
-            lax.all_gather(draft_gate, "fsdp", axis=0, tiled=True),
-            lax.all_gather(draft_up, "fsdp", axis=0, tiled=True),
-        ),
-    )
+    n_seq = lax.axis_size("seq")
+    n_fsdp = lax.axis_size("fsdp")
+    d_rows, d_cols = draft_gate.shape
+    v_rows = key_weight.shape[0]
+    kv_cols = key_weight.shape[1]
+    kv_block = jnp.concatenate([key_weight, value_weight], axis=1)
+    kv_block = kv_block.reshape(-1, d_cols)
+    block = jnp.concatenate([draft_gate, draft_up, kv_block], axis=0)
+    gathered = lax.all_gather(block, "fsdp", axis=0, tiled=False)
+    gate_w = gathered[:, :d_rows].reshape(n_fsdp * d_rows, d_cols)
+    up_w = gathered[:, d_rows : 2 * d_rows].reshape(n_fsdp * d_rows, d_cols)
+    kv_w = gathered[:, 2 * d_rows :].reshape(n_fsdp * v_rows, 2 * kv_cols)
+
+    gate = jnp.dot(draft_tokens, gate_w, preferred_element_type=jnp.float32)
+    upward = jnp.dot(draft_tokens, up_w, preferred_element_type=jnp.float32)
     partial_scores = jnp.sum(jax.nn.silu(gate) * upward * draft_head[None, :], axis=1)
-    own_scores = lax.psum_scatter(partial_scores, "seq", scatter_dimension=0, tiled=True)
-    draft_score = jnp.mean(own_scores.reshape(seg_count, SEGL), axis=1)
+
     normed = normalize_rows(verifier_rows, norm_gain)
-    seg_keys, seg_values = project_pair(
-        normed,
-        (
-            lax.all_gather(key_weight, "fsdp", axis=0, tiled=True),
-            lax.all_gather(value_weight, "fsdp", axis=0, tiled=True),
-        ),
-    )
+    seg_kv = jnp.dot(normed, kv_w, preferred_element_type=jnp.float32)
+    seg_keys = seg_kv[:, :kv_cols]
+    seg_values = seg_kv[:, kv_cols:]
     lane_pick = (
         owner[:, None] == jnp.arange(pool_query.shape[0], dtype=jnp.int32)[None, :]
     ).astype(jnp.float32)
@@ -93,16 +89,33 @@
         queries,
         HD,
     )
-    live_own = flags.astype(jnp.float32)
-    key_all, value_all, live_all = (
-        lax.all_gather(summary_key.reshape(seg_count, KVH * HD), "seq", axis=0, tiled=True),
-        lax.all_gather(summary_value.reshape(seg_count, KVH * HD), "seq", axis=0, tiled=True),
-        lax.all_gather(live_own, "seq", axis=0, tiled=True),
+    width = KVH * HD
+    live_row = jnp.zeros((1, width), jnp.float32).at[0, :seg_count].set(flags.astype(jnp.float32))
+    tail = jnp.concatenate(
+        [
+            partial_scores.reshape(-1, width),
+            summary_key.reshape(seg_count, width),
+            summary_value.reshape(seg_count, width),
+            live_row,
+        ],
+        axis=0,
     )
+    tail_all = lax.all_gather(tail, "seq", axis=0, tiled=False)
+    score_rows = partial_scores.shape[0] // width
+    scores_all = tail_all[:, :score_rows].reshape(n_seq, -1)
+    own = lax.axis_index("seq")
+    own_tokens = seg_count * SEGL
+    token_scores = jnp.sum(
+        lax.dynamic_slice_in_dim(scores_all, own * own_tokens, own_tokens, axis=1), axis=0
+    )
+    draft_score = jnp.mean(token_scores.reshape(seg_count, SEGL), axis=1)
+    key_all = tail_all[:, score_rows : score_rows + seg_count].reshape(-1, KVH, HD)
+    value_all = tail_all[:, score_rows + seg_count : score_rows + 2 * seg_count].reshape(-1, KVH, HD)
+    live_all = tail_all[:, score_rows + 2 * seg_count, :seg_count].reshape(-1)
     pooled = cross_pool(
         summary_key,
-        key_all.reshape(-1, KVH, HD),
-        value_all.reshape(-1, KVH, HD),
+        key_all,
+        value_all,
         live_all > 0.5,
         HD,
     )

time: 244 us -> 163 us (0.67)
  waiting for transfers between devices: 147 us -> 88.9 us
  blocking collectives: 35 us -> 12.4 us
  matrix products: 38.2 us -> 22.4 us
  local copies, waits for them, and re-layouts: 1.87 us -> 15.6 us
  other arithmetic: 6.1 us -> 9.46 us
    all_gather x4 -> x1, waiting for transfers between devices: 144 us -> 88.8 us  [local(): gathered = lax.all_gather(block, 'fsdp', axis=0, tiled=False)]
    dot_general x4 -> x3, matrix products: 34.2 us -> 18.4 us  [the longest x1 7.77 us: local(): upward = jnp.dot(draft_tokens, up_w, preferred_element_type=jnp.float32)]
    slice x0 -> x4, local copies, waits for them, and re-layouts: none -> 14.9 us  [the longest x1 8.34 us: local(): kv_w = gathered[:, 2 * d_rows:].reshape(n_fsdp * v_rows, 2 * kv_cols)]
    all_gather x2 -> x1, blocking collectives: 24.3 us -> 12.4 us  [local(): tail_all = lax.all_gather(tail, 'seq', axis=0, tiled=False)]
    unnamed x1 -> x0, blocking collectives: 10.7 us -> none
    unnamed x4 -> x1, waiting for transfers between devices: 2.58 us -> 0.02 us
  transfers between devices with their start and end apart: 4 -> 1, of which waited for: 4 -> 1; matrix products, arithmetic and copies ran while one was open for 15% -> 4% of each run, Pallas kernels for 0% -> 0%
where the time goes in v1:
time: 163 us
  waiting for transfers between devices  88.9 us (55%)
  matrix products  22.4 us (14%)
  local copies, waits for them, and re-layouts  15.6 us (10%)
  between operations  14.2 us (9%)
  blocking collectives  12.4 us (8%)
  other arithmetic  9.46 us (6%)
    all_gather x1, waiting for transfers between devices, local(): gathered = lax.all_gather(block, 'fsdp', axis=0, tiled=False)  88.8 us
    all_gather x1, blocking collectives, local(): tail_all = lax.all_gather(tail, 'seq', axis=0, tiled=False)  12.4 us
    slice x1, local copies, waits for them, and re-layouts, local(): kv_w = gathered[:, 2 * d_rows:].reshape(n_fsdp * v_rows, 2 * kv_cols)  8.34 us
    dot_general x1, matrix products, local(): upward = jnp.dot(draft_tokens, up_w, preferred_element_type=jnp.float32)  7.77 us
    slice x1, local copies, waits for them, and re-layouts, local(): gate_w = gathered[:, :d_rows].reshape(n_fsdp * d_rows, d_cols)  6.5 us
    dot_general x1, matrix products, local(): gate = jnp.dot(draft_tokens, gate_w, preferred_element_type=jnp.float32)  5.91 us
    dot_general x1, matrix products, local(): seg_kv = jnp.dot(normed, kv_w, preferred_element_type=jnp.float32)  4.69 us
  transfers between devices with their start and end apart: 1, of which 1 were waited for; matrix products, arithmetic and copies ran while one was open for 4% of the time, Pallas kernels for 0%

profile of v1, /device:TPU:0, one launch (start us, length us, event | category | flops | bytes accessed | tf_op | source)
XLA Modules:
  0.0 163.0 jit_solution(15603105879236558077)
XLA Ops:
  7.2 2.1 %maximum_maximum_fusion = bf16[384,1024]{1,0:T(8,128)(2,1)} fusion(bf16[256,512]{1,0:T(8,128)(2,1)} %param.20, bf16[256,512]{1,0:T(8,128)(2,1)} %param.19, bf16[64,1024]{1,0:T(8,128)(2,1)} %param.15, bf16[64,1024]{1,0:T(8,128)(2,1)} %param.14), kind=kLoop, calls=%fused_computation.29 | loop fusion | flops 3145728 | bytes 1572864 | tf_op jit(solution)/shard_map/concatenate | solution.py:68
  9.4 0.6 compare_reduce_fusion.1
  10.0 0.8 convolution_bitcast_fusion.1
  10.9 0.7 broadcast_compare_fusion
  11.5 1.3 fusion.46
  12.8 3.1 %fusion.1 = f32[256]{0:T(256)S(1)} fusion(bf16[256,8192]{1,0:T(8,128)(2,1)} %param.17), kind=kLoop, calls=%fused_computation.3 | loop fusion | flops 6291200 | bytes 4195328 | tf_op jit(solution)/shard_map/reduce_sum | solution.py:18
  16.0 88.8 %all-gather.5.cloned.1.call-done = bf16[12288,1024]{1,0:T(8,128)(2,1)} async-done(((bf16[384,1024]{1,0:T(8,128)(2,1)}), bf16[12288,1024]{1,0:T(8,128)(2,1)}) %all-gather.5.cloned.1.call-update) | async-done | bytes 25165840 | tf_op jit(solution)/shard_map/all_gather | solution.py:69
  104.8 8.3 %slice.54 = bf16[32,256,1024]{2,1,0:T(8,128)(2,1)S(1)} slice(bf16[32,384,1024]{2,1,0:T(8,128)(2,1)} %bitcast.91), slice={[0:32], [128:384], [0:1024]} | slice | bytes 33554432 | tf_op jit(solution)/shard_map/slice | solution.py:72
  113.2 6.5 %fusion.49 = (bf16[32,64,1024]{2,1,0:T(8,128)(2,1)}, bf16[32,64,1024]{2,1,0:T(8,128)(2,1)}) fusion(bf16[32,384,1024]{2,1,0:T(8,128)(2,1)} %bitcast.92), kind=kLoop, calls=%fused_computation.74 | loop fusion | bytes 16777216 | tf_op jit(solution)/shard_map/slice | solution.py:70
  119.7 4.7 %fusion.4 = f32[256,1024]{1,0:T(8,128)S(1)} fusion(bf16[8192,1024]{1,0:T(8,128)(2,1)S(1)} %bitcast.93, bf16[256,8192]{1,0:T(8,128)(2,1)S(1)} %copy-done.2, f32[8192]{0:T(1024)S(1)} %copy-done.5, f32[256]{0:T(256)S(1)} %add_rsqrt_fusion), kind=kOutput, calls=%fused_computation.6 | convolution fusion | flops 4303355904 | bytes 22053888 | tf_op jit(solution)/shard_map/dot_general | solution.py:79
  124.5 0.2 reshape.108
  124.7 0.9 fusion.26
  125.6 0.7 fusion.52
  126.3 0.6 fusion.24
  126.9 0.2 reshape.110
  127.1 0.5 fusion.22
  127.6 7.8 %fusion.54 = f32[1024,1024]{1,0:T(8,128)S(1)} fusion(bf16[2048,1024]{1,0:T(8,128)(2,1)} %bitcast.95, bf16[1024,2048]{1,0:T(8,128)(2,1)} %param.13), kind=kOutput, calls=%fused_computation.79 | convolution fusion | flops 4294967296 | bytes 12582912 | tf_op jit(solution)/shard_map/dot_general | solution.py:75
  135.5 5.9 %fusion.7 = f32[1024]{0:T(1024)S(1)} fusion(f32[1024,1024]{1,0:T(8,128)S(1)} %fusion.54, bf16[2048,1024]{1,0:T(8,128)(2,1)S(1)} %bitcast.94, bf16[1024,2048]{1,0:T(8,128)(2,1)S(1)} %copy-done.4, f32[1024]{0:T(1024)S(1)} %copy-done.6), kind=kOutput, calls=%fused_computation.9 | convolution fusion | flops 4302306304 | bytes 12591104 | tf_op jit(solution)/shard_map/dot_general | solution.py:74
  141.4 12.4 %all-gather.2 = f32[4,19,512]{2,1,0:T(8,128)S(1)} all-gather(f32[1,19,512]{2,1,0:T(8,128)S(1)} %fusion.30), channel_id=3, replica_groups=mesh['fsdp'=32,'seq'=4] {'seq'}, dimensions={0}, use_global_device_ids=true | all-gather | bytes 194560 | tf_op jit(solution)/shard_map/all_gather | solution.py:103
  154.2 0.1 reduce_sum.58
  154.3 0.5 add_divide_fusion
  154.8 0.3 fusion.53
  155.1 0.2 fusion.35
  155.3 0.9 fusion.21
  (31 shorter events, 0.6 us)
Async XLA Ops:
  7.2 2.9 %copy-start = (f32[4,4,128]{2,1,0:T(4,128)S(1)}, f32[4,4,128]{2,1,0:T(4,128)}, u32[]{:S(2)}) copy-start(f32[4,4,128]{2,1,0:T(4,128)} %param.21) | copy-start | bytes 24580
  7.2 97.6 %all-gather.5.cloned.1.call-start = ((), (), s32[]{:S(2)}) async-start(), calls=%async_computation | async-start | bytes 25952256 | tf_op jit(solution)/shard_map/all_gather | solution.py:69
  113.1 6.5 %copy-start.2 = (bf16[256,8192]{1,0:T(8,128)(2,1)S(1)}, bf16[256,8192]{1,0:T(8,128)(2,1)}, u32[]{:S(2)}) copy-start(bf16[256,8192]{1,0:T(8,128)(2,1)} %param.17) | copy-start | bytes 12582916
  113.2 6.5 %copy-start.5 = (f32[8192]{0:T(1024)S(1)}, f32[8192]{0:T(1024)}, u32[]{:S(2)}) copy-start(f32[8192]{0:T(1024)} %param.18) | copy-start | bytes 98308
  127.6 7.8 %copy-start.3 = (bf16[32,64,1024]{2,1,0:T(8,128)(2,1)S(1)}, bf16[32,64,1024]{2,1,0:T(8,128)(2,1)}, u32[]{:S(2)}) copy-start(bf16[32,64,1024]{2,1,0:T(8,128)(2,1)} %get-tuple-element.16) | copy-start | bytes 12582916
  127.6 7.8 %copy-start.4 = (bf16[1024,2048]{1,0:T(8,128)(2,1)S(1)}, bf16[1024,2048]{1,0:T(8,128)(2,1)}, u32[]{:S(2)}) copy-start(bf16[1024,2048]{1,0:T(8,128)(2,1)} %param.13) | copy-start | bytes 12582916
  127.6 7.8 %copy-start.6 = (f32[1024]{0:T(1024)S(1)}, f32[1024]{0:T(1024)}, u32[]{:S(2)}) copy-start(f32[1024]{0:T(1024)} %param.16) | copy-start | bytes 12292
  135.5 20.7 %copy-start.1 = (f32[4,4,128]{2,1,0:T(4,128)S(1)}, f32[4,4,128]{2,1,0:T(4,128)}, u32[]{:S(2)}) copy-start(f32[4,4,128]{2,1,0:T(4,128)} %param.21) | copy-start | bytes 24580
Sparse Core Ops, SparseCore 0:
  10.2 94.5 all-gather.4

commit v2 on v1

--- a/solution.py
+++ b/solution.py
@@ -3,6 +3,8 @@
 import jax
 import jax.numpy as jnp
 from jax import lax
+from jax.experimental import pallas as pl
+from jax.experimental.pallas import tpu as pltpu
 from jax.sharding import PartitionSpec as P
 
 KVH = 4
@@ -42,6 +44,76 @@
     weights = jnp.where(live_all[None, None, :], jnp.exp(scores - highest), 0.0)
     total = jnp.sum(weights, axis=2, keepdims=True)
     return jnp.einsum("jhi,ihd->jhd", weights, value_all, precision=lax.Precision.HIGHEST) / total
+
+
+def draft_kernel(tok_ref, g_ref, u_ref, head_ref, out_ref, gacc, uacc):
+    j = pl.program_id(0)
+
+    @pl.when(j == 0)
+    def _():
+        gacc[...] = jnp.zeros_like(gacc)
+        uacc[...] = jnp.zeros_like(uacc)
+
+    t = tok_ref[...]
+    k = g_ref.shape[0] * g_ref.shape[1]
+    gacc[...] += jnp.dot(t, g_ref[...].reshape(k, -1), preferred_element_type=jnp.float32)
+    uacc[...] += jnp.dot(t, u_ref[...].reshape(k, -1), preferred_element_type=jnp.float32)
+
+    @pl.when(j == pl.num_programs(0) - 1)
+    def _():
+        g = gacc[...]
+        act = g / (1.0 + jnp.exp(-g))
+        out_ref[...] = jnp.sum(act * uacc[...] * head_ref[...], axis=1, keepdims=True)
+
+
+def draft_scores(tokens, gathered, head, row0, d_rows, group):
+    n_dev, _, cols = gathered.shape
+    n_tok = tokens.shape[0]
+    k = group * d_rows
+    gate_blk = row0 // d_rows
+    return pl.pallas_call(
+        draft_kernel,
+        grid=(n_dev // group,),
+        in_specs=[
+            pl.BlockSpec((n_tok, k), lambda j: (0, j)),
+            pl.BlockSpec((group, d_rows, cols), lambda j: (j, gate_blk, 0)),
+            pl.BlockSpec((group, d_rows, cols), lambda j: (j, gate_blk + 1, 0)),
+            pl.BlockSpec((1, cols), lambda j: (0, 0)),
+        ],
+        out_specs=pl.BlockSpec((n_tok, 1), lambda j: (0, 0)),
+        out_shape=jax.ShapeDtypeStruct((n_tok, 1), jnp.float32),
+        scratch_shapes=[
+            pltpu.VMEM((n_tok, cols), jnp.float32),
+            pltpu.VMEM((n_tok, cols), jnp.float32),
+        ],
+    )(tokens, gathered, gathered, head.reshape(1, cols))[:, 0]
+
+
+def kv_kernel(x_ref, w_ref, out_ref):
+    j = pl.program_id(0)
+
+    @pl.when(j == 0)
+    def _():
+        out_ref[...] = jnp.zeros_like(out_ref)
+
+    k = w_ref.shape[0] * w_ref.shape[1]
+    out_ref[...] += jnp.dot(x_ref[...], w_ref[...].reshape(k, -1), preferred_element_type=jnp.float32)
+
+
+def kv_project(normed, gathered, v_rows, group):
+    n_dev, _, cols = gathered.shape
+    n_tok = normed.shape[0]
+    k = group * v_rows
+    return pl.pallas_call(
+        kv_kernel,
+        grid=(n_dev // group,),
+        in_specs=[
+            pl.BlockSpec((n_tok, k), lambda j: (0, j)),
+            pl.BlockSpec((group, v_rows, cols), lambda j: (j, 0, 0)),
+        ],
+        out_specs=pl.BlockSpec((n_tok, cols), lambda j: (0, 0)),
+        out_shape=jax.ShapeDtypeStruct((n_tok, cols), jnp.float32),
+    )(normed, gathered)
 
 
 def local(
@@ -65,18 +137,14 @@
     kv_cols = key_weight.shape[1]
     kv_block = jnp.concatenate([key_weight, value_weight], axis=1)
     kv_block = kv_block.reshape(-1, d_cols)
-    block = jnp.concatenate([draft_gate, draft_up, kv_block], axis=0)
+    block = jnp.concatenate([kv_block, draft_gate, draft_up], axis=0)
     gathered = lax.all_gather(block, "fsdp", axis=0, tiled=False)
-    gate_w = gathered[:, :d_rows].reshape(n_fsdp * d_rows, d_cols)
-    up_w = gathered[:, d_rows : 2 * d_rows].reshape(n_fsdp * d_rows, d_cols)
-    kv_w = gathered[:, 2 * d_rows :].reshape(n_fsdp * v_rows, 2 * kv_cols)
-
-    gate = jnp.dot(draft_tokens, gate_w, preferred_element_type=jnp.float32)
-    upward = jnp.dot(draft_tokens, up_w, preferred_element_type=jnp.float32)
-    partial_scores = jnp.sum(jax.nn.silu(gate) * upward * draft_head[None, :], axis=1)
+    kv_rows = kv_block.shape[0]
+
+    partial_scores = draft_scores(draft_tokens, gathered, draft_head, kv_rows, d_rows, 4)
 
     normed = normalize_rows(verifier_rows, norm_gain)
-    seg_kv = jnp.dot(normed, kv_w, preferred_element_type=jnp.float32)
+    seg_kv = kv_project(normed, gathered, kv_rows, 2)
     seg_keys = seg_kv[:, :kv_cols]
     seg_values = seg_kv[:, kv_cols:]
     lane_pick = (

time: 163 us -> 164 us (level)
  Pallas kernels: 0 us -> 30.8 us
  matrix products: 22.4 us -> 4.32 us
  local copies, waits for them, and re-layouts: 15.6 us -> 1.9 us
  other arithmetic: 9.46 us -> 13.9 us
  waiting for transfers between devices: 88.9 us -> 85.3 us
    pallas_call x0 -> x2, Pallas kernels: none -> 30.8 us  [the longest x1 16.3 us: kv_project(): pl.pallas_call(kv_kernel, grid=(n_dev // group,), in_specs=[pl.BlockSpec(...]
    dot_general x3 -> x0, matrix products: 18.4 us -> none  [the longest x1 7.77 us: local(): upward = jnp.dot(draft_tokens, up_w, preferred_element_type=jnp.float32)]
    slice x2 -> x0, local copies, waits for them, and re-layouts: 14.8 us -> none  [the longest x1 8.34 us: local(): kv_w = gathered[:, 2 * d_rows:].reshape(n_fsdp * v_rows, 2 * kv_cols)]
    all_gather x1, waiting for transfers between devices: 88.8 us -> 85.3 us  [local(): gathered = lax.all_gather(block, 'fsdp', axis=0, tiled=False)]
    convert_element_type x0 -> x1, other arithmetic: none -> 3.16 us  [normalize_rows(): return (values * scale * norm_gain).astype(jnp.bfloat16)]
  transfers between devices with their start and end apart: 1 -> 1, of which waited for: 1 -> 1; matrix products, arithmetic and copies ran while one was open for 4% -> 6% of each run, Pallas kernels for 0% -> 0%
where the time goes in v2:
time: 164 us; the launch traced here: 163 us
  waiting for transfers between devices  85.3 us (52%)
  Pallas kernels  30.8 us (19%)
  between operations  14.2 us (9%)
  other arithmetic  13.9 us (8%)
  blocking collectives  12.4 us (8%)
  matrix products  4.32 us (3%)
  local copies, waits for them, and re-layouts  1.9 us (1%)
    all_gather x1, waiting for transfers between devices, local(): gathered = lax.all_gather(block, 'fsdp', axis=0, tiled=False)  85.3 us
    pallas_call x1, Pallas kernels, kv_project(): pl.pallas_call(kv_kernel, grid=(n_dev // group,), in_specs=[pl.BlockSpec(...  16.3 us
    pallas_call x1, Pallas kernels, draft_scores(): pl.pallas_call(draft_kernel, grid=(n_dev // group,), in_specs=[pl.BlockSp...  14.5 us
    all_gather x1, blocking collectives, local(): tail_all = lax.all_gather(tail, 'seq', axis=0, tiled=False)  12.4 us
  transfers between devices with their start and end apart: 1, of which 1 were waited for; matrix products, arithmetic and copies ran while one was open for 6% of the time, Pallas kernels for 0%

profile of v2, /device:TPU:0, one launch (start us, length us, event | category | flops | bytes accessed | tf_op | source)
XLA Modules:
  0.0 162.9 jit_solution(8165579986079933205)
XLA Ops:
  7.2 2.2 %pad_maximum_fusion = bf16[384,1024]{1,0:T(8,128)(2,1)} fusion(bf16[64,1024]{1,0:T(8,128)(2,1)} %param.15, bf16[64,1024]{1,0:T(8,128)(2,1)} %param.14, bf16[256,512]{1,0:T(8,128)(2,1)} %param.20, bf16[256,512]{1,0:T(8,128)(2,1)} %param.19), kind=kLoop, calls=%fused_computation.18 | loop fusion | flops 3145728 | bytes 1572864 | tf_op jit(solution)/shard_map/concatenate | solution.py:140
  9.4 0.6 compare_reduce_fusion.1
  10.1 1.2 convolution_bitcast_fusion.1
  11.3 0.7 broadcast_compare_fusion
  11.9 1.3 fusion.37
  13.2 3.1 %fusion.1 = f32[256]{0:T(256)S(1)} fusion(bf16[256,8192]{1,0:T(8,128)(2,1)} %param.17), kind=kLoop, calls=%fused_computation.3 | loop fusion | flops 6291200 | bytes 4195328 | tf_op jit(solution)/shard_map/reduce_sum | solution.py:20
  16.4 3.2 %fusion.3.x_ref = bf16[256,8192]{1,0:T(8,128)(2,1)} fusion(bf16[256,8192]{1,0:T(8,128)(2,1)S(1)} %copy-done.1, f32[8192]{0:T(1024)S(1)} %copy-done.2, f32[256]{0:T(256)S(1)} %add_rsqrt_fusion), kind=kLoop, calls=%fused_computation.5 | loop fusion | flops 8388608 | bytes 8422400 | tf_op jit(solution)/shard_map/convert_element_type | solution.py:21
  19.5 85.3 %all-gather.5.cloned.1.call-done = bf16[12288,1024]{1,0:T(8,128)(2,1)} async-done(((bf16[384,1024]{1,0:T(8,128)(2,1)}), bf16[12288,1024]{1,0:T(8,128)(2,1)}) %all-gather.5.cloned.1.call-update) | async-done | bytes 25165840 | tf_op jit(solution)/shard_map/all_gather | solution.py:141
  104.8 16.3 %shard_map.123 = f32[256,1024]{1,0:T(8,128)} custom-call(bf16[256,8192]{1,0:T(8,128)(2,1)} %fusion.3.x_ref, bf16[32,384,1024]{2,1,0:T(8,128)(2,1)} %bitcast.65), custom_call_target="tpu_custom_call" | custom-call | tf_op jit(solution)/shard_map/pallas_call | solution.py:107
  121.1 1.3 fusion.40
  122.4 0.2 reshape.95
  122.6 0.9 fusion.17
  123.5 0.7 fusion.42
  124.2 0.6 fusion.15
  124.8 0.2 reshape.97
  125.0 0.5 fusion.13
  125.5 14.5 %shard_map.122 = f32[1024,1]{1,0:T(8,128)} custom-call(bf16[1024,2048]{1,0:T(8,128)(2,1)} %tok_ref.1, bf16[32,384,1024]{2,1,0:T(8,128)(2,1)} %bitcast.66, bf16[32,384,1024]{2,1,0:T(8,128)(2,1)} %bitcast.67, f32[1,1024]{1,0:T(1,128)} %bitcast.69), custom_call_target="tpu_custom_call" | custom-call | tf_op jit(solution)/shard_map/pallas_call | solution.py:74
  140.1 1.2 reduce.7
  141.4 12.4 %all-gather.2 = f32[4,19,512]{2,1,0:T(8,128)S(1)} all-gather(f32[1,19,512]{2,1,0:T(8,128)S(1)} %fusion.21), channel_id=3, replica_groups=mesh['fsdp'=32,'seq'=4] {'seq'}, dimensions={0}, use_global_device_ids=true | all-gather | bytes 194560 | tf_op jit(solution)/shard_map/all_gather | solution.py:171
  154.1 0.1 reduce_sum.48
  154.2 0.5 add_divide_fusion
  154.8 0.3 fusion.43
  155.0 0.2 fusion.26
  155.2 0.9 fusion.12
  (22 shorter events, 0.5 us)
Async XLA Ops:
  7.2 2.9 %copy-start = (f32[4,4,128]{2,1,0:T(4,128)S(1)}, f32[4,4,128]{2,1,0:T(4,128)}, u32[]{:S(2)}) copy-start(f32[4,4,128]{2,1,0:T(4,128)} %param.21) | copy-start | bytes 24580
  7.2 9.2 %copy-start.2 = (f32[8192]{0:T(1024)S(1)}, f32[8192]{0:T(1024)}, u32[]{:S(2)}) copy-start(f32[8192]{0:T(1024)} %param.18) | copy-start | bytes 98308
  7.2 97.6 %all-gather.5.cloned.1.call-start = ((), (), s32[]{:S(2)}) async-start(), calls=%async_computation | async-start | bytes 25952256 | tf_op jit(solution)/shard_map/all_gather | solution.py:141
  9.4 6.9 %copy-start.1 = (bf16[256,8192]{1,0:T(8,128)(2,1)S(1)}, bf16[256,8192]{1,0:T(8,128)(2,1)}, u32[]{:S(2)}) copy-start(bf16[256,8192]{1,0:T(8,128)(2,1)} %param.17) | copy-start | bytes 12582916
Sparse Core Ops, SparseCore 0:
  10.3 94.5 all-gather.4

commit v3 on v2

--- a/solution.py
+++ b/solution.py
@@ -96,8 +96,13 @@
     def _():
         out_ref[...] = jnp.zeros_like(out_ref)
 
-    k = w_ref.shape[0] * w_ref.shape[1]
-    out_ref[...] += jnp.dot(x_ref[...], w_ref[...].reshape(k, -1), preferred_element_type=jnp.float32)
+    group, rows, _ = w_ref.shape
+    acc = jnp.dot(x_ref[:, 0:rows], w_ref[0], preferred_element_type=jnp.float32)
+    for i in range(1, group):
+        acc += jnp.dot(
+            x_ref[:, i * rows : (i + 1) * rows], w_ref[i], preferred_element_type=jnp.float32
+        )
+    out_ref[...] += acc
 
 
 def kv_project(normed, gathered, v_rows, group):
@@ -141,10 +146,9 @@
     gathered = lax.all_gather(block, "fsdp", axis=0, tiled=False)
     kv_rows = kv_block.shape[0]
 
-    partial_scores = draft_scores(draft_tokens, gathered, draft_head, kv_rows, d_rows, 4)
 
     normed = normalize_rows(verifier_rows, norm_gain)
-    seg_kv = kv_project(normed, gathered, kv_rows, 2)
+    seg_kv = kv_project(normed, gathered, kv_rows, 8)
     seg_keys = seg_kv[:, :kv_cols]
     seg_values = seg_kv[:, kv_cols:]
     lane_pick = (
@@ -159,27 +163,33 @@
     )
     width = KVH * HD
     live_row = jnp.zeros((1, width), jnp.float32).at[0, :seg_count].set(flags.astype(jnp.float32))
-    tail = jnp.concatenate(
-        [
-            partial_scores.reshape(-1, width),
-            summary_key.reshape(seg_count, width),
-            summary_value.reshape(seg_count, width),
-            live_row,
-        ],
+    summary = jnp.concatenate(
+        [summary_key.reshape(seg_count, width), summary_value.reshape(seg_count, width), live_row],
         axis=0,
     )
-    tail_all = lax.all_gather(tail, "seq", axis=0, tiled=False)
-    score_rows = partial_scores.shape[0] // width
-    scores_all = tail_all[:, :score_rows].reshape(n_seq, -1)
+    shifts = range(1, n_seq)
+    summary_all = jnp.stack(
+        [summary]
+        + [lax.ppermute(summary, "seq", [(i, (i + k) % n_seq) for i in range(n_seq)]) for k in shifts]
+    )
+
+    partial_scores = draft_scores(draft_tokens, gathered, draft_head, kv_rows, d_rows, 8)
+    scores_all = jnp.stack(
+        [partial_scores]
+        + [
+            lax.ppermute(partial_scores, "seq", [(i, (i + k) % n_seq) for i in range(n_seq)])
+            for k in shifts
+        ]
+    )
     own = lax.axis_index("seq")
     own_tokens = seg_count * SEGL
     token_scores = jnp.sum(
         lax.dynamic_slice_in_dim(scores_all, own * own_tokens, own_tokens, axis=1), axis=0
     )
     draft_score = jnp.mean(token_scores.reshape(seg_count, SEGL), axis=1)
-    key_all = tail_all[:, score_rows : score_rows + seg_count].reshape(-1, KVH, HD)
-    value_all = tail_all[:, score_rows + seg_count : score_rows + 2 * seg_count].reshape(-1, KVH, HD)
-    live_all = tail_all[:, score_rows + 2 * seg_count, :seg_count].reshape(-1)
+    key_all = summary_all[:, :seg_count].reshape(-1, KVH, HD)
+    value_all = summary_all[:, seg_count : 2 * seg_count].reshape(-1, KVH, HD)
+    live_all = summary_all[:, 2 * seg_count, :seg_count].reshape(-1)
     pooled = cross_pool(
         summary_key,
         key_all,

time: 164 us -> 156 us (0.951)
  blocking collectives: 12.4 us -> 0 us
  starting transfers between devices: 0.04 us -> 9.12 us
  Pallas kernels: 30.8 us -> 24.4 us
  waiting for transfers between devices: 85.3 us -> 87.8 us
    all_gather x1 -> x0, blocking collectives: 12.4 us -> none  [local(): tail_all = lax.all_gather(tail, 'seq', axis=0, tiled=False)]
    ppermute x0 -> x6, starting transfers between devices: none -> 9.08 us  [the longest x3 5.68 us: local(): lax.ppermute(partial_scores, 'seq', [(i, (i + k) % n_seq) for i in range(...]
    pallas_call x1, Pallas kernels: 16.3 us -> 10.4 us  [kv_project(): pl.pallas_call(kv_kernel, grid=(n_dev // group,), in_specs=[pl.BlockSpec(...]
    ppermute x0 -> x6, waiting for transfers between devices: none -> 2.53 us  [the longest x3 2.52 us: local(): lax.ppermute(summary, 'seq', [(i, (i + k) % n_seq) for i in range(n_seq)])]
  transfers between devices with their start and end apart: 1 -> 7, of which waited for: 1 -> 4; matrix products, arithmetic and copies ran while one was open for 6% -> 10% of each run, Pallas kernels for 0% -> 7%
where the time goes in v3:
time: 156 us
  waiting for transfers between devices  87.8 us (56%)
  Pallas kernels  24.4 us (16%)
  between operations  14.2 us (9%)
  other arithmetic  14 us (9%)
  starting transfers between devices  9.12 us (6%)
  matrix products  4.32 us (3%)
  local copies, waits for them, and re-layouts  1.87 us (1%)
    all_gather x1, waiting for transfers between devices, local(): gathered = lax.all_gather(block, 'fsdp', axis=0, tiled=False)  85.3 us
    pallas_call x1, Pallas kernels, draft_scores(): pl.pallas_call(draft_kernel, grid=(n_dev // group,), in_specs=[pl.BlockSp...  14 us
    pallas_call x1, Pallas kernels, kv_project(): pl.pallas_call(kv_kernel, grid=(n_dev // group,), in_specs=[pl.BlockSpec(...  10.4 us
    ppermute x3, starting transfers between devices, local(): lax.ppermute(partial_scores, 'seq', [(i, (i + k) % n_seq) for i in range(...  5.68 us
    ppermute x3, starting transfers between devices, local(): lax.ppermute(summary, 'seq', [(i, (i + k) % n_seq) for i in range(n_seq)])  3.4 us
    convert_element_type x1, other arithmetic, normalize_rows(): return (values * scale * norm_gain).astype(jnp.bfloat16)  3.16 us
  transfers between devices with their start and end apart: 7, of which 4 were waited for; matrix products, arithmetic and copies ran while one was open for 10% of the time, Pallas kernels for 7%

profile of v3, /device:TPU:0, one launch (start us, length us, event | category | flops | bytes accessed | tf_op | source)
XLA Modules:
  0.0 155.7 jit_solution(7421746790341941977)
XLA Ops:
  7.2 2.2 %pad_maximum_fusion = bf16[384,1024]{1,0:T(8,128)(2,1)} fusion(bf16[64,1024]{1,0:T(8,128)(2,1)} %param.15, bf16[64,1024]{1,0:T(8,128)(2,1)} %param.14, bf16[256,512]{1,0:T(8,128)(2,1)} %param.20, bf16[256,512]{1,0:T(8,128)(2,1)} %param.19), kind=kLoop, calls=%fused_computation.18 | loop fusion | flops 3145728 | bytes 1572864 | tf_op jit(solution)/shard_map/concatenate | solution.py:145
  9.4 0.6 compare_reduce_fusion.1
  10.1 1.2 convolution_bitcast_fusion.1
  11.3 0.7 broadcast_compare_fusion
  11.9 1.3 fusion.40
  13.2 3.1 %fusion.1 = f32[256]{0:T(256)S(1)} fusion(bf16[256,8192]{1,0:T(8,128)(2,1)} %param.17), kind=kLoop, calls=%fused_computation.3 | loop fusion | flops 6291200 | bytes 4195328 | tf_op jit(solution)/shard_map/reduce_sum | solution.py:20
  16.4 3.2 %fusion.3.x_ref = bf16[256,8192]{1,0:T(8,128)(2,1)} fusion(bf16[256,8192]{1,0:T(8,128)(2,1)S(1)} %copy-done.1, f32[8192]{0:T(1024)S(1)} %copy-done.2, f32[256]{0:T(256)S(1)} %add_rsqrt_fusion), kind=kLoop, calls=%fused_computation.5 | loop fusion | flops 8388608 | bytes 8422400 | tf_op jit(solution)/shard_map/convert_element_type | solution.py:21
  19.5 85.3 %all-gather.3.cloned.1.call-done = bf16[12288,1024]{1,0:T(8,128)(2,1)} async-done(((bf16[384,1024]{1,0:T(8,128)(2,1)}), bf16[12288,1024]{1,0:T(8,128)(2,1)}) %all-gather.3.cloned.1.call-update) | async-done | bytes 25165840 | tf_op jit(solution)/shard_map/all_gather | solution.py:146
  104.8 14.0 %shard_map.122 = f32[1024,1]{1,0:T(8,128)} custom-call(bf16[1024,2048]{1,0:T(8,128)(2,1)} %tok_ref.1, bf16[32,384,1024]{2,1,0:T(8,128)(2,1)} %bitcast.69, bf16[32,384,1024]{2,1,0:T(8,128)(2,1)} %bitcast.70, f32[1,1024]{1,0:T(1,128)} %bitcast.82), custom_call_target="tpu_custom_call" | custom-call | tf_op jit(solution)/shard_map/pallas_call | solution.py:74
  118.8 1.2 reduce.7
  120.0 1.5 collective-permute-start
  121.6 2.7 %collective-permute-start.1 = (f32[1024]{0:T(1024)S(1)}, f32[1024]{0:T(1024)S(1)}, u32[]{:S(2)}, u32[]{:S(2)}) collective-permute-start(f32[1024]{0:T(1024)S(1)} %reduce.7), channel_id=1, source_target_pairs={{0,2},{1,3},{2,0},{3,1},{4,6},{5,7},{6,4},{7,5},{8,10},{9,11},{10,... | collective-permute-start | bytes 12296 | tf_op jit(solution)/shard_map/ppermute | solution.py:180
  124.3 1.5 collective-permute-start.2
  125.7 10.4 %shard_map.123 = f32[256,1024]{1,0:T(8,128)} custom-call(bf16[256,8192]{1,0:T(8,128)(2,1)} %fusion.3.x_ref, bf16[32,384,1024]{2,1,0:T(8,128)(2,1)} %bitcast.71), custom_call_target="tpu_custom_call" | custom-call | tf_op jit(solution)/shard_map/pallas_call | solution.py:112
  136.1 1.3 fusion.44
  137.6 0.9 fusion.17
  138.5 0.7 fusion.45
  139.2 0.6 fusion.15
  140.6 0.6 collective-permute-start.3
  141.2 0.9 collective-permute-start.4
  142.1 1.9 %collective-permute-start.5 = (f32[17,512]{1,0:T(8,128)S(1)}, f32[17,512]{1,0:T(8,128)S(1)}, u32[]{:S(2)}, u32[]{:S(2)}) collective-permute-start(f32[17,512]{1,0:T(8,128)S(1)} %get-tuple-element.19), channel_id=1, source_target_pairs={{0,3},{1,0},{2,1},{3,2},{4,7},{5,4},{6,5},{7,6},{8,11},{9,8},{10,9... | collective-permute-start | bytes 104456 | tf_op jit(solution)/shard_map/ppermute | solution.py:173
  144.8 1.1 collective-permute-done.3
  145.9 0.9 collective-permute-done.4
  148.0 0.9 fusion.12
  (32 shorter events, 3.1 us)
Async XLA Ops:
  7.2 2.9 %copy-start = (f32[4,4,128]{2,1,0:T(4,128)S(1)}, f32[4,4,128]{2,1,0:T(4,128)}, u32[]{:S(2)}) copy-start(f32[4,4,128]{2,1,0:T(4,128)} %param.21) | copy-start | bytes 24580
  7.2 9.2 %copy-start.2 = (f32[8192]{0:T(1024)S(1)}, f32[8192]{0:T(1024)}, u32[]{:S(2)}) copy-start(f32[8192]{0:T(1024)} %param.18) | copy-start | bytes 98308
  7.2 97.6 %all-gather.3.cloned.1.call-start = ((), (), s32[]{:S(2)}) async-start(), calls=%async_computation | async-start | bytes 25952256 | tf_op jit(solution)/shard_map/all_gather | solution.py:146
  9.4 6.9 %copy-start.1 = (bf16[256,8192]{1,0:T(8,128)(2,1)S(1)}, bf16[256,8192]{1,0:T(8,128)(2,1)}, u32[]{:S(2)}) copy-start(bf16[256,8192]{1,0:T(8,128)(2,1)} %param.17) | copy-start | bytes 12582916
  120.0 22.1 %collective-permute-start = (f32[1024]{0:T(1024)S(1)}, f32[1024]{0:T(1024)S(1)}, u32[]{:S(2)}, u32[]{:S(2)}) collective-permute-start(f32[1024]{0:T(1024)S(1)} %reduce.7), channel_id=1, source_target_pairs={{0,1},{1,2},{2,3},{3,0},{4,5},{5,6},{6,7},{7,4},{8,9},{9,10},{10,1... | collective-permute-start | bytes 12296 | tf_op jit(solution)/shard_map/ppermute | solution.py:180
  121.6 22.4 %collective-permute-start.1 = (f32[1024]{0:T(1024)S(1)}, f32[1024]{0:T(1024)S(1)}, u32[]{:S(2)}, u32[]{:S(2)}) collective-permute-start(f32[1024]{0:T(1024)S(1)} %reduce.7), channel_id=1, source_target_pairs={{0,2},{1,3},{2,0},{3,1},{4,6},{5,7},{6,4},{7,5},{8,10},{9,11},{10,... | collective-permute-start | bytes 12296 | tf_op jit(solution)/shard_map/ppermute | solution.py:180
  124.3 19.7 %collective-permute-start.2 = (f32[1024]{0:T(1024)S(1)}, f32[1024]{0:T(1024)S(1)}, u32[]{:S(2)}, u32[]{:S(2)}) collective-permute-start(f32[1024]{0:T(1024)S(1)} %reduce.7), channel_id=1, source_target_pairs={{0,3},{1,0},{2,1},{3,2},{4,7},{5,4},{6,5},{7,6},{8,11},{9,8},{10,9... | collective-permute-start | bytes 12296 | tf_op jit(solution)/shard_map/ppermute | solution.py:180
  140.6 5.4 %collective-permute-start.3 = (f32[17,512]{1,0:T(8,128)S(1)}, f32[17,512]{1,0:T(8,128)S(1)}, u32[]{:S(2)}, u32[]{:S(2)}) collective-permute-start(f32[17,512]{1,0:T(8,128)S(1)} %get-tuple-element.19), channel_id=1, source_target_pairs={{0,1},{1,2},{2,3},{3,0},{4,5},{5,6},{6,7},{7,4},{8,9},{9,10},{10,1... | collective-permute-start | bytes 104456 | tf_op jit(solution)/shard_map/ppermute | solution.py:173
  141.2 5.6 %collective-permute-start.4 = (f32[17,512]{1,0:T(8,128)S(1)}, f32[17,512]{1,0:T(8,128)S(1)}, u32[]{:S(2)}, u32[]{:S(2)}) collective-permute-start(f32[17,512]{1,0:T(8,128)S(1)} %get-tuple-element.19), channel_id=1, source_target_pairs={{0,2},{1,3},{2,0},{3,1},{4,6},{5,7},{6,4},{7,5},{8,10},{9,11},{10,... | collective-permute-start | bytes 104456 | tf_op jit(solution)/shard_map/ppermute | solution.py:173
  142.1 5.2 %collective-permute-start.5 = (f32[17,512]{1,0:T(8,128)S(1)}, f32[17,512]{1,0:T(8,128)S(1)}, u32[]{:S(2)}, u32[]{:S(2)}) collective-permute-start(f32[17,512]{1,0:T(8,128)S(1)} %get-tuple-element.19), channel_id=1, source_target_pairs={{0,3},{1,0},{2,1},{3,2},{4,7},{5,4},{6,5},{7,6},{8,11},{9,8},{10,9... | collective-permute-start | bytes 104456 | tf_op jit(solution)/shard_map/ppermute | solution.py:173
Sparse Core Ops, SparseCore 0:
  10.3 94.5 all-gather.2

commit v4 on v3

--- a/solution.py
+++ b/solution.py
@@ -22,28 +22,24 @@
 
 
 def segment_pool(seg_keys, seg_values, queries, head_size):
-    scores = jnp.einsum(
-        "sthd,shd->sth", seg_keys, queries, precision=lax.Precision.HIGHEST
-    ) / math.sqrt(head_size)
+    scores = jnp.sum(seg_keys * queries[:, None], axis=-1) / math.sqrt(head_size)
     scores = scores - jnp.max(scores, axis=1, keepdims=True)
     weights = jnp.exp(scores)
     weights = weights / jnp.sum(weights, axis=1, keepdims=True)
-    summary_key = jnp.einsum("sth,sthd->shd", weights, seg_keys, precision=lax.Precision.HIGHEST)
-    summary_value = jnp.einsum(
-        "sth,sthd->shd", weights, seg_values, precision=lax.Precision.HIGHEST
-    )
+    summary_key = jnp.sum(weights[..., None] * seg_keys, axis=1)
+    summary_value = jnp.sum(weights[..., None] * seg_values, axis=1)
     return (summary_key, summary_value)
 
 
 def cross_pool(query_keys, key_all, value_all, live_all, head_size):
-    scores = jnp.einsum(
-        "jhd,ihd->jhi", query_keys, key_all, precision=lax.Precision.HIGHEST
-    ) / math.sqrt(head_size)
+    scores = jnp.sum(query_keys[:, :, None, :] * jnp.swapaxes(key_all, 0, 1)[None], axis=-1)
+    scores = scores / math.sqrt(head_size)
     scores = jnp.where(live_all[None, None, :], scores, -1e30)
     highest = jnp.max(scores, axis=2, keepdims=True)
     weights = jnp.where(live_all[None, None, :], jnp.exp(scores - highest), 0.0)
     total = jnp.sum(weights, axis=2, keepdims=True)
-    return jnp.einsum("jhi,ihd->jhd", weights, value_all, precision=lax.Precision.HIGHEST) / total
+    pooled = jnp.sum(weights[..., None] * jnp.swapaxes(value_all, 0, 1)[None], axis=2)
+    return pooled / total
 
 
 def draft_kernel(tok_ref, g_ref, u_ref, head_ref, out_ref, gacc, uacc):
@@ -146,7 +142,6 @@
     gathered = lax.all_gather(block, "fsdp", axis=0, tiled=False)
     kv_rows = kv_block.shape[0]
 
-
     normed = normalize_rows(verifier_rows, norm_gain)
     seg_kv = kv_project(normed, gathered, kv_rows, 8)
     seg_keys = seg_kv[:, :kv_cols]
@@ -163,24 +158,26 @@
     )
     width = KVH * HD
     live_row = jnp.zeros((1, width), jnp.float32).at[0, :seg_count].set(flags.astype(jnp.float32))
-    summary = jnp.concatenate(
-        [summary_key.reshape(seg_count, width), summary_value.reshape(seg_count, width), live_row],
+    partial_scores = draft_scores(draft_tokens, gathered, draft_head, kv_rows, d_rows, 8)
+    tail = jnp.concatenate(
+        [
+            partial_scores.reshape(-1, width),
+            summary_key.reshape(seg_count, width),
+            summary_value.reshape(seg_count, width),
+            live_row,
+        ],
         axis=0,
     )
-    shifts = range(1, n_seq)
-    summary_all = jnp.stack(
-        [summary]
-        + [lax.ppermute(summary, "seq", [(i, (i + k) % n_seq) for i in range(n_seq)]) for k in shifts]
-    )
-
-    partial_scores = draft_scores(draft_tokens, gathered, draft_head, kv_rows, d_rows, 8)
-    scores_all = jnp.stack(
-        [partial_scores]
+    tail_all = jnp.stack(
+        [tail]
         + [
-            lax.ppermute(partial_scores, "seq", [(i, (i + k) % n_seq) for i in range(n_seq)])
-            for k in shifts
+            lax.ppermute(tail, "seq", [(i, (i + k) % n_seq) for i in range(n_seq)])
+            for k in range(1, n_seq)
         ]
     )
+    score_rows = partial_scores.shape[0] // width
+    scores_all = tail_all[:, :score_rows].reshape(n_seq, -1)
+    summary_all = tail_all[:, score_rows:]
     own = lax.axis_index("seq")
     own_tokens = seg_count * SEGL
     token_scores = jnp.sum(

time: 156 us -> 151 us (0.968)
  starting transfers between devices: 9.12 us -> 5.72 us
  matrix products: 4.32 us -> 1 us
    ppermute x6 -> x3, starting transfers between devices: 9.08 us -> 5.68 us  [local(): lax.ppermute(tail, 'seq', [(i, (i + k) % n_seq) for i in range(n_seq)])]
    dot_general x5 -> x0, matrix products: 3.15 us -> none  [the longest x1 0.93 us: segment_pool(): jnp.einsum('sthd,shd->sth', seg_keys, queries, precision=lax.Precision.HI...]
  transfers between devices with their start and end apart: 7 -> 4, of which waited for: 4 -> 3; matrix products, arithmetic and copies ran while one was open for 10% -> 6% of each run, Pallas kernels for 7% -> 0%
where the time goes in v4:
time: 151 us; the launch traced here: 150 us
  waiting for transfers between devices  88.8 us (59%)
  Pallas kernels  24.4 us (16%)
  other arithmetic  14.5 us (10%)
  between operations  14.2 us (9%)
  starting transfers between devices  5.72 us (4%)
  local copies, waits for them, and re-layouts  1.91 us (1%)
    all_gather x1, waiting for transfers between devices, local(): gathered = lax.all_gather(block, 'fsdp', axis=0, tiled=False)  86.1 us
    pallas_call x1, Pallas kernels, draft_scores(): pl.pallas_call(draft_kernel, grid=(n_dev // group,), in_specs=[pl.BlockSp...  14 us
    pallas_call x1, Pallas kernels, kv_project(): pl.pallas_call(kv_kernel, grid=(n_dev // group,), in_specs=[pl.BlockSpec(...  10.4 us
    ppermute x3, starting transfers between devices, local(): lax.ppermute(tail, 'seq', [(i, (i + k) % n_seq) for i in range(n_seq)])  5.68 us
    convert_element_type x1, other arithmetic, normalize_rows(): return (values * scale * norm_gain).astype(jnp.bfloat16)  3.16 us
    reduce_sum x1, other arithmetic, normalize_rows(): scale = lax.rsqrt(jnp.mean(values * values, axis=-1, keepdims=True) + eps)  3.1 us
  transfers between devices with their start and end apart: 4, of which 3 were waited for; matrix products, arithmetic and copies ran while one was open for 6% of the time, Pallas kernels for 0%

profile of v4, /device:TPU:0, one launch (start us, length us, event | category | flops | bytes accessed | tf_op | source)
XLA Modules:
  0.0 150.5 jit_solution(1115951015482975253)
XLA Ops:
  7.2 2.2 %pad_maximum_fusion = bf16[384,1024]{1,0:T(8,128)(2,1)} fusion(bf16[64,1024]{1,0:T(8,128)(2,1)} %param.15, bf16[64,1024]{1,0:T(8,128)(2,1)} %param.14, bf16[256,512]{1,0:T(8,128)(2,1)} %param.20, bf16[256,512]{1,0:T(8,128)(2,1)} %param.19), kind=kLoop, calls=%fused_computation.12 | loop fusion | flops 3145728 | bytes 1572864 | tf_op jit(solution)/shard_map/concatenate | solution.py:141
  9.4 1.0 fusion.19
  10.5 0.6 compare_reduce_fusion.1
  11.1 1.3 fusion.27
  12.4 3.1 %fusion.2 = f32[256]{0:T(256)S(1)} fusion(bf16[256,8192]{1,0:T(8,128)(2,1)} %param.17), kind=kLoop, calls=%fused_computation.4 | loop fusion | flops 6291200 | bytes 4195328 | tf_op jit(solution)/shard_map/reduce_sum | solution.py:20
  15.5 3.2 %fusion.4.x_ref = bf16[256,8192]{1,0:T(8,128)(2,1)} fusion(bf16[256,8192]{1,0:T(8,128)(2,1)S(1)} %copy-done.1, f32[8192]{0:T(1024)S(1)} %copy-done.2, f32[256]{0:T(256)S(1)} %add_rsqrt_fusion), kind=kLoop, calls=%fused_computation.6 | loop fusion | flops 8388608 | bytes 8422400 | tf_op jit(solution)/shard_map/convert_element_type | solution.py:21
  18.7 86.1 %all-gather.3.cloned.1.call-done = bf16[12288,1024]{1,0:T(8,128)(2,1)} async-done(((bf16[384,1024]{1,0:T(8,128)(2,1)}), bf16[12288,1024]{1,0:T(8,128)(2,1)}) %all-gather.3.cloned.1.call-update) | async-done | bytes 25165840 | tf_op jit(solution)/shard_map/all_gather | solution.py:142
  104.8 10.4 %shard_map.123 = f32[256,1024]{1,0:T(8,128)} custom-call(bf16[256,8192]{1,0:T(8,128)(2,1)} %fusion.4.x_ref, bf16[32,384,1024]{2,1,0:T(8,128)(2,1)} %bitcast.31), custom_call_target="tpu_custom_call" | custom-call | tf_op jit(solution)/shard_map/pallas_call | solution.py:108
  115.2 1.3 fusion.35
  116.5 0.2 reshape.113
  116.7 0.4 multiply_reduce_fusion.4
  117.1 0.2 reshape.115
  117.3 14.0 %shard_map.122 = f32[1024,1]{1,0:T(8,128)} custom-call(bf16[1024,2048]{1,0:T(8,128)(2,1)} %tok_ref.1, bf16[32,384,1024]{2,1,0:T(8,128)(2,1)} %bitcast.32, bf16[32,384,1024]{2,1,0:T(8,128)(2,1)} %bitcast.33, f32[1,1024]{1,0:T(1,128)} %bitcast.48), custom_call_target="tpu_custom_call" | custom-call | tf_op jit(solution)/shard_map/pallas_call | solution.py:70
  131.3 1.2 reduce.7
  132.6 0.3 multiply_reduce_fusion.3
  132.9 1.5 %collective-permute-start = (f32[19,512]{1,0:T(8,128)S(1)}, f32[19,512]{1,0:T(8,128)S(1)}, u32[]{:S(2)}, u32[]{:S(2)}) collective-permute-start(f32[19,512]{1,0:T(8,128)S(1)} %get-tuple-element.23), channel_id=1, source_target_pairs={{0,1},{1,2},{2,3},{3,0},{4,5},{5,6},{6,7},{7,4},{8,9},{9,10},{10,1... | collective-permute-start | bytes 116744 | tf_op jit(solution)/shard_map/ppermute | solution.py:174
  134.5 2.7 %collective-permute-start.1 = (f32[19,512]{1,0:T(8,128)S(1)}, f32[19,512]{1,0:T(8,128)S(1)}, u32[]{:S(2)}, u32[]{:S(2)}) collective-permute-start(f32[19,512]{1,0:T(8,128)S(1)} %get-tuple-element.23), channel_id=1, source_target_pairs={{0,2},{1,3},{2,0},{3,1},{4,6},{5,7},{6,4},{7,5},{8,10},{9,11},{10,... | collective-permute-start | bytes 116744 | tf_op jit(solution)/shard_map/ppermute | solution.py:174
  137.2 1.5 collective-permute-start.2
  138.6 1.5 collective-permute-done.1
  140.1 1.1 collective-permute-done.2
  141.4 0.2 multiply_reduce_fusion.1
  142.0 0.5 add_divide_fusion
  142.7 0.2 multiply_reduce_fusion
  143.0 0.7 fusion.15
  (32 shorter events, 0.9 us)
Async XLA Ops:
  7.2 2.3 %copy-start = (f32[4,4,128]{2,1,0:T(4,128)S(1)}, f32[4,4,128]{2,1,0:T(4,128)}, u32[]{:S(2)}) copy-start(f32[4,4,128]{2,1,0:T(4,128)} %param.21) | copy-start | bytes 24580
  7.2 8.3 %copy-start.2 = (f32[8192]{0:T(1024)S(1)}, f32[8192]{0:T(1024)}, u32[]{:S(2)}) copy-start(f32[8192]{0:T(1024)} %param.18) | copy-start | bytes 98308
  7.2 97.6 %all-gather.3.cloned.1.call-start = ((), (), s32[]{:S(2)}) async-start(), calls=%async_computation | async-start | bytes 25952256 | tf_op jit(solution)/shard_map/all_gather | solution.py:142
  9.4 6.1 %copy-start.1 = (bf16[256,8192]{1,0:T(8,128)(2,1)S(1)}, bf16[256,8192]{1,0:T(8,128)(2,1)}, u32[]{:S(2)}) copy-start(bf16[256,8192]{1,0:T(8,128)(2,1)} %param.17) | copy-start | bytes 12582916
  117.3 21.4 %copy-start.3 = (s32[8]{0:T(128)S(1)}, s32[8]{0:T(128)}, u32[]{:S(2)}) copy-start(s32[8]{0:T(128)} %param.22) | copy-start | bytes 100
  132.9 5.7 %collective-permute-start = (f32[19,512]{1,0:T(8,128)S(1)}, f32[19,512]{1,0:T(8,128)S(1)}, u32[]{:S(2)}, u32[]{:S(2)}) collective-permute-start(f32[19,512]{1,0:T(8,128)S(1)} %get-tuple-element.23), channel_id=1, source_target_pairs={{0,1},{1,2},{2,3},{3,0},{4,5},{5,6},{6,7},{7,4},{8,9},{9,10},{10,1... | collective-permute-start | bytes 116744 | tf_op jit(solution)/shard_map/ppermute | solution.py:174
  134.5 5.6 %collective-permute-start.1 = (f32[19,512]{1,0:T(8,128)S(1)}, f32[19,512]{1,0:T(8,128)S(1)}, u32[]{:S(2)}, u32[]{:S(2)}) collective-permute-start(f32[19,512]{1,0:T(8,128)S(1)} %get-tuple-element.23), channel_id=1, source_target_pairs={{0,2},{1,3},{2,0},{3,1},{4,6},{5,7},{6,4},{7,5},{8,10},{9,11},{10,... | collective-permute-start | bytes 116744 | tf_op jit(solution)/shard_map/ppermute | solution.py:174
  137.2 4.1 %collective-permute-start.2 = (f32[19,512]{1,0:T(8,128)S(1)}, f32[19,512]{1,0:T(8,128)S(1)}, u32[]{:S(2)}, u32[]{:S(2)}) collective-permute-start(f32[19,512]{1,0:T(8,128)S(1)} %get-tuple-element.23), channel_id=1, source_target_pairs={{0,3},{1,0},{2,1},{3,2},{4,7},{5,4},{6,5},{7,6},{8,11},{9,8},{10,9... | collective-permute-start | bytes 116744 | tf_op jit(solution)/shard_map/ppermute | solution.py:174
Sparse Core Ops, SparseCore 0:
  10.3 94.5 all-gather.2

commit v5 on v4

--- a/solution.py
+++ b/solution.py
@@ -59,7 +59,9 @@
     def _():
         g = gacc[...]
         act = g / (1.0 + jnp.exp(-g))
-        out_ref[...] = jnp.sum(act * uacc[...] * head_ref[...], axis=1, keepdims=True)
+        col = jnp.sum(act * uacc[...] * head_ref[...], axis=1, keepdims=True)
+        wide = jnp.broadcast_to(col, (col.shape[0], 128))
+        out_ref[...] = jnp.transpose(wide)[0 : out_ref.shape[0], :]
 
 
 def draft_scores(tokens, gathered, head, row0, d_rows, group):
@@ -76,13 +78,13 @@
             pl.BlockSpec((group, d_rows, cols), lambda j: (j, gate_blk + 1, 0)),
             pl.BlockSpec((1, cols), lambda j: (0, 0)),
         ],
-        out_specs=pl.BlockSpec((n_tok, 1), lambda j: (0, 0)),
-        out_shape=jax.ShapeDtypeStruct((n_tok, 1), jnp.float32),
+        out_specs=pl.BlockSpec((8, n_tok), lambda j: (0, 0)),
+        out_shape=jax.ShapeDtypeStruct((8, n_tok), jnp.float32),
         scratch_shapes=[
             pltpu.VMEM((n_tok, cols), jnp.float32),
             pltpu.VMEM((n_tok, cols), jnp.float32),
         ],
-    )(tokens, gathered, gathered, head.reshape(1, cols))[:, 0]
+    )(tokens, gathered, gathered, head.reshape(1, cols))[0]
 
 
 def kv_kernel(x_ref, w_ref, out_ref):
@@ -168,13 +170,12 @@
         ],
         axis=0,
     )
-    tail_all = jnp.stack(
-        [tail]
-        + [
-            lax.ppermute(tail, "seq", [(i, (i + k) % n_seq) for i in range(n_seq)])
-            for k in range(1, n_seq)
-        ]
-    )
+    tail_all = tail[None]
+    step = 1
+    while step < n_seq:
+        pairs = [(i, i ^ step) for i in range(n_seq)]
+        tail_all = jnp.concatenate([tail_all, lax.ppermute(tail_all, "seq", pairs)], axis=0)
+        step *= 2
     score_rows = partial_scores.shape[0] // width
     scores_all = tail_all[:, :score_rows].reshape(n_seq, -1)
     summary_all = tail_all[:, score_rows:]

time: 151 us -> 152 us (level)
  waiting for transfers between devices: 88.8 us -> 91.9 us
    ppermute x3 -> x2, waiting for transfers between devices: 2.62 us -> 5.76 us  [local(): lax.ppermute(tail_all, 'seq', pairs)]
    ppermute x3 -> x2, starting transfers between devices: 5.68 us -> 4.6 us  [local(): lax.ppermute(tail_all, 'seq', pairs)]
  transfers between devices with their start and end apart: 4 -> 3, of which waited for: 3 -> 3; matrix products, arithmetic and copies ran while one was open for 6% -> 6% of each run, Pallas kernels for 0% -> 0%
where the time goes in v5:
time: 152 us
  waiting for transfers between devices  91.9 us (60%)
  Pallas kernels  24.3 us (16%)
  between operations  14.2 us (9%)
  other arithmetic  13.2 us (9%)
  starting transfers between devices  4.64 us (3%)
  local copies, waits for them, and re-layouts  2.69 us (2%)
    all_gather x1, waiting for transfers between devices, local(): gathered = lax.all_gather(block, 'fsdp', axis=0, tiled=False)  86.1 us
    pallas_call x1, Pallas kernels, draft_scores(): pl.pallas_call(draft_kernel, grid=(n_dev // group,), in_specs=[pl.BlockSp...  13.9 us
    pallas_call x1, Pallas kernels, kv_project(): pl.pallas_call(kv_kernel, grid=(n_dev // group,), in_specs=[pl.BlockSpec(...  10.4 us
    ppermute x2, waiting for transfers between devices, local(): lax.ppermute(tail_all, 'seq', pairs)  5.76 us
    ppermute x2, starting transfers between devices, local(): lax.ppermute(tail_all, 'seq', pairs)  4.6 us
    convert_element_type x1, other arithmetic, normalize_rows(): return (values * scale * norm_gain).astype(jnp.bfloat16)  3.16 us
    reduce_sum x1, other arithmetic, normalize_rows(): scale = lax.rsqrt(jnp.mean(values * values, axis=-1, keepdims=True) + eps)  3.1 us
  transfers between devices with their start and end apart: 3, of which 3 were waited for; matrix products, arithmetic and copies ran while one was open for 6% of the time, Pallas kernels for 0%

profile of v5, /device:TPU:0, one launch (start us, length us, event | category | flops | bytes accessed | tf_op | source)
XLA Modules:
  0.0 152.0 jit_solution(14042947810117839988)
XLA Ops:
  7.2 2.2 %pad_maximum_fusion = bf16[384,1024]{1,0:T(8,128)(2,1)} fusion(bf16[64,1024]{1,0:T(8,128)(2,1)} %param.15, bf16[64,1024]{1,0:T(8,128)(2,1)} %param.14, bf16[256,512]{1,0:T(8,128)(2,1)} %param.20, bf16[256,512]{1,0:T(8,128)(2,1)} %param.19), kind=kLoop, calls=%fused_computation.12 | loop fusion | flops 3145728 | bytes 1572864 | tf_op jit(solution)/shard_map/concatenate | solution.py:143
  9.4 1.0 fusion.20
  10.5 0.6 compare_reduce_fusion.1
  11.1 1.3 fusion.28
  12.4 3.1 %fusion.2 = f32[256]{0:T(256)S(1)} fusion(bf16[256,8192]{1,0:T(8,128)(2,1)} %param.17), kind=kLoop, calls=%fused_computation.4 | loop fusion | flops 6291200 | bytes 4195328 | tf_op jit(solution)/shard_map/reduce_sum | solution.py:20
  15.5 3.2 %fusion.4.x_ref = bf16[256,8192]{1,0:T(8,128)(2,1)} fusion(bf16[256,8192]{1,0:T(8,128)(2,1)S(1)} %copy-done.1, f32[8192]{0:T(1024)S(1)} %copy-done.2, f32[256]{0:T(256)S(1)} %add_rsqrt_fusion), kind=kLoop, calls=%fused_computation.6 | loop fusion | flops 8388608 | bytes 8422400 | tf_op jit(solution)/shard_map/convert_element_type | solution.py:21
  18.7 86.1 %all-gather.3.cloned.1.call-done = bf16[12288,1024]{1,0:T(8,128)(2,1)} async-done(((bf16[384,1024]{1,0:T(8,128)(2,1)}), bf16[12288,1024]{1,0:T(8,128)(2,1)}) %all-gather.3.cloned.1.call-update) | async-done | bytes 25165840 | tf_op jit(solution)/shard_map/all_gather | solution.py:144
  104.8 10.4 %shard_map.123 = f32[256,1024]{1,0:T(8,128)} custom-call(bf16[256,8192]{1,0:T(8,128)(2,1)} %fusion.4.x_ref, bf16[32,384,1024]{2,1,0:T(8,128)(2,1)} %bitcast.28), custom_call_target="tpu_custom_call" | custom-call | tf_op jit(solution)/shard_map/pallas_call | solution.py:110
  115.2 1.3 fusion.35
  116.5 0.2 reshape.113
  116.7 0.4 multiply_reduce_fusion.4
  117.1 0.2 reshape.115
  117.3 13.9 %shard_map.122 = f32[8,1024]{1,0:T(8,128)} custom-call(bf16[1024,2048]{1,0:T(8,128)(2,1)} %tok_ref.1, bf16[32,384,1024]{2,1,0:T(8,128)(2,1)} %bitcast.29, bf16[32,384,1024]{2,1,0:T(8,128)(2,1)} %bitcast.30, f32[1,1024]{1,0:T(1,128)} %bitcast.36), custom_call_target="tpu_custom_call" | custom-call | tf_op jit(solution)/shard_map/pallas_call | solution.py:72
  131.2 0.8 slice_reduce_fusion
  132.0 0.3 multiply_reduce_fusion.3
  132.4 1.5 %collective-permute-start = (f32[1,19,512]{2,1,0:T(8,128)S(1)}, f32[1,19,512]{2,1,0:T(8,128)S(1)}, u32[]{:S(2)}, u32[]{:S(2)}) collective-permute-start(f32[1,19,512]{2,1,0:T(8,128)S(1)} %fusion.14), channel_id=1, source_target_pairs={{0,1},{1,0},{2,3},{3,2},{4,5},{5,4},{6,7},{7,6},{8,9},{9,8},{10,11... | collective-permute-start | bytes 116744 | tf_op jit(solution)/shard_map/ppermute | solution.py:177
  133.9 2.6 %collective-permute-done = f32[1,19,512]{2,1,0:T(8,128)S(1)} collective-permute-done((f32[1,19,512]{2,1,0:T(8,128)S(1)}, f32[1,19,512]{2,1,0:T(8,128)S(1)}, u32[]{:S(2)}, u32[]{:S(2)}) %collective-permute-start) | collective-permute-done | bytes 38944 | tf_op jit(solution)/shard_map/ppermute | solution.py:177
  136.5 3.1 %collective-permute-start.1 = (f32[2,19,512]{2,1,0:T(8,128)S(1)}, f32[2,19,512]{2,1,0:T(8,128)S(1)}, u32[]{:S(2)}, u32[]{:S(2)}) collective-permute-start(f32[2,19,512]{2,1,0:T(8,128)S(1)} %pad_maximum_fusion.1), channel_id=1, source_target_pairs={{0,2},{1,3},{2,0},{3,1},{4,6},{5,7},{6,4},{7,5},{8,10},{9,11},{10,... | collective-permute-start | bytes 233480 | tf_op jit(solution)/shard_map/ppermute | solution.py:177
  139.6 3.1 %collective-permute-done.1 = f32[2,19,512]{2,1,0:T(8,128)S(1)} collective-permute-done((f32[2,19,512]{2,1,0:T(8,128)S(1)}, f32[2,19,512]{2,1,0:T(8,128)S(1)}, u32[]{:S(2)}, u32[]{:S(2)}) %collective-permute-start.1) | collective-permute-done | bytes 77856 | tf_op jit(solution)/shard_map/ppermute | solution.py:177
  142.9 0.2 multiply_reduce_fusion.1
  143.4 0.5 add_divide_fusion
  144.0 0.2 fusion.36
  144.1 0.2 multiply_reduce_fusion
  144.4 0.7 fusion.16
  (31 shorter events, 0.7 us)
Async XLA Ops:
  7.2 2.3 %copy-start = (f32[4,4,128]{2,1,0:T(4,128)S(1)}, f32[4,4,128]{2,1,0:T(4,128)}, u32[]{:S(2)}) copy-start(f32[4,4,128]{2,1,0:T(4,128)} %param.21) | copy-start | bytes 24580
  7.2 8.3 %copy-start.2 = (f32[8192]{0:T(1024)S(1)}, f32[8192]{0:T(1024)}, u32[]{:S(2)}) copy-start(f32[8192]{0:T(1024)} %param.18) | copy-start | bytes 98308
  7.2 97.6 %all-gather.3.cloned.1.call-start = ((), (), s32[]{:S(2)}) async-start(), calls=%async_computation | async-start | bytes 25952256 | tf_op jit(solution)/shard_map/all_gather | solution.py:144
  9.4 6.1 %copy-start.1 = (bf16[256,8192]{1,0:T(8,128)(2,1)S(1)}, bf16[256,8192]{1,0:T(8,128)(2,1)}, u32[]{:S(2)}) copy-start(bf16[256,8192]{1,0:T(8,128)(2,1)} %param.17) | copy-start | bytes 12582916
  117.3 22.3 %copy-start.3 = (s32[8]{0:T(128)S(1)}, s32[8]{0:T(128)}, u32[]{:S(2)}) copy-start(s32[8]{0:T(128)} %param.22) | copy-start | bytes 100
  132.4 4.2 %collective-permute-start = (f32[1,19,512]{2,1,0:T(8,128)S(1)}, f32[1,19,512]{2,1,0:T(8,128)S(1)}, u32[]{:S(2)}, u32[]{:S(2)}) collective-permute-start(f32[1,19,512]{2,1,0:T(8,128)S(1)} %fusion.14), channel_id=1, source_target_pairs={{0,1},{1,0},{2,3},{3,2},{4,5},{5,4},{6,7},{7,6},{8,9},{9,8},{10,11... | collective-permute-start | bytes 116744 | tf_op jit(solution)/shard_map/ppermute | solution.py:177
  136.5 6.2 %collective-permute-start.1 = (f32[2,19,512]{2,1,0:T(8,128)S(1)}, f32[2,19,512]{2,1,0:T(8,128)S(1)}, u32[]{:S(2)}, u32[]{:S(2)}) collective-permute-start(f32[2,19,512]{2,1,0:T(8,128)S(1)} %pad_maximum_fusion.1), channel_id=1, source_target_pairs={{0,2},{1,3},{2,0},{3,1},{4,6},{5,7},{6,4},{7,5},{8,10},{9,11},{10,... | collective-permute-start | bytes 233480 | tf_op jit(solution)/shard_map/ppermute | solution.py:177
Sparse Core Ops, SparseCore 0:
  10.3 94.5 all-gather.2

commit v6 on v4

--- a/solution.py
+++ b/solution.py
@@ -42,55 +42,14 @@
     return pooled / total
 
 
-def draft_kernel(tok_ref, g_ref, u_ref, head_ref, out_ref, gacc, uacc):
+def fused_kernel(x_ref, w_ref, tok_ref, g_ref, u_ref, head_ref, kv_ref, score_ref, gacc, uacc):
     j = pl.program_id(0)
 
     @pl.when(j == 0)
     def _():
+        kv_ref[...] = jnp.zeros_like(kv_ref)
         gacc[...] = jnp.zeros_like(gacc)
         uacc[...] = jnp.zeros_like(uacc)
-
-    t = tok_ref[...]
-    k = g_ref.shape[0] * g_ref.shape[1]
-    gacc[...] += jnp.dot(t, g_ref[...].reshape(k, -1), preferred_element_type=jnp.float32)
-    uacc[...] += jnp.dot(t, u_ref[...].reshape(k, -1), preferred_element_type=jnp.float32)
-
-    @pl.when(j == pl.num_programs(0) - 1)
-    def _():
-        g = gacc[...]
-        act = g / (1.0 + jnp.exp(-g))
-        out_ref[...] = jnp.sum(act * uacc[...] * head_ref[...], axis=1, keepdims=True)
-
-
-def draft_scores(tokens, gathered, head, row0, d_rows, group):
-    n_dev, _, cols = gathered.shape
-    n_tok = tokens.shape[0]
-    k = group * d_rows
-    gate_blk = row0 // d_rows
-    return pl.pallas_call(
-        draft_kernel,
-        grid=(n_dev // group,),
-        in_specs=[
-            pl.BlockSpec((n_tok, k), lambda j: (0, j)),
-            pl.BlockSpec((group, d_rows, cols), lambda j: (j, gate_blk, 0)),
-            pl.BlockSpec((group, d_rows, cols), lambda j: (j, gate_blk + 1, 0)),
-            pl.BlockSpec((1, cols), lambda j: (0, 0)),
-        ],
-        out_specs=pl.BlockSpec((n_tok, 1), lambda j: (0, 0)),
-        out_shape=jax.ShapeDtypeStruct((n_tok, 1), jnp.float32),
-        scratch_shapes=[
-            pltpu.VMEM((n_tok, cols), jnp.float32),
-            pltpu.VMEM((n_tok, cols), jnp.float32),
-        ],
-    )(tokens, gathered, gathered, head.reshape(1, cols))[:, 0]
-
-
-def kv_kernel(x_ref, w_ref, out_ref):
-    j = pl.program_id(0)
-
-    @pl.when(j == 0)
-    def _():
-        out_ref[...] = jnp.zeros_like(out_ref)
 
     group, rows, _ = w_ref.shape
     acc = jnp.dot(x_ref[:, 0:rows], w_ref[0], preferred_element_type=jnp.float32)
@@ -98,23 +57,53 @@
         acc += jnp.dot(
             x_ref[:, i * rows : (i + 1) * rows], w_ref[i], preferred_element_type=jnp.float32
         )
-    out_ref[...] += acc
-
-
-def kv_project(normed, gathered, v_rows, group):
+    kv_ref[...] += acc
+
+    t = tok_ref[...]
+    k = g_ref.shape[0] * g_ref.shape[1]
+    gacc[...] += jnp.dot(t, g_ref[...].reshape(k, -1), preferred_element_type=jnp.float32)
+    uacc[...] += jnp.dot(t, u_ref[...].reshape(k, -1), preferred_element_type=jnp.float32)
+
+    @pl.when(j == pl.num_programs(0) - 1)
+    def _():
+        g = gacc[...]
+        act = g / (1.0 + jnp.exp(-g))
+        col = jnp.sum(act * uacc[...] * head_ref[...], axis=1, keepdims=True)
+        wide = jnp.broadcast_to(col, (col.shape[0], 128))
+        score_ref[...] = jnp.transpose(wide)[0 : score_ref.shape[0], :]
+
+
+def project_all(normed, tokens, gathered, head, kv_rows, d_rows, steps):
     n_dev, _, cols = gathered.shape
-    n_tok = normed.shape[0]
-    k = group * v_rows
-    return pl.pallas_call(
-        kv_kernel,
-        grid=(n_dev // group,),
+    n_norm = normed.shape[0]
+    n_tok = tokens.shape[0]
+    group = n_dev // steps
+    gate_blk = kv_rows // d_rows
+    seg_kv, scores = pl.pallas_call(
+        fused_kernel,
+        grid=(steps,),
         in_specs=[
-            pl.BlockSpec((n_tok, k), lambda j: (0, j)),
-            pl.BlockSpec((group, v_rows, cols), lambda j: (j, 0, 0)),
-        ],
-        out_specs=pl.BlockSpec((n_tok, cols), lambda j: (0, 0)),
-        out_shape=jax.ShapeDtypeStruct((n_tok, cols), jnp.float32),
-    )(normed, gathered)
+            pl.BlockSpec((n_norm, group * kv_rows), lambda j: (0, j)),
+            pl.BlockSpec((group, kv_rows, cols), lambda j: (j, 0, 0)),
+            pl.BlockSpec((n_tok, group * d_rows), lambda j: (0, j)),
+            pl.BlockSpec((group, d_rows, cols), lambda j: (j, gate_blk, 0)),
+            pl.BlockSpec((group, d_rows, cols), lambda j: (j, gate_blk + 1, 0)),
+            pl.BlockSpec((1, cols), lambda j: (0, 0)),
+        ],
+        out_specs=[
+            pl.BlockSpec((n_norm, cols), lambda j: (0, 0)),
+            pl.BlockSpec((8, n_tok), lambda j: (0, 0)),
+        ],
+        out_shape=[
+            jax.ShapeDtypeStruct((n_norm, cols), jnp.float32),
+            jax.ShapeDtypeStruct((8, n_tok), jnp.float32),
+        ],
+        scratch_shapes=[
+            pltpu.VMEM((n_tok, cols), jnp.float32),
+            pltpu.VMEM((n_tok, cols), jnp.float32),
+        ],
+    )(normed, gathered, tokens, gathered, gathered, head.reshape(1, cols))
+    return seg_kv, scores[0]
 
 
 def local(
@@ -143,7 +132,9 @@
     kv_rows = kv_block.shape[0]
 
     normed = normalize_rows(verifier_rows, norm_gain)
-    seg_kv = kv_project(normed, gathered, kv_rows, 8)
+    seg_kv, partial_scores = project_all(
+        normed, draft_tokens, gathered, draft_head, kv_rows, d_rows, 4
+    )
     seg_keys = seg_kv[:, :kv_cols]
     seg_values = seg_kv[:, kv_cols:]
     lane_pick = (
@@ -158,7 +149,6 @@
     )
     width = KVH * HD
     live_row = jnp.zeros((1, width), jnp.float32).at[0, :seg_count].set(flags.astype(jnp.float32))
-    partial_scores = draft_scores(draft_tokens, gathered, draft_head, kv_rows, d_rows, 8)
     tail = jnp.concatenate(
         [
             partial_scores.reshape(-1, width),

time: 151 us -> 146 us (0.967)
  Pallas kernels: 24.4 us -> 20.3 us
    pallas_call x2 -> x1, Pallas kernels: 24.4 us -> 20.3 us  [project_all(): pl.pallas_call(fused_kernel, grid=(steps,), in_specs=[pl.BlockSpec((n_nor...]
where the time goes in v6:
time: 146 us
  waiting for transfers between devices  88.8 us (61%)
  Pallas kernels  20.3 us (14%)
  between operations  14.2 us (10%)
  other arithmetic  13.2 us (9%)
  starting transfers between devices  5.72 us (4%)
  local copies, waits for them, and re-layouts  2.69 us (2%)
    all_gather x1, waiting for transfers between devices, local(): gathered = lax.all_gather(block, 'fsdp', axis=0, tiled=False)  86.1 us
    pallas_call x1, Pallas kernels, project_all(): pl.pallas_call(fused_kernel, grid=(steps,), in_specs=[pl.BlockSpec((n_nor...  20.3 us
    ppermute x3, starting transfers between devices, local(): lax.ppermute(tail, 'seq', [(i, (i + k) % n_seq) for i in range(n_seq)])  5.68 us
    convert_element_type x1, other arithmetic, normalize_rows(): return (values * scale * norm_gain).astype(jnp.bfloat16)  3.16 us
    reduce_sum x1, other arithmetic, normalize_rows(): scale = lax.rsqrt(jnp.mean(values * values, axis=-1, keepdims=True) + eps)  3.1 us
  transfers between devices with their start and end apart: 4, of which 3 were waited for; matrix products, arithmetic and copies ran while one was open for 6% of the time, Pallas kernels for 0%

profile of v6, /device:TPU:0, one launch (start us, length us, event | category | flops | bytes accessed | tf_op | source)
XLA Modules:
  0.0 145.9 jit_solution(17648976305837826034)
XLA Ops:
  7.2 2.2 %pad_maximum_fusion = bf16[384,1024]{1,0:T(8,128)(2,1)} fusion(bf16[64,1024]{1,0:T(8,128)(2,1)} %param.15, bf16[64,1024]{1,0:T(8,128)(2,1)} %param.14, bf16[256,512]{1,0:T(8,128)(2,1)} %param.20, bf16[256,512]{1,0:T(8,128)(2,1)} %param.19), kind=kLoop, calls=%fused_computation.12 | loop fusion | flops 3145728 | bytes 1572864 | tf_op jit(solution)/shard_map/concatenate | solution.py:130
  9.4 1.0 fusion.19
  10.5 0.6 compare_reduce_fusion.1
  11.1 1.3 fusion.27
  12.4 3.1 %fusion.2 = f32[256]{0:T(256)S(1)} fusion(bf16[256,8192]{1,0:T(8,128)(2,1)} %param.17), kind=kLoop, calls=%fused_computation.4 | loop fusion | flops 6291200 | bytes 4195328 | tf_op jit(solution)/shard_map/reduce_sum | solution.py:20
  15.5 3.2 %fusion.4.x_ref = bf16[256,8192]{1,0:T(8,128)(2,1)} fusion(bf16[256,8192]{1,0:T(8,128)(2,1)S(1)} %copy-done.1, f32[8192]{0:T(1024)S(1)} %copy-done.2, f32[256]{0:T(256)S(1)} %add_rsqrt_fusion), kind=kLoop, calls=%fused_computation.6 | loop fusion | flops 8388608 | bytes 8422400 | tf_op jit(solution)/shard_map/convert_element_type | solution.py:21
  18.7 86.1 %all-gather.3.cloned.1.call-done = bf16[12288,1024]{1,0:T(8,128)(2,1)} async-done(((bf16[384,1024]{1,0:T(8,128)(2,1)}), bf16[12288,1024]{1,0:T(8,128)(2,1)}) %all-gather.3.cloned.1.call-update) | async-done | bytes 25165840 | tf_op jit(solution)/shard_map/all_gather | solution.py:131
  104.8 20.3 %shard_map.122 = (f32[256,1024]{1,0:T(8,128)}, f32[8,1024]{1,0:T(8,128)}) custom-call(bf16[256,8192]{1,0:T(8,128)(2,1)} %fusion.4.x_ref, bf16[32,384,1024]{2,1,0:T(8,128)(2,1)} %bitcast.31, bf16[1024,2048]{1,0:T(8,128)(2,1)} %tok_ref.1, bf16[32,384,1024]{2,1,0:T(8,128)(2,1)} %bitcast.32, bf16[32,384,1024]{2,1,0:T(8,128)(2,1)} %bitcast.33, f32[1,1024]{1,0:T(1,128)} %bitcast.48), custom_call_target="tpu_custom_call" | custom-call | tf_op jit(solution)/shard_map/pallas_call | solution.py:82
  125.1 1.3 fusion.35
  126.4 0.2 reshape.113
  126.6 0.4 multiply_reduce_fusion.4
  127.0 0.2 reshape.115
  127.2 0.8 slice_reduce_fusion
  128.0 0.3 multiply_reduce_fusion.3
  128.4 1.5 %collective-permute-start = (f32[19,512]{1,0:T(8,128)S(1)}, f32[19,512]{1,0:T(8,128)S(1)}, u32[]{:S(2)}, u32[]{:S(2)}) collective-permute-start(f32[19,512]{1,0:T(8,128)S(1)} %get-tuple-element.27), channel_id=1, source_target_pairs={{0,1},{1,2},{2,3},{3,0},{4,5},{5,6},{6,7},{7,4},{8,9},{9,10},{10,1... | collective-permute-start | bytes 116744 | tf_op jit(solution)/shard_map/ppermute | solution.py:164
  129.9 2.7 %collective-permute-start.1 = (f32[19,512]{1,0:T(8,128)S(1)}, f32[19,512]{1,0:T(8,128)S(1)}, u32[]{:S(2)}, u32[]{:S(2)}) collective-permute-start(f32[19,512]{1,0:T(8,128)S(1)} %get-tuple-element.27), channel_id=1, source_target_pairs={{0,2},{1,3},{2,0},{3,1},{4,6},{5,7},{6,4},{7,5},{8,10},{9,11},{10,... | collective-permute-start | bytes 116744 | tf_op jit(solution)/shard_map/ppermute | solution.py:164
  132.6 1.5 collective-permute-start.2
  134.1 1.5 %collective-permute-done.1 = f32[19,512]{1,0:T(8,128)S(1)} collective-permute-done((f32[19,512]{1,0:T(8,128)S(1)}, f32[19,512]{1,0:T(8,128)S(1)}, u32[]{:S(2)}, u32[]{:S(2)}) %collective-permute-start.1) | collective-permute-done | bytes 38944 | tf_op jit(solution)/shard_map/ppermute | solution.py:164
  135.5 1.1 collective-permute-done.2
  136.9 0.2 multiply_reduce_fusion.1
  137.4 0.5 add_divide_fusion
  137.9 0.2 fusion.36
  138.1 0.2 multiply_reduce_fusion
  138.4 0.7 fusion.15
  (31 shorter events, 0.7 us)
Async XLA Ops:
  7.2 2.3 %copy-start = (f32[4,4,128]{2,1,0:T(4,128)S(1)}, f32[4,4,128]{2,1,0:T(4,128)}, u32[]{:S(2)}) copy-start(f32[4,4,128]{2,1,0:T(4,128)} %param.21) | copy-start | bytes 24580
  7.2 8.3 %copy-start.2 = (f32[8192]{0:T(1024)S(1)}, f32[8192]{0:T(1024)}, u32[]{:S(2)}) copy-start(f32[8192]{0:T(1024)} %param.18) | copy-start | bytes 98308
  7.2 97.6 %all-gather.3.cloned.1.call-start = ((), (), s32[]{:S(2)}) async-start(), calls=%async_computation | async-start | bytes 25952256 | tf_op jit(solution)/shard_map/all_gather | solution.py:131
  9.4 6.1 %copy-start.1 = (bf16[256,8192]{1,0:T(8,128)(2,1)S(1)}, bf16[256,8192]{1,0:T(8,128)(2,1)}, u32[]{:S(2)}) copy-start(bf16[256,8192]{1,0:T(8,128)(2,1)} %param.17) | copy-start | bytes 12582916
  125.1 8.9 %copy-start.3 = (s32[8]{0:T(128)S(1)}, s32[8]{0:T(128)}, u32[]{:S(2)}) copy-start(s32[8]{0:T(128)} %param.22) | copy-start | bytes 100
  128.4 5.7 %collective-permute-start = (f32[19,512]{1,0:T(8,128)S(1)}, f32[19,512]{1,0:T(8,128)S(1)}, u32[]{:S(2)}, u32[]{:S(2)}) collective-permute-start(f32[19,512]{1,0:T(8,128)S(1)} %get-tuple-element.27), channel_id=1, source_target_pairs={{0,1},{1,2},{2,3},{3,0},{4,5},{5,6},{6,7},{7,4},{8,9},{9,10},{10,1... | collective-permute-start | bytes 116744 | tf_op jit(solution)/shard_map/ppermute | solution.py:164
  129.9 5.6 %collective-permute-start.1 = (f32[19,512]{1,0:T(8,128)S(1)}, f32[19,512]{1,0:T(8,128)S(1)}, u32[]{:S(2)}, u32[]{:S(2)}) collective-permute-start(f32[19,512]{1,0:T(8,128)S(1)} %get-tuple-element.27), channel_id=1, source_target_pairs={{0,2},{1,3},{2,0},{3,1},{4,6},{5,7},{6,4},{7,5},{8,10},{9,11},{10,... | collective-permute-start | bytes 116744 | tf_op jit(solution)/shard_map/ppermute | solution.py:164
  132.6 4.1 %collective-permute-start.2 = (f32[19,512]{1,0:T(8,128)S(1)}, f32[19,512]{1,0:T(8,128)S(1)}, u32[]{:S(2)}, u32[]{:S(2)}) collective-permute-start(f32[19,512]{1,0:T(8,128)S(1)} %get-tuple-element.27), channel_id=1, source_target_pairs={{0,3},{1,0},{2,1},{3,2},{4,7},{5,4},{6,5},{7,6},{8,11},{9,8},{10,9... | collective-permute-start | bytes 116744 | tf_op jit(solution)/shard_map/ppermute | solution.py:164
Sparse Core Ops, SparseCore 0:
  10.3 94.5 all-gather.2

commit v7 on v6

--- a/solution.py
+++ b/solution.py
@@ -42,7 +42,10 @@
     return pooled / total
 
 
-def fused_kernel(x_ref, w_ref, tok_ref, g_ref, u_ref, head_ref, kv_ref, score_ref, gacc, uacc):
+def fused_kernel(
+    x_ref, k_ref, v_ref, tok_ref, glo_ref, ghi_ref, ulo_ref, uhi_ref, head_ref,
+    kv_ref, score_ref, gacc, uacc,
+):
     j = pl.program_id(0)
 
     @pl.when(j == 0)
@@ -51,18 +54,29 @@
         gacc[...] = jnp.zeros_like(gacc)
         uacc[...] = jnp.zeros_like(uacc)
 
-    group, rows, _ = w_ref.shape
-    acc = jnp.dot(x_ref[:, 0:rows], w_ref[0], preferred_element_type=jnp.float32)
-    for i in range(1, group):
-        acc += jnp.dot(
-            x_ref[:, i * rows : (i + 1) * rows], w_ref[i], preferred_element_type=jnp.float32
-        )
-    kv_ref[...] += acc
+    def blocks_dot(x, w_ref):
+        group, rows, _ = w_ref.shape
+        acc = jnp.dot(x[:, 0:rows], w_ref[0], preferred_element_type=jnp.float32)
+        for i in range(1, group):
+            acc += jnp.dot(x[:, i * rows : (i + 1) * rows], w_ref[i], preferred_element_type=jnp.float32)
+        return acc
+
+    half = k_ref.shape[2]
+    x = x_ref[...]
+    kv_ref[:, 0:half] += blocks_dot(x, k_ref)
+    kv_ref[:, half:] += blocks_dot(x, v_ref)
 
     t = tok_ref[...]
-    k = g_ref.shape[0] * g_ref.shape[1]
-    gacc[...] += jnp.dot(t, g_ref[...].reshape(k, -1), preferred_element_type=jnp.float32)
-    uacc[...] += jnp.dot(t, u_ref[...].reshape(k, -1), preferred_element_type=jnp.float32)
+    k = glo_ref.shape[0] * glo_ref.shape[1]
+    dh = glo_ref.shape[2]
+
+    def flat_dot(w_ref):
+        return jnp.dot(t, w_ref[...].reshape(k, -1), preferred_element_type=jnp.float32)
+
+    gacc[:, 0:dh] += flat_dot(glo_ref)
+    gacc[:, dh:] += flat_dot(ghi_ref)
+    uacc[:, 0:dh] += flat_dot(ulo_ref)
+    uacc[:, dh:] += flat_dot(uhi_ref)
 
     @pl.when(j == pl.num_programs(0) - 1)
     def _():
@@ -74,35 +88,40 @@
 
 
 def project_all(normed, tokens, gathered, head, kv_rows, d_rows, steps):
-    n_dev, _, cols = gathered.shape
+    n_dev, _, half = gathered.shape
     n_norm = normed.shape[0]
     n_tok = tokens.shape[0]
     group = n_dev // steps
-    gate_blk = kv_rows // d_rows
+    g0 = 2 * kv_rows // d_rows
+    w_spec = lambda row_blk: pl.BlockSpec((group, kv_rows, half), lambda j: (j, row_blk, 0))
+    d_spec = lambda row_blk: pl.BlockSpec((group, d_rows, half), lambda j: (j, row_blk, 0))
     seg_kv, scores = pl.pallas_call(
         fused_kernel,
         grid=(steps,),
         in_specs=[
             pl.BlockSpec((n_norm, group * kv_rows), lambda j: (0, j)),
-            pl.BlockSpec((group, kv_rows, cols), lambda j: (j, 0, 0)),
+            w_spec(0),
+            w_spec(1),
             pl.BlockSpec((n_tok, group * d_rows), lambda j: (0, j)),
-            pl.BlockSpec((group, d_rows, cols), lambda j: (j, gate_blk, 0)),
-            pl.BlockSpec((group, d_rows, cols), lambda j: (j, gate_blk + 1, 0)),
-            pl.BlockSpec((1, cols), lambda j: (0, 0)),
+            d_spec(g0),
+            d_spec(g0 + 1),
+            d_spec(g0 + 2),
+            d_spec(g0 + 3),
+            pl.BlockSpec((1, 2 * half), lambda j: (0, 0)),
         ],
         out_specs=[
-            pl.BlockSpec((n_norm, cols), lambda j: (0, 0)),
+            pl.BlockSpec((n_norm, 2 * half), lambda j: (0, 0)),
             pl.BlockSpec((8, n_tok), lambda j: (0, 0)),
         ],
         out_shape=[
-            jax.ShapeDtypeStruct((n_norm, cols), jnp.float32),
+            jax.ShapeDtypeStruct((n_norm, 2 * half), jnp.float32),
             jax.ShapeDtypeStruct((8, n_tok), jnp.float32),
         ],
         scratch_shapes=[
-            pltpu.VMEM((n_tok, cols), jnp.float32),
-            pltpu.VMEM((n_tok, cols), jnp.float32),
-        ],
-    )(normed, gathered, tokens, gathered, gathered, head.reshape(1, cols))
+            pltpu.VMEM((n_tok, 2 * half), jnp.float32),
+            pltpu.VMEM((n_tok, 2 * half), jnp.float32),
+        ],
+    )(normed, gathered, gathered, tokens, gathered, gathered, gathered, gathered, head.reshape(1, -1))
     return seg_kv, scores[0]
 
 
@@ -125,11 +144,20 @@
     d_rows, d_cols = draft_gate.shape
     v_rows = key_weight.shape[0]
     kv_cols = key_weight.shape[1]
-    kv_block = jnp.concatenate([key_weight, value_weight], axis=1)
-    kv_block = kv_block.reshape(-1, d_cols)
-    block = jnp.concatenate([kv_block, draft_gate, draft_up], axis=0)
+    dh = d_cols // 2
+    block = jnp.concatenate(
+        [
+            key_weight,
+            value_weight,
+            draft_gate[:, :dh],
+            draft_gate[:, dh:],
+            draft_up[:, :dh],
+            draft_up[:, dh:],
+        ],
+        axis=0,
+    )
     gathered = lax.all_gather(block, "fsdp", axis=0, tiled=False)
-    kv_rows = kv_block.shape[0]
+    kv_rows = v_rows
 
     normed = normalize_rows(verifier_rows, norm_gain)
     seg_kv, partial_scores = project_all(

time: 146 us -> 150 us (1.027)
  local copies, waits for them, and re-layouts: 2.69 us -> 8.91 us
  waiting for transfers between devices: 88.8 us -> 86 us
    unnamed x9 -> x12, local copies, waits for them, and re-layouts: 0.03 us -> 5.41 us
    all_gather x1, waiting for transfers between devices: 86.1 us -> 83.4 us  [local(): gathered = lax.all_gather(block, 'fsdp', axis=0, tiled=False)]
    convert_element_type x1, other arithmetic: 3.16 us -> 5.34 us  [normalize_rows(): return (values * scale * norm_gain).astype(jnp.bfloat16)]
    concatenate x1 -> x0, other arithmetic: 2.16 us -> none  [local(): block = jnp.concatenate([kv_block, draft_gate, draft_up], axis=0)]
  transfers between devices with their start and end apart: 4 -> 4, of which waited for: 3 -> 3; matrix products, arithmetic and copies ran while one was open for 6% -> 8% of each run, Pallas kernels for 0% -> 0%
where the time goes in v7:
time: 150 us; the launch traced here: 149 us
  waiting for transfers between devices  86 us (57%)
  Pallas kernels  20.3 us (14%)
  between operations  14.2 us (9%)
  other arithmetic  13.3 us (9%)
  local copies, waits for them, and re-layouts  8.91 us (6%)
  starting transfers between devices  5.72 us (4%)
    all_gather x1, waiting for transfers between devices, local(): gathered = lax.all_gather(block, 'fsdp', axis=0, tiled=False)  83.4 us
    pallas_call x1, Pallas kernels, project_all(): pl.pallas_call(fused_kernel, grid=(steps,), in_specs=[pl.BlockSpec((n_nor...  20.3 us
    ppermute x3, starting transfers between devices, local(): lax.ppermute(tail, 'seq', [(i, (i + k) % n_seq) for i in range(n_seq)])  5.68 us
    unnamed x12, local copies, waits for them, and re-layouts  5.41 us
    convert_element_type x1, other arithmetic, normalize_rows(): return (values * scale * norm_gain).astype(jnp.bfloat16)  5.34 us
    reduce_sum x1, other arithmetic, normalize_rows(): scale = lax.rsqrt(jnp.mean(values * values, axis=-1, keepdims=True) + eps)  3.1 us
  transfers between devices with their start and end apart: 4, of which 3 were waited for; matrix products, arithmetic and copies ran while one was open for 8% of the time, Pallas kernels for 0%

profile of v7, /device:TPU:0, one launch (start us, length us, event | category | flops | bytes accessed | tf_op | source)
XLA Modules:
  0.0 149.3 jit_solution(7648007323787276311)
XLA Ops:
  7.2 1.0 constant_dynamic-update-slice_fusion.1
  8.2 1.0 constant_dynamic-update-slice_fusion
  9.2 0.8 slice_dynamic-update-slice_fusion.3
  10.0 0.8 slice_dynamic-update-slice_fusion.2
  10.9 0.8 slice_dynamic-update-slice_fusion.1
  11.7 0.8 slice_dynamic-update-slice_fusion
  12.6 0.9 copy-done.1
  13.5 0.9 fusion.19
  14.4 0.6 compare_reduce_fusion.1
  15.0 1.3 fusion.27
  16.3 3.1 %fusion.2 = f32[256]{0:T(256)S(1)} fusion(bf16[256,8192]{1,0:T(8,128)(2,1)} %param.17), kind=kLoop, calls=%fused_computation.4 | loop fusion | flops 6291200 | bytes 4195328 | tf_op jit(solution)/shard_map/reduce_sum | solution.py:20
  19.4 5.3 %fusion.4.x_ref = bf16[256,8192]{1,0:T(8,128)(2,1)} fusion(bf16[256,8192]{1,0:T(8,128)(2,1)} %param.17, f32[8192]{0:T(1024)} %param.18, f32[256]{0:T(256)S(1)} %add_rsqrt_fusion), kind=kLoop, calls=%fused_computation.6 | loop fusion | flops 8388608 | bytes 8422400 | tf_op jit(solution)/shard_map/convert_element_type | solution.py:21
  24.8 83.4 %all-gather.3.cloned.1.call-done = bf16[24576,512]{1,0:T(8,128)(2,1)} async-done(((bf16[768,512]{1,0:T(8,128)(2,1)}), bf16[24576,512]{1,0:T(8,128)(2,1)}) %all-gather.3.cloned.1.call-update) | async-done | bytes 25165840 | tf_op jit(solution)/shard_map/all_gather | solution.py:159
  108.2 20.3 %shard_map.122 = (f32[256,1024]{1,0:T(8,128)}, f32[8,1024]{1,0:T(8,128)}) custom-call(bf16[256,8192]{1,0:T(8,128)(2,1)} %fusion.4.x_ref, bf16[32,768,512]{2,1,0:T(8,128)(2,1)} %bitcast.31, bf16[32,768,512]{2,1,0:T(8,128)(2,1)} %bitcast.32, bf16[1024,2048]{1,0:T(8,128)(2,1)} %tok_ref.1, bf16[32,768,512]{2,1,0:T(8,128)(2,1)} %bitcast.33, ...), custom_call_target="tpu_custom_call" | custom-call | tf_op jit(solution)/shard_map/pallas_call | solution.py:98
  128.5 1.3 fusion.35
  130.0 0.4 multiply_reduce_fusion.4
  130.6 0.8 slice_reduce_fusion
  131.8 1.5 %collective-permute-start = (f32[19,512]{1,0:T(8,128)S(1)}, f32[19,512]{1,0:T(8,128)S(1)}, u32[]{:S(2)}, u32[]{:S(2)}) collective-permute-start(f32[19,512]{1,0:T(8,128)S(1)} %get-tuple-element.27), channel_id=1, source_target_pairs={{0,1},{1,2},{2,3},{3,0},{4,5},{5,6},{6,7},{7,4},{8,9},{9,10},{10,1... | collective-permute-start | bytes 116744 | tf_op jit(solution)/shard_map/ppermute | solution.py:192
  133.3 2.7 %collective-permute-start.1 = (f32[19,512]{1,0:T(8,128)S(1)}, f32[19,512]{1,0:T(8,128)S(1)}, u32[]{:S(2)}, u32[]{:S(2)}) collective-permute-start(f32[19,512]{1,0:T(8,128)S(1)} %get-tuple-element.27), channel_id=1, source_target_pairs={{0,2},{1,3},{2,0},{3,1},{4,6},{5,7},{6,4},{7,5},{8,10},{9,11},{10,... | collective-permute-start | bytes 116744 | tf_op jit(solution)/shard_map/ppermute | solution.py:192
  136.0 1.5 collective-permute-start.2
  137.4 1.5 collective-permute-done.1
  138.9 1.1 collective-permute-done.2
  140.8 0.5 add_divide_fusion
  141.8 0.7 fusion.15
  (34 shorter events, 2.0 us)
Async XLA Ops:
  7.2 6.3 %copy-start = (f32[4,4,128]{2,1,0:T(4,128)S(1)}, f32[4,4,128]{2,1,0:T(4,128)}, u32[]{:S(2)}) copy-start(f32[4,4,128]{2,1,0:T(4,128)} %param.21) | copy-start | bytes 24580
  7.2 101.0 %all-gather.3.cloned.1.call-start = ((), (), s32[]{:S(2)}) async-start(), calls=%async_computation | async-start | bytes 25952256 | tf_op jit(solution)/shard_map/all_gather | solution.py:159
  12.5 0.9 copy-start.1
  108.2 29.3 %copy-start.2 = (s32[8]{0:T(128)S(1)}, s32[8]{0:T(128)}, u32[]{:S(2)}) copy-start(s32[8]{0:T(128)} %param.22) | copy-start | bytes 100
  131.8 5.7 %collective-permute-start = (f32[19,512]{1,0:T(8,128)S(1)}, f32[19,512]{1,0:T(8,128)S(1)}, u32[]{:S(2)}, u32[]{:S(2)}) collective-permute-start(f32[19,512]{1,0:T(8,128)S(1)} %get-tuple-element.27), channel_id=1, source_target_pairs={{0,1},{1,2},{2,3},{3,0},{4,5},{5,6},{6,7},{7,4},{8,9},{9,10},{10,1... | collective-permute-start | bytes 116744 | tf_op jit(solution)/shard_map/ppermute | solution.py:192
  133.3 5.6 %collective-permute-start.1 = (f32[19,512]{1,0:T(8,128)S(1)}, f32[19,512]{1,0:T(8,128)S(1)}, u32[]{:S(2)}, u32[]{:S(2)}) collective-permute-start(f32[19,512]{1,0:T(8,128)S(1)} %get-tuple-element.27), channel_id=1, source_target_pairs={{0,2},{1,3},{2,0},{3,1},{4,6},{5,7},{6,4},{7,5},{8,10},{9,11},{10,... | collective-permute-start | bytes 116744 | tf_op jit(solution)/shard_map/ppermute | solution.py:192
  136.0 4.1 %collective-permute-start.2 = (f32[19,512]{1,0:T(8,128)S(1)}, f32[19,512]{1,0:T(8,128)S(1)}, u32[]{:S(2)}, u32[]{:S(2)}) collective-permute-start(f32[19,512]{1,0:T(8,128)S(1)} %get-tuple-element.27), channel_id=1, source_target_pairs={{0,3},{1,0},{2,1},{3,2},{4,7},{5,4},{6,5},{7,6},{8,11},{9,8},{10,9... | collective-permute-start | bytes 116744 | tf_op jit(solution)/shard_map/ppermute | solution.py:192
Sparse Core Ops, SparseCore 0:
  13.6 94.5 all-gather.2

commit v8 on v6

--- a/solution.py
+++ b/solution.py
@@ -104,6 +104,34 @@
         ],
     )(normed, gathered, tokens, gathered, gathered, head.reshape(1, cols))
     return seg_kv, scores[0]
+
+
+def pack_kernel(k_hbm, v_hbm, g_hbm, u_hbm, out_hbm, sems):
+    rows, half = k_hbm.shape
+    d_rows = g_hbm.shape[0]
+    copies = [
+        pltpu.make_async_copy(k_hbm, out_hbm.at[0:rows, 0:half], sems.at[0]),
+        pltpu.make_async_copy(v_hbm, out_hbm.at[0:rows, half : 2 * half], sems.at[1]),
+        pltpu.make_async_copy(g_hbm, out_hbm.at[rows : rows + d_rows, :], sems.at[2]),
+        pltpu.make_async_copy(u_hbm, out_hbm.at[rows + d_rows : rows + 2 * d_rows, :], sems.at[3]),
+    ]
+    for c in copies:
+        c.start()
+    for c in copies:
+        c.wait()
+
+
+def pack_block(key_weight, value_weight, draft_gate, draft_up):
+    rows, half = key_weight.shape
+    d_rows, cols = draft_gate.shape
+    any_spec = pl.BlockSpec(memory_space=pl.ANY)
+    return pl.pallas_call(
+        pack_kernel,
+        in_specs=[any_spec] * 4,
+        out_specs=any_spec,
+        out_shape=jax.ShapeDtypeStruct((rows + 2 * d_rows, cols), key_weight.dtype),
+        scratch_shapes=[pltpu.SemaphoreType.DMA((4,))],
+    )(key_weight, value_weight, draft_gate, draft_up)
 
 
 def local(
@@ -125,11 +153,9 @@
     d_rows, d_cols = draft_gate.shape
     v_rows = key_weight.shape[0]
     kv_cols = key_weight.shape[1]
-    kv_block = jnp.concatenate([key_weight, value_weight], axis=1)
-    kv_block = kv_block.reshape(-1, d_cols)
-    block = jnp.concatenate([kv_block, draft_gate, draft_up], axis=0)
+    block = pack_block(key_weight, value_weight, draft_gate, draft_up)
     gathered = lax.all_gather(block, "fsdp", axis=0, tiled=False)
-    kv_rows = kv_block.shape[0]
+    kv_rows = key_weight.shape[0]
 
     normed = normalize_rows(verifier_rows, norm_gain)
     seg_kv, partial_scores = project_all(

time: 146 us -> 168 us (1.15)
  Pallas kernels: 20.3 us -> 45.3 us
  waiting for transfers between devices: 88.8 us -> 86 us
    pallas_call x0 -> x1, Pallas kernels: none -> 25 us  [pack_block(): pl.pallas_call(pack_kernel, in_specs=[any_spec] * 4, out_specs=any_spec,...]
    all_gather x1, waiting for transfers between devices: 86.1 us -> 83.4 us  [local(): gathered = lax.all_gather(block, 'fsdp', axis=0, tiled=False)]
    convert_element_type x1, other arithmetic: 3.16 us -> 5.34 us  [normalize_rows(): return (values * scale * norm_gain).astype(jnp.bfloat16)]
    concatenate x1 -> x0, other arithmetic: 2.16 us -> none  [local(): block = jnp.concatenate([kv_block, draft_gate, draft_up], axis=0)]
  transfers between devices with their start and end apart: 4 -> 4, of which waited for: 3 -> 3; matrix products, arithmetic and copies ran while one was open for 6% -> 7% of each run, Pallas kernels for 0% -> 0%
where the time goes in v8:
time: 168 us
  waiting for transfers between devices  86 us (51%)
  Pallas kernels  45.3 us (27%)
  between operations  14.2 us (8%)
  other arithmetic  13.3 us (8%)
  starting transfers between devices  5.72 us (3%)
  local copies, waits for them, and re-layouts  2.67 us (2%)
    all_gather x1, waiting for transfers between devices, local(): gathered = lax.all_gather(block, 'fsdp', axis=0, tiled=False)  83.4 us
    pallas_call x1, Pallas kernels, pack_block(): pl.pallas_call(pack_kernel, in_specs=[any_spec] * 4, out_specs=any_spec,...  25 us
    pallas_call x1, Pallas kernels, project_all(): pl.pallas_call(fused_kernel, grid=(steps,), in_specs=[pl.BlockSpec((n_nor...  20.3 us
    ppermute x3, starting transfers between devices, local(): lax.ppermute(tail, 'seq', [(i, (i + k) % n_seq) for i in range(n_seq)])  5.68 us
    convert_element_type x1, other arithmetic, normalize_rows(): return (values * scale * norm_gain).astype(jnp.bfloat16)  5.34 us
  transfers between devices with their start and end apart: 4, of which 3 were waited for; matrix products, arithmetic and copies ran while one was open for 7% of the time, Pallas kernels for 0%

profile of v8, /device:TPU:0, one launch (start us, length us, event | category | flops | bytes accessed | tf_op | source)
XLA Modules:
  0.0 168.0 jit_solution(475416346504246478)
XLA Ops:
  7.2 25.0 %shard_map.122 = bf16[384,1024]{1,0:T(8,128)(2,1)} custom-call(bf16[256,512]{1,0:T(8,128)(2,1)} %k_hbm.1, bf16[256,512]{1,0:T(8,128)(2,1)} %v_hbm.1, bf16[64,1024]{1,0:T(8,128)(2,1)} %g_hbm.1, bf16[64,1024]{1,0:T(8,128)(2,1)} %u_hbm.1), custom_call_target="tpu_custom_call" | custom-call | tf_op jit(solution)/shard_map/pallas_call | solution.py:128
  32.2 0.9 fusion.19
  33.1 0.6 compare_reduce_fusion.1
  33.7 1.3 fusion.27
  35.0 3.1 %fusion.2 = f32[256]{0:T(256)S(1)} fusion(bf16[256,8192]{1,0:T(8,128)(2,1)} %param.17), kind=kLoop, calls=%fused_computation.4 | loop fusion | flops 6291200 | bytes 4195328 | tf_op jit(solution)/shard_map/reduce_sum | solution.py:20
  38.2 5.3 %fusion.4.x_ref = bf16[256,8192]{1,0:T(8,128)(2,1)} fusion(bf16[256,8192]{1,0:T(8,128)(2,1)} %param.17, f32[8192]{0:T(1024)} %param.18, f32[256]{0:T(256)S(1)} %add_rsqrt_fusion), kind=kLoop, calls=%fused_computation.6 | loop fusion | flops 8388608 | bytes 8422400 | tf_op jit(solution)/shard_map/convert_element_type | solution.py:21
  43.5 83.4 %all-gather.3.cloned.1.call-done = bf16[12288,1024]{1,0:T(8,128)(2,1)} async-done(((bf16[384,1024]{1,0:T(8,128)(2,1)}), bf16[12288,1024]{1,0:T(8,128)(2,1)}) %all-gather.3.cloned.1.call-update) | async-done | bytes 25165840 | tf_op jit(solution)/shard_map/all_gather | solution.py:157
  126.9 20.3 %shard_map.123 = (f32[256,1024]{1,0:T(8,128)}, f32[8,1024]{1,0:T(8,128)}) custom-call(bf16[256,8192]{1,0:T(8,128)(2,1)} %fusion.4.x_ref, bf16[32,384,1024]{2,1,0:T(8,128)(2,1)} %bitcast.31, bf16[1024,2048]{1,0:T(8,128)(2,1)} %tok_ref.1, bf16[32,384,1024]{2,1,0:T(8,128)(2,1)} %bitcast.32, bf16[32,384,1024]{2,1,0:T(8,128)(2,1)} %bitcast.33, f32[1,1024]{1,0:T(1,128)} %bitcast.48), custom_call_target="tpu_custom_call" | custom-call | tf_op jit(solution)/shard_map/pallas_call | solution.py:82
  147.2 1.3 fusion.35
  148.5 0.2 reshape.113
  148.7 0.4 multiply_reduce_fusion.4
  149.1 0.2 reshape.115
  149.3 0.8 slice_reduce_fusion
  150.1 0.3 multiply_reduce_fusion.3
  150.4 1.5 collective-permute-start
  152.0 2.7 %collective-permute-start.1 = (f32[19,512]{1,0:T(8,128)S(1)}, f32[19,512]{1,0:T(8,128)S(1)}, u32[]{:S(2)}, u32[]{:S(2)}) collective-permute-start(f32[19,512]{1,0:T(8,128)S(1)} %get-tuple-element.27), channel_id=1, source_target_pairs={{0,2},{1,3},{2,0},{3,1},{4,6},{5,7},{6,4},{7,5},{8,10},{9,11},{10,... | collective-permute-start | bytes 116744 | tf_op jit(solution)/shard_map/ppermute | solution.py:190
  154.7 1.5 collective-permute-start.2
  156.1 1.5 collective-permute-done.1
  157.6 1.1 collective-permute-done.2
  158.9 0.2 multiply_reduce_fusion.1
  159.5 0.5 add_divide_fusion
  160.0 0.2 fusion.36
  160.1 0.2 multiply_reduce_fusion
  160.5 0.7 fusion.15
  (27 shorter events, 0.7 us)
Async XLA Ops:
  7.2 25.1 %copy-start = (f32[4,4,128]{2,1,0:T(4,128)S(1)}, f32[4,4,128]{2,1,0:T(4,128)}, u32[]{:S(2)}) copy-start(f32[4,4,128]{2,1,0:T(4,128)} %param.21) | copy-start | bytes 24580
  7.2 119.7 %all-gather.3.cloned.1.call-start = ((), (), s32[]{:S(2)}) async-start(), calls=%async_computation | async-start | bytes 25952256 | tf_op jit(solution)/shard_map/all_gather | solution.py:157
  126.9 29.2 %copy-start.1 = (s32[8]{0:T(128)S(1)}, s32[8]{0:T(128)}, u32[]{:S(2)}) copy-start(s32[8]{0:T(128)} %param.22) | copy-start | bytes 100
  150.4 5.7 %collective-permute-start = (f32[19,512]{1,0:T(8,128)S(1)}, f32[19,512]{1,0:T(8,128)S(1)}, u32[]{:S(2)}, u32[]{:S(2)}) collective-permute-start(f32[19,512]{1,0:T(8,128)S(1)} %get-tuple-element.27), channel_id=1, source_target_pairs={{0,1},{1,2},{2,3},{3,0},{4,5},{5,6},{6,7},{7,4},{8,9},{9,10},{10,1... | collective-permute-start | bytes 116744 | tf_op jit(solution)/shard_map/ppermute | solution.py:190
  152.0 5.6 %collective-permute-start.1 = (f32[19,512]{1,0:T(8,128)S(1)}, f32[19,512]{1,0:T(8,128)S(1)}, u32[]{:S(2)}, u32[]{:S(2)}) collective-permute-start(f32[19,512]{1,0:T(8,128)S(1)} %get-tuple-element.27), channel_id=1, source_target_pairs={{0,2},{1,3},{2,0},{3,1},{4,6},{5,7},{6,4},{7,5},{8,10},{9,11},{10,... | collective-permute-start | bytes 116744 | tf_op jit(solution)/shard_map/ppermute | solution.py:190
  154.7 4.1 %collective-permute-start.2 = (f32[19,512]{1,0:T(8,128)S(1)}, f32[19,512]{1,0:T(8,128)S(1)}, u32[]{:S(2)}, u32[]{:S(2)}) collective-permute-start(f32[19,512]{1,0:T(8,128)S(1)} %get-tuple-element.27), channel_id=1, source_target_pairs={{0,3},{1,0},{2,1},{3,2},{4,7},{5,4},{6,5},{7,6},{8,11},{9,8},{10,9... | collective-permute-start | bytes 116744 | tf_op jit(solution)/shard_map/ppermute | solution.py:190
Sparse Core Ops, SparseCore 0:
  32.3 94.5 all-gather.2

commit v9 on v6

--- a/solution.py
+++ b/solution.py
@@ -42,7 +42,9 @@
     return pooled / total
 
 
-def fused_kernel(x_ref, w_ref, tok_ref, g_ref, u_ref, head_ref, kv_ref, score_ref, gacc, uacc):
+def fused_kernel(
+    x_ref, w_ref, tok_ref, g_ref, u_ref, head_ref, q_ref, live_ref, tail_ref, kv_ref, gacc, uacc
+):
     j = pl.program_id(0)
 
     @pl.when(j == 0)
@@ -70,16 +72,39 @@
         act = g / (1.0 + jnp.exp(-g))
         col = jnp.sum(act * uacc[...] * head_ref[...], axis=1, keepdims=True)
         wide = jnp.broadcast_to(col, (col.shape[0], 128))
-        score_ref[...] = jnp.transpose(wide)[0 : score_ref.shape[0], :]
-
-
-def project_all(normed, tokens, gathered, head, kv_rows, d_rows, steps):
+        row = jnp.transpose(wide)[0:1, :]
+        width = tail_ref.shape[1]
+        score_rows = row.shape[1] // width
+        for r in range(score_rows):
+            tail_ref[r : r + 1, :] = row[:, r * width : (r + 1) * width]
+        segs = q_ref.shape[0]
+        kv = kv_ref[...]
+        keys = kv[:, 0:width].reshape(segs, -1, width)
+        values = kv[:, width:].reshape(segs, -1, width)
+        prod = keys * q_ref[...]
+        for h in range(width // HD):
+            lanes = slice(h * HD, (h + 1) * HD)
+            sc = jnp.sum(prod[:, :, lanes], axis=2, keepdims=True) / math.sqrt(HD)
+            sc = sc - jnp.max(sc, axis=1, keepdims=True)
+            wt = jnp.exp(sc)
+            wt = wt / jnp.sum(wt, axis=1, keepdims=True)
+            r0 = score_rows
+            tail_ref[r0 : r0 + segs, lanes] = jnp.sum(wt * keys[:, :, lanes], axis=1)
+            r0 = score_rows + segs
+            tail_ref[r0 : r0 + segs, lanes] = jnp.sum(wt * values[:, :, lanes], axis=1)
+        tail_ref[score_rows + 2 * segs :, :] = live_ref[...]
+
+
+def project_all(normed, tokens, gathered, head, queries, live_row, kv_rows, d_rows, steps):
     n_dev, _, cols = gathered.shape
     n_norm = normed.shape[0]
     n_tok = tokens.shape[0]
+    segs = queries.shape[0]
+    width = queries.shape[2]
+    tail_rows = n_tok // width + 2 * segs + 1
     group = n_dev // steps
     gate_blk = kv_rows // d_rows
-    seg_kv, scores = pl.pallas_call(
+    return pl.pallas_call(
         fused_kernel,
         grid=(steps,),
         in_specs=[
@@ -89,21 +114,17 @@
             pl.BlockSpec((group, d_rows, cols), lambda j: (j, gate_blk, 0)),
             pl.BlockSpec((group, d_rows, cols), lambda j: (j, gate_blk + 1, 0)),
             pl.BlockSpec((1, cols), lambda j: (0, 0)),
+            pl.BlockSpec(queries.shape, lambda j: (0, 0, 0)),
+            pl.BlockSpec(live_row.shape, lambda j: (0, 0)),
         ],
-        out_specs=[
-            pl.BlockSpec((n_norm, cols), lambda j: (0, 0)),
-            pl.BlockSpec((8, n_tok), lambda j: (0, 0)),
-        ],
-        out_shape=[
-            jax.ShapeDtypeStruct((n_norm, cols), jnp.float32),
-            jax.ShapeDtypeStruct((8, n_tok), jnp.float32),
-        ],
+        out_specs=pl.BlockSpec((tail_rows, width), lambda j: (0, 0)),
+        out_shape=jax.ShapeDtypeStruct((tail_rows, width), jnp.float32),
         scratch_shapes=[
+            pltpu.VMEM((n_norm, cols), jnp.float32),
             pltpu.VMEM((n_tok, cols), jnp.float32),
             pltpu.VMEM((n_tok, cols), jnp.float32),
         ],
-    )(normed, gathered, tokens, gathered, gathered, head.reshape(1, cols))
-    return seg_kv, scores[0]
+    )(normed, gathered, tokens, gathered, gathered, head.reshape(1, cols), queries, live_row)
 
 
 def local(
@@ -132,32 +153,25 @@
     kv_rows = kv_block.shape[0]
 
     normed = normalize_rows(verifier_rows, norm_gain)
-    seg_kv, partial_scores = project_all(
-        normed, draft_tokens, gathered, draft_head, kv_rows, d_rows, 4
-    )
-    seg_keys = seg_kv[:, :kv_cols]
-    seg_values = seg_kv[:, kv_cols:]
     lane_pick = (
         owner[:, None] == jnp.arange(pool_query.shape[0], dtype=jnp.int32)[None, :]
     ).astype(jnp.float32)
     queries = jnp.einsum("sc,chd->shd", lane_pick, pool_query, precision=lax.Precision.HIGHEST)
-    summary_key, summary_value = segment_pool(
-        seg_keys.reshape(seg_count, SEGL, KVH, HD),
-        seg_values.reshape(seg_count, SEGL, KVH, HD),
-        queries,
-        HD,
-    )
     width = KVH * HD
     live_row = jnp.zeros((1, width), jnp.float32).at[0, :seg_count].set(flags.astype(jnp.float32))
-    tail = jnp.concatenate(
-        [
-            partial_scores.reshape(-1, width),
-            summary_key.reshape(seg_count, width),
-            summary_value.reshape(seg_count, width),
-            live_row,
-        ],
-        axis=0,
-    )
+    tail = project_all(
+        normed,
+        draft_tokens,
+        gathered,
+        draft_head,
+        queries.reshape(seg_count, 1, width),
+        live_row,
+        kv_rows,
+        d_rows,
+        4,
+    )
+    score_rows = draft_tokens.shape[0] // width
+    summary_key = tail[score_rows : score_rows + seg_count].reshape(seg_count, KVH, HD)
     tail_all = jnp.stack(
         [tail]
         + [
@@ -165,7 +179,6 @@
             for k in range(1, n_seq)
         ]
     )
-    score_rows = partial_scores.shape[0] // width
     scores_all = tail_all[:, :score_rows].reshape(n_seq, -1)
     summary_all = tail_all[:, score_rows:]
     own = lax.axis_index("seq")

time: 146 us -> 146 us (level)
  other arithmetic: 13.2 us -> 15.7 us
    slice x2 -> x0, local copies, waits for them, and re-layouts: 2.05 us -> none  [the longest x1 1.28 us: local(): seg_values = seg_kv[:, kv_cols:]]
    all_gather x1, waiting for transfers between devices: 86.1 us -> 84.1 us  [local(): gathered = lax.all_gather(block, 'fsdp', axis=0, tiled=False)]
  transfers between devices with their start and end apart: 4 -> 4, of which waited for: 3 -> 3; matrix products, arithmetic and copies ran while one was open for 6% -> 8% of each run, Pallas kernels for 0% -> 0%
where the time goes in v9:
time: 146 us
  waiting for transfers between devices  88 us (60%)
  Pallas kernels  20.2 us (14%)
  other arithmetic  15.7 us (11%)
  between operations  14.1 us (10%)
  starting transfers between devices  4.44 us (3%)
  local copies, waits for them, and re-layouts  2.24 us (2%)
    all_gather x1, waiting for transfers between devices, local(): gathered = lax.all_gather(block, 'fsdp', axis=0, tiled=False)  84.1 us
    pallas_call x1, Pallas kernels, project_all(): pl.pallas_call(fused_kernel, grid=(steps,), in_specs=[pl.BlockSpec((n_nor...  20.2 us
    ppermute x3, starting transfers between devices, local(): lax.ppermute(tail, 'seq', [(i, (i + k) % n_seq) for i in range(n_seq)])  4.4 us
    ppermute x3, waiting for transfers between devices, local(): lax.ppermute(tail, 'seq', [(i, (i + k) % n_seq) for i in range(n_seq)])  3.86 us
    convert_element_type x1, other arithmetic, normalize_rows(): return (values * scale * norm_gain).astype(jnp.bfloat16)  3.16 us
    reduce_sum x1, other arithmetic, normalize_rows(): scale = lax.rsqrt(jnp.mean(values * values, axis=-1, keepdims=True) + eps)  3.1 us
  transfers between devices with their start and end apart: 4, of which 3 were waited for; matrix products, arithmetic and copies ran while one was open for 8% of the time, Pallas kernels for 0%

profile of v9, /device:TPU:0, one launch (start us, length us, event | category | flops | bytes accessed | tf_op | source)
XLA Modules:
  0.0 145.6 jit_solution(8987177281357040838)
XLA Ops:
  7.2 2.2 %pad_maximum_fusion = bf16[384,1024]{1,0:T(8,128)(2,1)} fusion(bf16[64,1024]{1,0:T(8,128)(2,1)} %param.15, bf16[64,1024]{1,0:T(8,128)(2,1)} %param.14, bf16[256,512]{1,0:T(8,128)(2,1)} %param.20, bf16[256,512]{1,0:T(8,128)(2,1)} %param.19), kind=kLoop, calls=%fused_computation.9 | loop fusion | flops 3145728 | bytes 1572864 | tf_op jit(solution)/shard_map/concatenate | solution.py:151
  9.4 0.9 fusion.10
  10.3 0.6 copy.24
  10.9 0.6 compare_reduce_fusion.1
  11.5 1.6 %fusion.18 = f32[1,8]{1,0:T(1,128)S(1)} fusion(pred[]{:T(512)} %compare_reduce_fusion.1, s32[8]{0:T(128)} %param.22), kind=kLoop, calls=%fused_computation.37 | loop fusion | flops 16 | bytes 65 | tf_op jit(solution)/shard_map/reshape.39
  13.2 0.6 scatter.4.live_ref
  13.7 0.7 broadcast_compare_fusion
  14.4 3.1 %fusion.1 = f32[256]{0:T(256)S(1)} fusion(bf16[256,8192]{1,0:T(8,128)(2,1)} %param.17), kind=kLoop, calls=%fused_computation.3 | loop fusion | flops 6291200 | bytes 4195328 | tf_op jit(solution)/shard_map/reduce_sum | solution.py:20
  17.5 3.2 %fusion.3.x_ref = bf16[256,8192]{1,0:T(8,128)(2,1)} fusion(bf16[256,8192]{1,0:T(8,128)(2,1)S(1)} %copy-done.1, f32[8192]{0:T(1024)S(1)} %copy-done.2, f32[256]{0:T(256)S(1)} %add_rsqrt_fusion), kind=kLoop, calls=%fused_computation.5 | loop fusion | flops 8388608 | bytes 8422400 | tf_op jit(solution)/shard_map/convert_element_type | solution.py:21
  20.7 84.1 %all-gather.3.cloned.1.call-done = bf16[12288,1024]{1,0:T(8,128)(2,1)} async-done(((bf16[384,1024]{1,0:T(8,128)(2,1)}), bf16[12288,1024]{1,0:T(8,128)(2,1)}) %all-gather.3.cloned.1.call-update) | async-done | bytes 25165840 | tf_op jit(solution)/shard_map/all_gather | solution.py:152
  104.8 20.2 %shard_map.122 = f32[19,512]{1,0:T(8,128)} custom-call(bf16[256,8192]{1,0:T(8,128)(2,1)} %fusion.3.x_ref, bf16[32,384,1024]{2,1,0:T(8,128)(2,1)} %bitcast.27, bf16[1024,2048]{1,0:T(8,128)(2,1)} %tok_ref.1, bf16[32,384,1024]{2,1,0:T(8,128)(2,1)} %bitcast.28, bf16[32,384,1024]{2,1,0:T(8,128)(2,1)} %bitcast.29, f32[1,1024]{1,0:T(1,128)} %bitcast.46, ...), custom_call_target="tpu_custom_call" | custom-call | tf_op jit(solution)/shard_map/pallas_call | solution.py:107
  125.1 2.7 %collective-permute-start.2 = (f32[19,512]{1,0:T(8,128)}, f32[19,512]{1,0:T(8,128)S(1)}, u32[]{:S(2)}, u32[]{:S(2)}) collective-permute-start(f32[19,512]{1,0:T(8,128)} %shard_map.122), channel_id=1, source_target_pairs={{0,3},{1,0},{2,1},{3,2},{4,7},{5,4},{6,5},{7,6},{8,11},{9,8},{10,9... | collective-permute-start | bytes 116744 | tf_op jit(solution)/shard_map/ppermute | solution.py:178
  127.7 0.8 collective-permute-start.1
  128.6 0.9 collective-permute-start
  129.5 0.8 slice_bitcast_fusion
  130.3 3.3 %collective-permute-done.1 = f32[19,512]{1,0:T(8,128)S(1)} collective-permute-done((f32[19,512]{1,0:T(8,128)}, f32[19,512]{1,0:T(8,128)S(1)}, u32[]{:S(2)}, u32[]{:S(2)}) %collective-permute-start.1) | collective-permute-done | bytes 38944 | tf_op jit(solution)/shard_map/ppermute | solution.py:178
  133.6 0.5 collective-permute-done
  134.1 0.7 compare_reduce_fusion
  134.8 0.7 maximum_bitcast_fusion
  135.6 0.9 pad_maximum_fusion.4
  136.8 0.5 add_divide_fusion
  137.3 0.2 multiply_reduce_fusion.1
  137.7 0.2 multiply_reduce_fusion
  138.1 0.7 fusion.8
  (22 shorter events, 0.7 us)
Async XLA Ops:
  7.2 2.3 %copy-start = (f32[4,4,128]{2,1,0:T(4,128)S(1)}, f32[4,4,128]{2,1,0:T(4,128)}, u32[]{:S(2)}) copy-start(f32[4,4,128]{2,1,0:T(4,128)} %param.21) | copy-start | bytes 24580
  7.2 10.3 %copy-start.2 = (f32[8192]{0:T(1024)S(1)}, f32[8192]{0:T(1024)}, u32[]{:S(2)}) copy-start(f32[8192]{0:T(1024)} %param.18) | copy-start | bytes 98308
  7.2 97.6 %all-gather.3.cloned.1.call-start = ((), (), s32[]{:S(2)}) async-start(), calls=%async_computation | async-start | bytes 25952256 | tf_op jit(solution)/shard_map/all_gather | solution.py:152
  10.9 6.6 %copy-start.1 = (bf16[256,8192]{1,0:T(8,128)(2,1)S(1)}, bf16[256,8192]{1,0:T(8,128)(2,1)}, u32[]{:S(2)}) copy-start(bf16[256,8192]{1,0:T(8,128)(2,1)} %param.17) | copy-start | bytes 12582916
  125.1 5.2 %collective-permute-start.2 = (f32[19,512]{1,0:T(8,128)}, f32[19,512]{1,0:T(8,128)S(1)}, u32[]{:S(2)}, u32[]{:S(2)}) collective-permute-start(f32[19,512]{1,0:T(8,128)} %shard_map.122), channel_id=1, source_target_pairs={{0,3},{1,0},{2,1},{3,2},{4,7},{5,4},{6,5},{7,6},{8,11},{9,8},{10,9... | collective-permute-start | bytes 116744 | tf_op jit(solution)/shard_map/ppermute | solution.py:178
  127.7 5.9 %collective-permute-start.1 = (f32[19,512]{1,0:T(8,128)}, f32[19,512]{1,0:T(8,128)S(1)}, u32[]{:S(2)}, u32[]{:S(2)}) collective-permute-start(f32[19,512]{1,0:T(8,128)} %shard_map.122), channel_id=1, source_target_pairs={{0,2},{1,3},{2,0},{3,1},{4,6},{5,7},{6,4},{7,5},{8,10},{9,11},{10,... | collective-permute-start | bytes 116744 | tf_op jit(solution)/shard_map/ppermute | solution.py:178
  128.6 5.5 %collective-permute-start = (f32[19,512]{1,0:T(8,128)}, f32[19,512]{1,0:T(8,128)S(1)}, u32[]{:S(2)}, u32[]{:S(2)}) collective-permute-start(f32[19,512]{1,0:T(8,128)} %shard_map.122), channel_id=1, source_target_pairs={{0,1},{1,2},{2,3},{3,0},{4,5},{5,6},{6,7},{7,4},{8,9},{9,10},{10,1... | collective-permute-start | bytes 116744 | tf_op jit(solution)/shard_map/ppermute | solution.py:178
Sparse Core Ops, SparseCore 0:
  10.3 94.5 all-gather.2

commit v10 on v9

--- a/solution.py
+++ b/solution.py
@@ -172,31 +172,36 @@
     )
     score_rows = draft_tokens.shape[0] // width
     summary_key = tail[score_rows : score_rows + seg_count].reshape(seg_count, KVH, HD)
-    tail_all = jnp.stack(
-        [tail]
-        + [
-            lax.ppermute(tail, "seq", [(i, (i + k) % n_seq) for i in range(n_seq)])
-            for k in range(1, n_seq)
-        ]
-    )
-    scores_all = tail_all[:, :score_rows].reshape(n_seq, -1)
-    summary_all = tail_all[:, score_rows:]
+    tails = [tail] + [
+        lax.ppermute(tail, "seq", [(i, (i + k) % n_seq) for i in range(n_seq)])
+        for k in range(1, n_seq)
+    ]
     own = lax.axis_index("seq")
     own_tokens = seg_count * SEGL
-    token_scores = jnp.sum(
-        lax.dynamic_slice_in_dim(scores_all, own * own_tokens, own_tokens, axis=1), axis=0
+    token_scores = sum(
+        lax.dynamic_slice_in_dim(t[:score_rows].reshape(-1), own * own_tokens, own_tokens)
+        for t in tails
     )
     draft_score = jnp.mean(token_scores.reshape(seg_count, SEGL), axis=1)
-    key_all = summary_all[:, :seg_count].reshape(-1, KVH, HD)
-    value_all = summary_all[:, seg_count : 2 * seg_count].reshape(-1, KVH, HD)
-    live_all = summary_all[:, 2 * seg_count, :seg_count].reshape(-1)
-    pooled = cross_pool(
-        summary_key,
-        key_all,
-        value_all,
-        live_all > 0.5,
-        HD,
-    )
+    query_keys = summary_key[:, :, None, :]
+    scores, lives = [], []
+    for t in tails:
+        keys = t[score_rows : score_rows + seg_count].reshape(seg_count, KVH, HD)
+        live = t[score_rows + 2 * seg_count, :seg_count] > 0.5
+        sc = jnp.sum(query_keys * jnp.swapaxes(keys, 0, 1)[None], axis=-1) / math.sqrt(HD)
+        scores.append(jnp.where(live[None, None, :], sc, -1e30))
+        lives.append(live)
+    highest = scores[0].max(axis=2, keepdims=True)
+    for sc in scores[1:]:
+        highest = jnp.maximum(highest, sc.max(axis=2, keepdims=True))
+    total = 0.0
+    pooled = 0.0
+    for t, sc, live in zip(tails, scores, lives):
+        values = t[score_rows + seg_count : score_rows + 2 * seg_count].reshape(seg_count, KVH, HD)
+        wt = jnp.where(live[None, None, :], jnp.exp(sc - highest), 0.0)
+        total = total + jnp.sum(wt, axis=2, keepdims=True)
+        pooled = pooled + jnp.sum(wt[..., None] * jnp.swapaxes(values, 0, 1)[None], axis=2)
+    pooled = pooled / total
     own_pooled = pooled.reshape(seg_count, KVH * HD)
     verdict = jnp.where(
         flags[:, None] == 1, jax.nn.sigmoid(draft_score)[:, None] * own_pooled, 0.0

time: 146 us -> 147 us (level)
  no operation moved by 1% of the time
where the time goes in v10:
time: 147 us
  waiting for transfers between devices  88.8 us (60%)
  Pallas kernels  20.2 us (14%)
  other arithmetic  14.7 us (10%)
  between operations  14.2 us (10%)
  starting transfers between devices  4.44 us (3%)
  local copies, waits for them, and re-layouts  3.71 us (3%)
    all_gather x1, waiting for transfers between devices, local(): gathered = lax.all_gather(block, 'fsdp', axis=0, tiled=False)  84.1 us
    pallas_call x1, Pallas kernels, project_all(): pl.pallas_call(fused_kernel, grid=(steps,), in_specs=[pl.BlockSpec((n_nor...  20.2 us
    ppermute x3, waiting for transfers between devices, local(): lax.ppermute(tail, 'seq', [(i, (i + k) % n_seq) for i in range(n_seq)])  4.65 us
    ppermute x3, starting transfers between devices, local(): lax.ppermute(tail, 'seq', [(i, (i + k) % n_seq) for i in range(n_seq)])  4.4 us
    convert_element_type x1, other arithmetic, normalize_rows(): return (values * scale * norm_gain).astype(jnp.bfloat16)  3.16 us
    reduce_sum x1, other arithmetic, normalize_rows(): scale = lax.rsqrt(jnp.mean(values * values, axis=-1, keepdims=True) + eps)  3.1 us
  transfers between devices with their start and end apart: 4, of which 3 were waited for; matrix products, arithmetic and copies ran while one was open for 8% of the time, Pallas kernels for 0%

profile of v10, /device:TPU:0, one launch (start us, length us, event | category | flops | bytes accessed | tf_op | source)
XLA Modules:
  0.0 146.9 jit_solution(10477931536124839577)
XLA Ops:
  7.2 2.2 %pad_maximum_fusion = bf16[384,1024]{1,0:T(8,128)(2,1)} fusion(bf16[64,1024]{1,0:T(8,128)(2,1)} %param.15, bf16[64,1024]{1,0:T(8,128)(2,1)} %param.14, bf16[256,512]{1,0:T(8,128)(2,1)} %param.20, bf16[256,512]{1,0:T(8,128)(2,1)} %param.19), kind=kLoop, calls=%fused_computation.5 | loop fusion | flops 3145728 | bytes 1572864 | tf_op jit(solution)/shard_map/concatenate | solution.py:151
  9.4 0.9 fusion.9
  10.3 0.6 copy.17
  10.9 0.6 compare_reduce_fusion
  11.5 1.6 %fusion.14 = f32[1,8]{1,0:T(1,128)S(1)} fusion(pred[]{:T(512)} %compare_reduce_fusion, s32[8]{0:T(128)} %param.22), kind=kLoop, calls=%fused_computation.58 | loop fusion | flops 16 | bytes 65 | tf_op jit(solution)/shard_map/reshape.48
  13.2 0.6 scatter.4.live_ref
  13.7 0.7 broadcast_compare_fusion
  14.4 3.1 %fusion = f32[256]{0:T(256)S(1)} fusion(bf16[256,8192]{1,0:T(8,128)(2,1)} %param.17), kind=kLoop, calls=%fused_computation.2 | loop fusion | flops 6291200 | bytes 4195328 | tf_op jit(solution)/shard_map/reduce_sum | solution.py:20
  17.5 3.2 %fusion.2.x_ref = bf16[256,8192]{1,0:T(8,128)(2,1)} fusion(bf16[256,8192]{1,0:T(8,128)(2,1)S(1)} %copy-done.1, f32[8192]{0:T(1024)S(1)} %copy-done.2, f32[256]{0:T(256)S(1)} %add_rsqrt_fusion), kind=kLoop, calls=%fused_computation.4 | loop fusion | flops 8388608 | bytes 8422400 | tf_op jit(solution)/shard_map/convert_element_type | solution.py:21
  20.7 84.1 %all-gather.3.cloned.1.call-done = bf16[12288,1024]{1,0:T(8,128)(2,1)} async-done(((bf16[384,1024]{1,0:T(8,128)(2,1)}), bf16[12288,1024]{1,0:T(8,128)(2,1)}) %all-gather.3.cloned.1.call-update) | async-done | bytes 25165840 | tf_op jit(solution)/shard_map/all_gather | solution.py:152
  104.8 20.2 %shard_map.122 = f32[19,512]{1,0:T(8,128)} custom-call(bf16[256,8192]{1,0:T(8,128)(2,1)} %fusion.2.x_ref, bf16[32,384,1024]{2,1,0:T(8,128)(2,1)} %bitcast.69, bf16[1024,2048]{1,0:T(8,128)(2,1)} %tok_ref.1, bf16[32,384,1024]{2,1,0:T(8,128)(2,1)} %bitcast.70, bf16[32,384,1024]{2,1,0:T(8,128)(2,1)} %bitcast.71, f32[1,1024]{1,0:T(1,128)} %bitcast.77, ...), custom_call_target="tpu_custom_call" | custom-call | tf_op jit(solution)/shard_map/pallas_call | solution.py:107
  125.1 0.7 slice_bitcast_fusion.12
  125.8 0.8 slice_bitcast_fusion.3
  126.6 2.7 %collective-permute-start.2 = (f32[19,512]{1,0:T(8,128)}, f32[19,512]{1,0:T(8,128)S(1)}, u32[]{:S(2)}, u32[]{:S(2)}) collective-permute-start(f32[19,512]{1,0:T(8,128)} %shard_map.122), channel_id=1, source_target_pairs={{0,3},{1,0},{2,1},{3,2},{4,7},{5,4},{6,5},{7,6},{8,11},{9,8},{10,9... | collective-permute-start | bytes 116744 | tf_op jit(solution)/shard_map/ppermute | solution.py:176
  129.3 0.7 compare_bitcast_fusion.3
  130.0 0.8 collective-permute-start.1
  130.9 0.9 collective-permute-start
  131.7 4.1 %collective-permute-done.1 = f32[19,512]{1,0:T(8,128)S(1)} collective-permute-done((f32[19,512]{1,0:T(8,128)}, f32[19,512]{1,0:T(8,128)S(1)}, u32[]{:S(2)}, u32[]{:S(2)}) %collective-permute-start.1) | collective-permute-done | bytes 38944 | tf_op jit(solution)/shard_map/ppermute | solution.py:176
  135.9 0.5 collective-permute-done
  136.6 0.1 reduce_sum.127
  136.7 0.5 add_divide_fusion
  137.2 0.3 multiply_reduce_fusion.6
  138.2 0.2 fusion.15
  139.3 0.7 fusion.4
  (45 shorter events, 1.9 us)
Async XLA Ops:
  7.2 2.3 %copy-start = (f32[4,4,128]{2,1,0:T(4,128)S(1)}, f32[4,4,128]{2,1,0:T(4,128)}, u32[]{:S(2)}) copy-start(f32[4,4,128]{2,1,0:T(4,128)} %param.21) | copy-start | bytes 24580
  7.2 10.3 %copy-start.2 = (f32[8192]{0:T(1024)S(1)}, f32[8192]{0:T(1024)}, u32[]{:S(2)}) copy-start(f32[8192]{0:T(1024)} %param.18) | copy-start | bytes 98308
  7.2 97.6 %all-gather.3.cloned.1.call-start = ((), (), s32[]{:S(2)}) async-start(), calls=%async_computation | async-start | bytes 25952256 | tf_op jit(solution)/shard_map/all_gather | solution.py:152
  10.9 6.6 %copy-start.1 = (bf16[256,8192]{1,0:T(8,128)(2,1)S(1)}, bf16[256,8192]{1,0:T(8,128)(2,1)}, u32[]{:S(2)}) copy-start(bf16[256,8192]{1,0:T(8,128)(2,1)} %param.17) | copy-start | bytes 12582916
  126.6 5.1 %collective-permute-start.2 = (f32[19,512]{1,0:T(8,128)}, f32[19,512]{1,0:T(8,128)S(1)}, u32[]{:S(2)}, u32[]{:S(2)}) collective-permute-start(f32[19,512]{1,0:T(8,128)} %shard_map.122), channel_id=1, source_target_pairs={{0,3},{1,0},{2,1},{3,2},{4,7},{5,4},{6,5},{7,6},{8,11},{9,8},{10,9... | collective-permute-start | bytes 116744 | tf_op jit(solution)/shard_map/ppermute | solution.py:176
  130.0 5.9 %collective-permute-start.1 = (f32[19,512]{1,0:T(8,128)}, f32[19,512]{1,0:T(8,128)S(1)}, u32[]{:S(2)}, u32[]{:S(2)}) collective-permute-start(f32[19,512]{1,0:T(8,128)} %shard_map.122), channel_id=1, source_target_pairs={{0,2},{1,3},{2,0},{3,1},{4,6},{5,7},{6,4},{7,5},{8,10},{9,11},{10,... | collective-permute-start | bytes 116744 | tf_op jit(solution)/shard_map/ppermute | solution.py:176
  130.9 5.5 %collective-permute-start = (f32[19,512]{1,0:T(8,128)}, f32[19,512]{1,0:T(8,128)S(1)}, u32[]{:S(2)}, u32[]{:S(2)}) collective-permute-start(f32[19,512]{1,0:T(8,128)} %shard_map.122), channel_id=1, source_target_pairs={{0,1},{1,2},{2,3},{3,0},{4,5},{5,6},{6,7},{7,4},{8,9},{9,10},{10,1... | collective-permute-start | bytes 116744 | tf_op jit(solution)/shard_map/ppermute | solution.py:176
Sparse Core Ops, SparseCore 0:
  10.3 94.5 all-gather.2

commit v11 on v9

--- a/solution.py
+++ b/solution.py
@@ -127,6 +127,24 @@
     )(normed, gathered, tokens, gathered, gathered, head.reshape(1, cols), queries, live_row)
 
 
+def pack_kernel(k_ref, v_ref, g_ref, u_ref, out_ref):
+    rows, half = k_ref.shape
+    d_rows = g_ref.shape[0]
+    out_ref[0:rows, 0:half] = k_ref[...]
+    out_ref[0:rows, half:] = v_ref[...]
+    out_ref[rows : rows + d_rows, :] = g_ref[...]
+    out_ref[rows + d_rows :, :] = u_ref[...]
+
+
+def pack_block(key_weight, value_weight, draft_gate, draft_up):
+    rows = key_weight.shape[0]
+    d_rows, cols = draft_gate.shape
+    return pl.pallas_call(
+        pack_kernel,
+        out_shape=jax.ShapeDtypeStruct((rows + 2 * d_rows, cols), key_weight.dtype),
+    )(key_weight, value_weight, draft_gate, draft_up)
+
+
 def local(
     draft_tokens,
     draft_gate,
@@ -146,11 +164,9 @@
     d_rows, d_cols = draft_gate.shape
     v_rows = key_weight.shape[0]
     kv_cols = key_weight.shape[1]
-    kv_block = jnp.concatenate([key_weight, value_weight], axis=1)
-    kv_block = kv_block.reshape(-1, d_cols)
-    block = jnp.concatenate([kv_block, draft_gate, draft_up], axis=0)
+    block = pack_block(key_weight, value_weight, draft_gate, draft_up)
     gathered = lax.all_gather(block, "fsdp", axis=0, tiled=False)
-    kv_rows = kv_block.shape[0]
+    kv_rows = key_weight.shape[0]
 
     normed = normalize_rows(verifier_rows, norm_gain)
     lane_pick = (

time: 146 us -> 146 us (level)
  Pallas kernels: 20.2 us -> 22.3 us
  waiting for transfers between devices: 88 us -> 86.2 us
    convert_element_type x1, other arithmetic: 3.16 us -> 5.34 us  [normalize_rows(): return (values * scale * norm_gain).astype(jnp.bfloat16)]
    concatenate x1 -> x0, other arithmetic: 2.16 us -> none  [local(): block = jnp.concatenate([kv_block, draft_gate, draft_up], axis=0)]
    pallas_call x0 -> x1, Pallas kernels: none -> 2.08 us  [pack_block(): pl.pallas_call(pack_kernel, out_shape=jax.ShapeDtypeStruct((rows + 2 * d_...]
    all_gather x1, waiting for transfers between devices: 84.1 us -> 82.4 us  [local(): gathered = lax.all_gather(block, 'fsdp', axis=0, tiled=False)]
  transfers between devices with their start and end apart: 4 -> 4, of which waited for: 3 -> 3; matrix products, arithmetic and copies ran while one was open for 8% -> 10% of each run, Pallas kernels for 0% -> 0%
where the time goes in v11:
time: 146 us
  waiting for transfers between devices  86.2 us (59%)
  Pallas kernels  22.3 us (15%)
  other arithmetic  15.4 us (11%)
  between operations  14.1 us (10%)
  starting transfers between devices  4.44 us (3%)
  local copies, waits for them, and re-layouts  2.24 us (2%)
    all_gather x1, waiting for transfers between devices, local(): gathered = lax.all_gather(block, 'fsdp', axis=0, tiled=False)  82.4 us
    pallas_call x1, Pallas kernels, project_all(): pl.pallas_call(fused_kernel, grid=(steps,), in_specs=[pl.BlockSpec((n_nor...  20.2 us
    convert_element_type x1, other arithmetic, normalize_rows(): return (values * scale * norm_gain).astype(jnp.bfloat16)  5.34 us
    ppermute x3, starting transfers between devices, local(): lax.ppermute(tail, 'seq', [(i, (i + k) % n_seq) for i in range(n_seq)])  4.4 us
    ppermute x3, waiting for transfers between devices, local(): lax.ppermute(tail, 'seq', [(i, (i + k) % n_seq) for i in range(n_seq)])  3.86 us
    reduce_sum x1, other arithmetic, normalize_rows(): scale = lax.rsqrt(jnp.mean(values * values, axis=-1, keepdims=True) + eps)  3.1 us
  transfers between devices with their start and end apart: 4, of which 3 were waited for; matrix products, arithmetic and copies ran while one was open for 10% of the time, Pallas kernels for 0%

profile of v11, /device:TPU:0, one launch (start us, length us, event | category | flops | bytes accessed | tf_op | source)
XLA Modules:
  0.0 145.6 jit_solution(6280950292653235470)
XLA Ops:
  7.2 2.1 %shard_map.122 = bf16[384,1024]{1,0:T(8,128)(2,1)} custom-call(bf16[256,512]{1,0:T(8,128)(2,1)} %k_ref.1, bf16[256,512]{1,0:T(8,128)(2,1)} %v_ref.1, bf16[64,1024]{1,0:T(8,128)(2,1)} %g_ref.1, bf16[64,1024]{1,0:T(8,128)(2,1)} %u_ref.1), custom_call_target="tpu_custom_call" | custom-call | tf_op jit(solution)/shard_map/pallas_call | solution.py:142
  9.3 0.9 fusion.10
  10.2 0.6 copy.24
  10.8 0.6 compare_reduce_fusion.1
  11.4 1.3 fusion.18
  12.7 0.6 scatter.4.live_ref
  13.3 0.7 broadcast_compare_fusion
  14.0 3.1 %fusion.1 = f32[256]{0:T(256)S(1)} fusion(bf16[256,8192]{1,0:T(8,128)(2,1)} %param.17), kind=kLoop, calls=%fused_computation.3 | loop fusion | flops 6291200 | bytes 4195328 | tf_op jit(solution)/shard_map/reduce_sum | solution.py:20
  17.1 5.3 %fusion.3.x_ref = bf16[256,8192]{1,0:T(8,128)(2,1)} fusion(bf16[256,8192]{1,0:T(8,128)(2,1)} %param.17, f32[8192]{0:T(1024)} %param.18, f32[256]{0:T(256)S(1)} %add_rsqrt_fusion), kind=kLoop, calls=%fused_computation.5 | loop fusion | flops 8388608 | bytes 8422400 | tf_op jit(solution)/shard_map/convert_element_type | solution.py:21
  22.4 82.4 %all-gather.3.cloned.1.call-done = bf16[12288,1024]{1,0:T(8,128)(2,1)} async-done(((bf16[384,1024]{1,0:T(8,128)(2,1)}), bf16[12288,1024]{1,0:T(8,128)(2,1)}) %all-gather.3.cloned.1.call-update) | async-done | bytes 25165840 | tf_op jit(solution)/shard_map/all_gather | solution.py:168
  104.8 20.2 %shard_map.123 = f32[19,512]{1,0:T(8,128)} custom-call(bf16[256,8192]{1,0:T(8,128)(2,1)} %fusion.3.x_ref, bf16[32,384,1024]{2,1,0:T(8,128)(2,1)} %bitcast.27, bf16[1024,2048]{1,0:T(8,128)(2,1)} %tok_ref.1, bf16[32,384,1024]{2,1,0:T(8,128)(2,1)} %bitcast.28, bf16[32,384,1024]{2,1,0:T(8,128)(2,1)} %bitcast.29, f32[1,1024]{1,0:T(1,128)} %bitcast.46, ...), custom_call_target="tpu_custom_call" | custom-call | tf_op jit(solution)/shard_map/pallas_call | solution.py:107
  125.0 2.7 %collective-permute-start.2 = (f32[19,512]{1,0:T(8,128)}, f32[19,512]{1,0:T(8,128)S(1)}, u32[]{:S(2)}, u32[]{:S(2)}) collective-permute-start(f32[19,512]{1,0:T(8,128)} %shard_map.123), channel_id=1, source_target_pairs={{0,3},{1,0},{2,1},{3,2},{4,7},{5,4},{6,5},{7,6},{8,11},{9,8},{10,9... | collective-permute-start | bytes 116744 | tf_op jit(solution)/shard_map/ppermute | solution.py:194
  127.7 0.8 collective-permute-start.1
  128.6 0.9 collective-permute-start
  129.4 0.8 slice_bitcast_fusion
  130.3 3.3 %collective-permute-done.1 = f32[19,512]{1,0:T(8,128)S(1)} collective-permute-done((f32[19,512]{1,0:T(8,128)}, f32[19,512]{1,0:T(8,128)S(1)}, u32[]{:S(2)}, u32[]{:S(2)}) %collective-permute-start.1) | collective-permute-done | bytes 38944 | tf_op jit(solution)/shard_map/ppermute | solution.py:194
  133.6 0.5 collective-permute-done
  134.1 0.7 compare_reduce_fusion
  134.8 0.7 maximum_bitcast_fusion
  135.5 0.9 pad_maximum_fusion.3
  136.8 0.5 add_divide_fusion
  137.3 0.2 multiply_reduce_fusion.1
  137.7 0.2 multiply_reduce_fusion
  138.0 0.7 fusion.8
  (18 shorter events, 0.7 us)
Async XLA Ops:
  7.2 2.2 %copy-start = (f32[4,4,128]{2,1,0:T(4,128)S(1)}, f32[4,4,128]{2,1,0:T(4,128)}, u32[]{:S(2)}) copy-start(f32[4,4,128]{2,1,0:T(4,128)} %param.21) | copy-start | bytes 24580
  7.2 97.6 %all-gather.3.cloned.1.call-start = ((), (), s32[]{:S(2)}) async-start(), calls=%async_computation | async-start | bytes 25952256 | tf_op jit(solution)/shard_map/all_gather | solution.py:168
  125.0 5.2 %collective-permute-start.2 = (f32[19,512]{1,0:T(8,128)}, f32[19,512]{1,0:T(8,128)S(1)}, u32[]{:S(2)}, u32[]{:S(2)}) collective-permute-start(f32[19,512]{1,0:T(8,128)} %shard_map.123), channel_id=1, source_target_pairs={{0,3},{1,0},{2,1},{3,2},{4,7},{5,4},{6,5},{7,6},{8,11},{9,8},{10,9... | collective-permute-start | bytes 116744 | tf_op jit(solution)/shard_map/ppermute | solution.py:194
  127.7 5.9 %collective-permute-start.1 = (f32[19,512]{1,0:T(8,128)}, f32[19,512]{1,0:T(8,128)S(1)}, u32[]{:S(2)}, u32[]{:S(2)}) collective-permute-start(f32[19,512]{1,0:T(8,128)} %shard_map.123), channel_id=1, source_target_pairs={{0,2},{1,3},{2,0},{3,1},{4,6},{5,7},{6,4},{7,5},{8,10},{9,11},{10,... | collective-permute-start | bytes 116744 | tf_op jit(solution)/shard_map/ppermute | solution.py:194
  128.6 5.5 %collective-permute-start = (f32[19,512]{1,0:T(8,128)}, f32[19,512]{1,0:T(8,128)S(1)}, u32[]{:S(2)}, u32[]{:S(2)}) collective-permute-start(f32[19,512]{1,0:T(8,128)} %shard_map.123), channel_id=1, source_target_pairs={{0,1},{1,2},{2,3},{3,0},{4,5},{5,6},{6,7},{7,4},{8,9},{9,10},{10,1... | collective-permute-start | bytes 116744 | tf_op jit(solution)/shard_map/ppermute | solution.py:194
Sparse Core Ops, SparseCore 0:
  10.2 94.5 all-gather.2

commit v12 on v6

--- a/solution.py
+++ b/solution.py
@@ -67,7 +67,7 @@
     @pl.when(j == pl.num_programs(0) - 1)
     def _():
         g = gacc[...]
-        act = g / (1.0 + jnp.exp(-g))
+        act = g * (0.5 + 0.5 * jnp.tanh(0.5 * g))
         col = jnp.sum(act * uacc[...] * head_ref[...], axis=1, keepdims=True)
         wide = jnp.broadcast_to(col, (col.shape[0], 128))
         score_ref[...] = jnp.transpose(wide)[0 : score_ref.shape[0], :]

time: 146 us -> 146 us (level)
  no operation moved by 1% of the time
where the time goes in v12:
time: 146 us
  waiting for transfers between devices  88.8 us (61%)
  Pallas kernels  20.2 us (14%)
  between operations  14.2 us (10%)
  other arithmetic  13.2 us (9%)
  starting transfers between devices  5.72 us (4%)
  local copies, waits for them, and re-layouts  2.69 us (2%)
    all_gather x1, waiting for transfers between devices, local(): gathered = lax.all_gather(block, 'fsdp', axis=0, tiled=False)  86.1 us
    pallas_call x1, Pallas kernels, project_all(): pl.pallas_call(fused_kernel, grid=(steps,), in_specs=[pl.BlockSpec((n_nor...  20.2 us
    ppermute x3, starting transfers between devices, local(): lax.ppermute(tail, 'seq', [(i, (i + k) % n_seq) for i in range(n_seq)])  5.68 us
    convert_element_type x1, other arithmetic, normalize_rows(): return (values * scale * norm_gain).astype(jnp.bfloat16)  3.16 us
    reduce_sum x1, other arithmetic, normalize_rows(): scale = lax.rsqrt(jnp.mean(values * values, axis=-1, keepdims=True) + eps)  3.1 us
  transfers between devices with their start and end apart: 4, of which 3 were waited for; matrix products, arithmetic and copies ran while one was open for 6% of the time, Pallas kernels for 0%

profile of v12, /device:TPU:0, one launch (start us, length us, event | category | flops | bytes accessed | tf_op | source)
XLA Modules:
  0.0 145.8 jit_solution(1994978771334659101)
XLA Ops:
  7.2 2.2 %pad_maximum_fusion = bf16[384,1024]{1,0:T(8,128)(2,1)} fusion(bf16[64,1024]{1,0:T(8,128)(2,1)} %param.15, bf16[64,1024]{1,0:T(8,128)(2,1)} %param.14, bf16[256,512]{1,0:T(8,128)(2,1)} %param.20, bf16[256,512]{1,0:T(8,128)(2,1)} %param.19), kind=kLoop, calls=%fused_computation.12 | loop fusion | flops 3145728 | bytes 1572864 | tf_op jit(solution)/shard_map/concatenate | solution.py:130
  9.4 1.0 fusion.19
  10.5 0.6 compare_reduce_fusion.1
  11.1 1.3 fusion.27
  12.4 3.1 %fusion.2 = f32[256]{0:T(256)S(1)} fusion(bf16[256,8192]{1,0:T(8,128)(2,1)} %param.17), kind=kLoop, calls=%fused_computation.4 | loop fusion | flops 6291200 | bytes 4195328 | tf_op jit(solution)/shard_map/reduce_sum | solution.py:20
  15.5 3.2 %fusion.4.x_ref = bf16[256,8192]{1,0:T(8,128)(2,1)} fusion(bf16[256,8192]{1,0:T(8,128)(2,1)S(1)} %copy-done.1, f32[8192]{0:T(1024)S(1)} %copy-done.2, f32[256]{0:T(256)S(1)} %add_rsqrt_fusion), kind=kLoop, calls=%fused_computation.6 | loop fusion | flops 8388608 | bytes 8422400 | tf_op jit(solution)/shard_map/convert_element_type | solution.py:21
  18.7 86.1 %all-gather.3.cloned.1.call-done = bf16[12288,1024]{1,0:T(8,128)(2,1)} async-done(((bf16[384,1024]{1,0:T(8,128)(2,1)}), bf16[12288,1024]{1,0:T(8,128)(2,1)}) %all-gather.3.cloned.1.call-update) | async-done | bytes 25165840 | tf_op jit(solution)/shard_map/all_gather | solution.py:131
  104.8 20.2 %shard_map.122 = (f32[256,1024]{1,0:T(8,128)}, f32[8,1024]{1,0:T(8,128)}) custom-call(bf16[256,8192]{1,0:T(8,128)(2,1)} %fusion.4.x_ref, bf16[32,384,1024]{2,1,0:T(8,128)(2,1)} %bitcast.31, bf16[1024,2048]{1,0:T(8,128)(2,1)} %tok_ref.1, bf16[32,384,1024]{2,1,0:T(8,128)(2,1)} %bitcast.32, bf16[32,384,1024]{2,1,0:T(8,128)(2,1)} %bitcast.33, f32[1,1024]{1,0:T(1,128)} %bitcast.48), custom_call_target="tpu_custom_call" | custom-call | tf_op jit(solution)/shard_map/pallas_call | solution.py:82
  125.0 1.3 fusion.35
  126.2 0.2 reshape.113
  126.4 0.4 multiply_reduce_fusion.4
  126.9 0.2 reshape.115
  127.0 0.8 slice_reduce_fusion
  127.8 0.3 multiply_reduce_fusion.3
  128.2 1.5 %collective-permute-start = (f32[19,512]{1,0:T(8,128)S(1)}, f32[19,512]{1,0:T(8,128)S(1)}, u32[]{:S(2)}, u32[]{:S(2)}) collective-permute-start(f32[19,512]{1,0:T(8,128)S(1)} %get-tuple-element.27), channel_id=1, source_target_pairs={{0,1},{1,2},{2,3},{3,0},{4,5},{5,6},{6,7},{7,4},{8,9},{9,10},{10,1... | collective-permute-start | bytes 116744 | tf_op jit(solution)/shard_map/ppermute | solution.py:164
  129.8 2.7 %collective-permute-start.1 = (f32[19,512]{1,0:T(8,128)S(1)}, f32[19,512]{1,0:T(8,128)S(1)}, u32[]{:S(2)}, u32[]{:S(2)}) collective-permute-start(f32[19,512]{1,0:T(8,128)S(1)} %get-tuple-element.27), channel_id=1, source_target_pairs={{0,2},{1,3},{2,0},{3,1},{4,6},{5,7},{6,4},{7,5},{8,10},{9,11},{10,... | collective-permute-start | bytes 116744 | tf_op jit(solution)/shard_map/ppermute | solution.py:164
  132.4 1.5 collective-permute-start.2
  133.9 1.5 %collective-permute-done.1 = f32[19,512]{1,0:T(8,128)S(1)} collective-permute-done((f32[19,512]{1,0:T(8,128)S(1)}, f32[19,512]{1,0:T(8,128)S(1)}, u32[]{:S(2)}, u32[]{:S(2)}) %collective-permute-start.1) | collective-permute-done | bytes 38944 | tf_op jit(solution)/shard_map/ppermute | solution.py:164
  135.4 1.1 collective-permute-done.2
  136.7 0.2 multiply_reduce_fusion.1
  137.2 0.5 add_divide_fusion
  137.8 0.2 fusion.36
  137.9 0.2 multiply_reduce_fusion
  138.2 0.7 fusion.15
  (31 shorter events, 0.7 us)
Async XLA Ops:
  7.2 2.3 %copy-start = (f32[4,4,128]{2,1,0:T(4,128)S(1)}, f32[4,4,128]{2,1,0:T(4,128)}, u32[]{:S(2)}) copy-start(f32[4,4,128]{2,1,0:T(4,128)} %param.21) | copy-start | bytes 24580
  7.2 8.3 %copy-start.2 = (f32[8192]{0:T(1024)S(1)}, f32[8192]{0:T(1024)}, u32[]{:S(2)}) copy-start(f32[8192]{0:T(1024)} %param.18) | copy-start | bytes 98308
  7.2 97.6 %all-gather.3.cloned.1.call-start = ((), (), s32[]{:S(2)}) async-start(), calls=%async_computation | async-start | bytes 25952256 | tf_op jit(solution)/shard_map/all_gather | solution.py:131
  9.4 6.1 %copy-start.1 = (bf16[256,8192]{1,0:T(8,128)(2,1)S(1)}, bf16[256,8192]{1,0:T(8,128)(2,1)}, u32[]{:S(2)}) copy-start(bf16[256,8192]{1,0:T(8,128)(2,1)} %param.17) | copy-start | bytes 12582916
  125.0 8.9 %copy-start.3 = (s32[8]{0:T(128)S(1)}, s32[8]{0:T(128)}, u32[]{:S(2)}) copy-start(s32[8]{0:T(128)} %param.22) | copy-start | bytes 100
  128.2 5.7 %collective-permute-start = (f32[19,512]{1,0:T(8,128)S(1)}, f32[19,512]{1,0:T(8,128)S(1)}, u32[]{:S(2)}, u32[]{:S(2)}) collective-permute-start(f32[19,512]{1,0:T(8,128)S(1)} %get-tuple-element.27), channel_id=1, source_target_pairs={{0,1},{1,2},{2,3},{3,0},{4,5},{5,6},{6,7},{7,4},{8,9},{9,10},{10,1... | collective-permute-start | bytes 116744 | tf_op jit(solution)/shard_map/ppermute | solution.py:164
  129.8 5.6 %collective-permute-start.1 = (f32[19,512]{1,0:T(8,128)S(1)}, f32[19,512]{1,0:T(8,128)S(1)}, u32[]{:S(2)}, u32[]{:S(2)}) collective-permute-start(f32[19,512]{1,0:T(8,128)S(1)} %get-tuple-element.27), channel_id=1, source_target_pairs={{0,2},{1,3},{2,0},{3,1},{4,6},{5,7},{6,4},{7,5},{8,10},{9,11},{10,... | collective-permute-start | bytes 116744 | tf_op jit(solution)/shard_map/ppermute | solution.py:164
  132.4 4.1 %collective-permute-start.2 = (f32[19,512]{1,0:T(8,128)S(1)}, f32[19,512]{1,0:T(8,128)S(1)}, u32[]{:S(2)}, u32[]{:S(2)}) collective-permute-start(f32[19,512]{1,0:T(8,128)S(1)} %get-tuple-element.27), channel_id=1, source_target_pairs={{0,3},{1,0},{2,1},{3,2},{4,7},{5,4},{6,5},{7,6},{8,11},{9,8},{10,9... | collective-permute-start | bytes 116744 | tf_op jit(solution)/shard_map/ppermute | solution.py:164
Sparse Core Ops, SparseCore 0:
  10.3 94.5 all-gather.2

commit v13 on v6

--- a/solution.py
+++ b/solution.py
@@ -59,10 +59,14 @@
         )
     kv_ref[...] += acc
 
-    t = tok_ref[...]
-    k = g_ref.shape[0] * g_ref.shape[1]
-    gacc[...] += jnp.dot(t, g_ref[...].reshape(k, -1), preferred_element_type=jnp.float32)
-    uacc[...] += jnp.dot(t, u_ref[...].reshape(k, -1), preferred_element_type=jnp.float32)
+    sub = g_ref.shape[0] // 2
+    k = sub * g_ref.shape[1]
+    h = j % 2
+    t = tok_ref[:, pl.ds(pl.multiple_of(h * k, k), k)]
+    g_w = g_ref[pl.ds(h * sub, sub)].reshape(k, -1)
+    u_w = u_ref[pl.ds(h * sub, sub)].reshape(k, -1)
+    gacc[...] += jnp.dot(t, g_w, preferred_element_type=jnp.float32)
+    uacc[...] += jnp.dot(t, u_w, preferred_element_type=jnp.float32)
 
     @pl.when(j == pl.num_programs(0) - 1)
     def _():
@@ -78,6 +82,7 @@
     n_norm = normed.shape[0]
     n_tok = tokens.shape[0]
     group = n_dev // steps
+    d_group = 2 * group
     gate_blk = kv_rows // d_rows
     seg_kv, scores = pl.pallas_call(
         fused_kernel,
@@ -85,9 +90,9 @@
         in_specs=[
             pl.BlockSpec((n_norm, group * kv_rows), lambda j: (0, j)),
             pl.BlockSpec((group, kv_rows, cols), lambda j: (j, 0, 0)),
-            pl.BlockSpec((n_tok, group * d_rows), lambda j: (0, j)),
-            pl.BlockSpec((group, d_rows, cols), lambda j: (j, gate_blk, 0)),
-            pl.BlockSpec((group, d_rows, cols), lambda j: (j, gate_blk + 1, 0)),
+            pl.BlockSpec((n_tok, d_group * d_rows), lambda j: (0, j // 2)),
+            pl.BlockSpec((d_group, d_rows, cols), lambda j: (j // 2, gate_blk, 0)),
+            pl.BlockSpec((d_group, d_rows, cols), lambda j: (j // 2, gate_blk + 1, 0)),
             pl.BlockSpec((1, cols), lambda j: (0, 0)),
         ],
         out_specs=[
@@ -133,7 +138,7 @@
 
     normed = normalize_rows(verifier_rows, norm_gain)
     seg_kv, partial_scores = project_all(
-        normed, draft_tokens, gathered, draft_head, kv_rows, d_rows, 4
+        normed, draft_tokens, gathered, draft_head, kv_rows, d_rows, 8
     )
     seg_keys = seg_kv[:, :kv_cols]
     seg_values = seg_kv[:, kv_cols:]

time: 146 us -> 149 us (1.021)
  Pallas kernels: 20.3 us -> 23 us
    pallas_call x1, Pallas kernels: 20.3 us -> 23 us  [project_all(): pl.pallas_call(fused_kernel, grid=(steps,), in_specs=[pl.BlockSpec((n_nor...]
where the time goes in v13:
time: 149 us
  waiting for transfers between devices  88.8 us (60%)
  Pallas kernels  23 us (15%)
  between operations  14.2 us (10%)
  other arithmetic  13.2 us (9%)
  starting transfers between devices  5.72 us (4%)
  local copies, waits for them, and re-layouts  2.69 us (2%)
    all_gather x1, waiting for transfers between devices, local(): gathered = lax.all_gather(block, 'fsdp', axis=0, tiled=False)  86.1 us
    pallas_call x1, Pallas kernels, project_all(): pl.pallas_call(fused_kernel, grid=(steps,), in_specs=[pl.BlockSpec((n_nor...  23 us
    ppermute x3, starting transfers between devices, local(): lax.ppermute(tail, 'seq', [(i, (i + k) % n_seq) for i in range(n_seq)])  5.68 us
    convert_element_type x1, other arithmetic, normalize_rows(): return (values * scale * norm_gain).astype(jnp.bfloat16)  3.16 us
    reduce_sum x1, other arithmetic, normalize_rows(): scale = lax.rsqrt(jnp.mean(values * values, axis=-1, keepdims=True) + eps)  3.1 us
  transfers between devices with their start and end apart: 4, of which 3 were waited for; matrix products, arithmetic and copies ran while one was open for 6% of the time, Pallas kernels for 0%

profile of v13, /device:TPU:0, one launch (start us, length us, event | category | flops | bytes accessed | tf_op | source)
XLA Modules:
  0.0 148.7 jit_solution(15657166404132027941)
XLA Ops:
  7.2 2.2 %pad_maximum_fusion = bf16[384,1024]{1,0:T(8,128)(2,1)} fusion(bf16[64,1024]{1,0:T(8,128)(2,1)} %param.15, bf16[64,1024]{1,0:T(8,128)(2,1)} %param.14, bf16[256,512]{1,0:T(8,128)(2,1)} %param.20, bf16[256,512]{1,0:T(8,128)(2,1)} %param.19), kind=kLoop, calls=%fused_computation.12 | loop fusion | flops 3145728 | bytes 1572864 | tf_op jit(solution)/shard_map/concatenate | solution.py:135
  9.4 1.0 fusion.19
  10.5 0.6 compare_reduce_fusion.1
  11.1 1.3 fusion.27
  12.4 3.1 %fusion.2 = f32[256]{0:T(256)S(1)} fusion(bf16[256,8192]{1,0:T(8,128)(2,1)} %param.17), kind=kLoop, calls=%fused_computation.4 | loop fusion | flops 6291200 | bytes 4195328 | tf_op jit(solution)/shard_map/reduce_sum | solution.py:20
  15.5 3.2 %fusion.4.x_ref = bf16[256,8192]{1,0:T(8,128)(2,1)} fusion(bf16[256,8192]{1,0:T(8,128)(2,1)S(1)} %copy-done.1, f32[8192]{0:T(1024)S(1)} %copy-done.2, f32[256]{0:T(256)S(1)} %add_rsqrt_fusion), kind=kLoop, calls=%fused_computation.6 | loop fusion | flops 8388608 | bytes 8422400 | tf_op jit(solution)/shard_map/convert_element_type | solution.py:21
  18.7 86.1 %all-gather.3.cloned.1.call-done = bf16[12288,1024]{1,0:T(8,128)(2,1)} async-done(((bf16[384,1024]{1,0:T(8,128)(2,1)}), bf16[12288,1024]{1,0:T(8,128)(2,1)}) %all-gather.3.cloned.1.call-update) | async-done | bytes 25165840 | tf_op jit(solution)/shard_map/all_gather | solution.py:136
  104.8 23.0 %shard_map.122 = (f32[256,1024]{1,0:T(8,128)}, f32[8,1024]{1,0:T(8,128)}) custom-call(bf16[256,8192]{1,0:T(8,128)(2,1)} %fusion.4.x_ref, bf16[32,384,1024]{2,1,0:T(8,128)(2,1)} %bitcast.31, bf16[1024,2048]{1,0:T(8,128)(2,1)} %tok_ref.1, bf16[32,384,1024]{2,1,0:T(8,128)(2,1)} %bitcast.32, bf16[32,384,1024]{2,1,0:T(8,128)(2,1)} %bitcast.33, f32[1,1024]{1,0:T(1,128)} %bitcast.48), custom_call_target="tpu_custom_call" | custom-call | tf_op jit(solution)/shard_map/pallas_call | solution.py:87
  127.9 1.3 fusion.35
  129.1 0.2 reshape.113
  129.3 0.4 multiply_reduce_fusion.4
  129.7 0.2 reshape.115
  129.9 0.8 slice_reduce_fusion
  130.7 0.3 multiply_reduce_fusion.3
  131.1 1.5 %collective-permute-start = (f32[19,512]{1,0:T(8,128)S(1)}, f32[19,512]{1,0:T(8,128)S(1)}, u32[]{:S(2)}, u32[]{:S(2)}) collective-permute-start(f32[19,512]{1,0:T(8,128)S(1)} %get-tuple-element.27), channel_id=1, source_target_pairs={{0,1},{1,2},{2,3},{3,0},{4,5},{5,6},{6,7},{7,4},{8,9},{9,10},{10,1... | collective-permute-start | bytes 116744 | tf_op jit(solution)/shard_map/ppermute | solution.py:169
  132.7 2.7 %collective-permute-start.1 = (f32[19,512]{1,0:T(8,128)S(1)}, f32[19,512]{1,0:T(8,128)S(1)}, u32[]{:S(2)}, u32[]{:S(2)}) collective-permute-start(f32[19,512]{1,0:T(8,128)S(1)} %get-tuple-element.27), channel_id=1, source_target_pairs={{0,2},{1,3},{2,0},{3,1},{4,6},{5,7},{6,4},{7,5},{8,10},{9,11},{10,... | collective-permute-start | bytes 116744 | tf_op jit(solution)/shard_map/ppermute | solution.py:169
  135.3 1.5 collective-permute-start.2
  136.8 1.5 %collective-permute-done.1 = f32[19,512]{1,0:T(8,128)S(1)} collective-permute-done((f32[19,512]{1,0:T(8,128)S(1)}, f32[19,512]{1,0:T(8,128)S(1)}, u32[]{:S(2)}, u32[]{:S(2)}) %collective-permute-start.1) | collective-permute-done | bytes 38944 | tf_op jit(solution)/shard_map/ppermute | solution.py:169
  138.3 1.1 collective-permute-done.2
  139.6 0.2 multiply_reduce_fusion.1
  140.1 0.5 add_divide_fusion
  140.6 0.2 fusion.36
  140.8 0.2 multiply_reduce_fusion
  141.1 0.7 fusion.15
  (31 shorter events, 0.7 us)
Async XLA Ops:
  7.2 2.3 %copy-start = (f32[4,4,128]{2,1,0:T(4,128)S(1)}, f32[4,4,128]{2,1,0:T(4,128)}, u32[]{:S(2)}) copy-start(f32[4,4,128]{2,1,0:T(4,128)} %param.21) | copy-start | bytes 24580
  7.2 8.3 %copy-start.2 = (f32[8192]{0:T(1024)S(1)}, f32[8192]{0:T(1024)}, u32[]{:S(2)}) copy-start(f32[8192]{0:T(1024)} %param.18) | copy-start | bytes 98308
  7.2 97.6 %all-gather.3.cloned.1.call-start = ((), (), s32[]{:S(2)}) async-start(), calls=%async_computation | async-start | bytes 25952256 | tf_op jit(solution)/shard_map/all_gather | solution.py:136
  9.4 6.1 %copy-start.1 = (bf16[256,8192]{1,0:T(8,128)(2,1)S(1)}, bf16[256,8192]{1,0:T(8,128)(2,1)}, u32[]{:S(2)}) copy-start(bf16[256,8192]{1,0:T(8,128)(2,1)} %param.17) | copy-start | bytes 12582916
  127.9 8.9 %copy-start.3 = (s32[8]{0:T(128)S(1)}, s32[8]{0:T(128)}, u32[]{:S(2)}) copy-start(s32[8]{0:T(128)} %param.22) | copy-start | bytes 100
  131.1 5.7 %collective-permute-start = (f32[19,512]{1,0:T(8,128)S(1)}, f32[19,512]{1,0:T(8,128)S(1)}, u32[]{:S(2)}, u32[]{:S(2)}) collective-permute-start(f32[19,512]{1,0:T(8,128)S(1)} %get-tuple-element.27), channel_id=1, source_target_pairs={{0,1},{1,2},{2,3},{3,0},{4,5},{5,6},{6,7},{7,4},{8,9},{9,10},{10,1... | collective-permute-start | bytes 116744 | tf_op jit(solution)/shard_map/ppermute | solution.py:169
  132.7 5.6 %collective-permute-start.1 = (f32[19,512]{1,0:T(8,128)S(1)}, f32[19,512]{1,0:T(8,128)S(1)}, u32[]{:S(2)}, u32[]{:S(2)}) collective-permute-start(f32[19,512]{1,0:T(8,128)S(1)} %get-tuple-element.27), channel_id=1, source_target_pairs={{0,2},{1,3},{2,0},{3,1},{4,6},{5,7},{6,4},{7,5},{8,10},{9,11},{10,... | collective-permute-start | bytes 116744 | tf_op jit(solution)/shard_map/ppermute | solution.py:169
  135.3 4.1 %collective-permute-start.2 = (f32[19,512]{1,0:T(8,128)S(1)}, f32[19,512]{1,0:T(8,128)S(1)}, u32[]{:S(2)}, u32[]{:S(2)}) collective-permute-start(f32[19,512]{1,0:T(8,128)S(1)} %get-tuple-element.27), channel_id=1, source_target_pairs={{0,3},{1,0},{2,1},{3,2},{4,7},{5,4},{6,5},{7,6},{8,11},{9,8},{10,9... | collective-permute-start | bytes 116744 | tf_op jit(solution)/shard_map/ppermute | solution.py:169
Sparse Core Ops, SparseCore 0:
  10.3 94.5 all-gather.2

commit v14 on v6

--- a/solution.py
+++ b/solution.py
@@ -162,7 +162,7 @@
         [tail]
         + [
             lax.ppermute(tail, "seq", [(i, (i + k) % n_seq) for i in range(n_seq)])
-            for k in range(1, n_seq)
+            for k in sorted(range(1, n_seq), key=lambda k: min(k, n_seq - k))
         ]
     )
     score_rows = partial_scores.shape[0] // width

time: 146 us -> 147 us (level)
  transfers between devices with their start and end apart: 4 -> 4, of which waited for: 3 -> 4; matrix products, arithmetic and copies ran while one was open for 6% -> 6% of each run, Pallas kernels for 0% -> 0%
where the time goes in v14:
time: 147 us; the launch traced here: 146 us
  waiting for transfers between devices  89.9 us (61%)
  Pallas kernels  20.3 us (14%)
  between operations  14.2 us (10%)
  other arithmetic  13.2 us (9%)
  starting transfers between devices  5.11 us (3%)
  local copies, waits for them, and re-layouts  2.69 us (2%)
    all_gather x1, waiting for transfers between devices, local(): gathered = lax.all_gather(block, 'fsdp', axis=0, tiled=False)  86.1 us
    pallas_call x1, Pallas kernels, project_all(): pl.pallas_call(fused_kernel, grid=(steps,), in_specs=[pl.BlockSpec((n_nor...  20.3 us
    ppermute x3, starting transfers between devices, local(): lax.ppermute(tail, 'seq', [(i, (i + k) % n_seq) for i in range(n_seq)])  5.07 us
    ppermute x3, waiting for transfers between devices, local(): lax.ppermute(tail, 'seq', [(i, (i + k) % n_seq) for i in range(n_seq)])  3.82 us
    convert_element_type x1, other arithmetic, normalize_rows(): return (values * scale * norm_gain).astype(jnp.bfloat16)  3.16 us
    reduce_sum x1, other arithmetic, normalize_rows(): scale = lax.rsqrt(jnp.mean(values * values, axis=-1, keepdims=True) + eps)  3.1 us
  transfers between devices with their start and end apart: 4, of which 4 were waited for; matrix products, arithmetic and copies ran while one was open for 6% of the time, Pallas kernels for 0%

profile of v14, /device:TPU:0, one launch (start us, length us, event | category | flops | bytes accessed | tf_op | source)
XLA Modules:
  0.0 146.5 jit_solution(1494594378355603736)
XLA Ops:
  7.2 2.2 %pad_maximum_fusion = bf16[384,1024]{1,0:T(8,128)(2,1)} fusion(bf16[64,1024]{1,0:T(8,128)(2,1)} %param.15, bf16[64,1024]{1,0:T(8,128)(2,1)} %param.14, bf16[256,512]{1,0:T(8,128)(2,1)} %param.20, bf16[256,512]{1,0:T(8,128)(2,1)} %param.19), kind=kLoop, calls=%fused_computation.12 | loop fusion | flops 3145728 | bytes 1572864 | tf_op jit(solution)/shard_map/concatenate | solution.py:130
  9.4 1.0 fusion.19
  10.5 0.6 compare_reduce_fusion.1
  11.1 1.3 fusion.27
  12.4 3.1 %fusion.2 = f32[256]{0:T(256)S(1)} fusion(bf16[256,8192]{1,0:T(8,128)(2,1)} %param.17), kind=kLoop, calls=%fused_computation.4 | loop fusion | flops 6291200 | bytes 4195328 | tf_op jit(solution)/shard_map/reduce_sum | solution.py:20
  15.5 3.2 %fusion.4.x_ref = bf16[256,8192]{1,0:T(8,128)(2,1)} fusion(bf16[256,8192]{1,0:T(8,128)(2,1)S(1)} %copy-done.1, f32[8192]{0:T(1024)S(1)} %copy-done.2, f32[256]{0:T(256)S(1)} %add_rsqrt_fusion), kind=kLoop, calls=%fused_computation.6 | loop fusion | flops 8388608 | bytes 8422400 | tf_op jit(solution)/shard_map/convert_element_type | solution.py:21
  18.7 86.1 %all-gather.3.cloned.1.call-done = bf16[12288,1024]{1,0:T(8,128)(2,1)} async-done(((bf16[384,1024]{1,0:T(8,128)(2,1)}), bf16[12288,1024]{1,0:T(8,128)(2,1)}) %all-gather.3.cloned.1.call-update) | async-done | bytes 25165840 | tf_op jit(solution)/shard_map/all_gather | solution.py:131
  104.8 20.3 %shard_map.122 = (f32[256,1024]{1,0:T(8,128)}, f32[8,1024]{1,0:T(8,128)}) custom-call(bf16[256,8192]{1,0:T(8,128)(2,1)} %fusion.4.x_ref, bf16[32,384,1024]{2,1,0:T(8,128)(2,1)} %bitcast.31, bf16[1024,2048]{1,0:T(8,128)(2,1)} %tok_ref.1, bf16[32,384,1024]{2,1,0:T(8,128)(2,1)} %bitcast.32, bf16[32,384,1024]{2,1,0:T(8,128)(2,1)} %bitcast.33, f32[1,1024]{1,0:T(1,128)} %bitcast.48), custom_call_target="tpu_custom_call" | custom-call | tf_op jit(solution)/shard_map/pallas_call | solution.py:82
  125.1 1.3 fusion.35
  126.4 0.2 reshape.113
  126.6 0.4 multiply_reduce_fusion.4
  127.0 0.2 reshape.115
  127.2 0.8 slice_reduce_fusion
  128.0 0.3 multiply_reduce_fusion.3
  128.4 1.5 %collective-permute-start = (f32[19,512]{1,0:T(8,128)S(1)}, f32[19,512]{1,0:T(8,128)S(1)}, u32[]{:S(2)}, u32[]{:S(2)}) collective-permute-start(f32[19,512]{1,0:T(8,128)S(1)} %get-tuple-element.27), channel_id=1, source_target_pairs={{0,1},{1,2},{2,3},{3,0},{4,5},{5,6},{6,7},{7,4},{8,9},{9,10},{10,1... | collective-permute-start | bytes 116744 | tf_op jit(solution)/shard_map/ppermute | solution.py:164
  129.9 1.8 %collective-permute-start.1 = (f32[19,512]{1,0:T(8,128)S(1)}, f32[19,512]{1,0:T(8,128)S(1)}, u32[]{:S(2)}, u32[]{:S(2)}) collective-permute-start(f32[19,512]{1,0:T(8,128)S(1)} %get-tuple-element.27), channel_id=1, source_target_pairs={{0,3},{1,0},{2,1},{3,2},{4,7},{5,4},{6,5},{7,6},{8,11},{9,8},{10,9... | collective-permute-start | bytes 116744 | tf_op jit(solution)/shard_map/ppermute | solution.py:164
  131.7 1.8 %collective-permute-start.2 = (f32[19,512]{1,0:T(8,128)S(1)}, f32[19,512]{1,0:T(8,128)S(1)}, u32[]{:S(2)}, u32[]{:S(2)}) collective-permute-start(f32[19,512]{1,0:T(8,128)S(1)} %get-tuple-element.27), channel_id=1, source_target_pairs={{0,2},{1,3},{2,0},{3,1},{4,6},{5,7},{6,4},{7,5},{8,10},{9,11},{10,... | collective-permute-start | bytes 116744 | tf_op jit(solution)/shard_map/ppermute | solution.py:164
  133.4 0.3 collective-permute-done
  133.7 0.3 collective-permute-done.1
  134.0 3.3 %collective-permute-done.2 = f32[19,512]{1,0:T(8,128)S(1)} collective-permute-done((f32[19,512]{1,0:T(8,128)S(1)}, f32[19,512]{1,0:T(8,128)S(1)}, u32[]{:S(2)}, u32[]{:S(2)}) %collective-permute-start.2) | collective-permute-done | bytes 38944 | tf_op jit(solution)/shard_map/ppermute | solution.py:164
  137.4 0.2 multiply_reduce_fusion.1
  138.0 0.5 add_divide_fusion
  138.7 0.2 multiply_reduce_fusion
  139.0 0.7 fusion.15
  (31 shorter events, 0.9 us)
Async XLA Ops:
  7.2 2.3 %copy-start = (f32[4,4,128]{2,1,0:T(4,128)S(1)}, f32[4,4,128]{2,1,0:T(4,128)}, u32[]{:S(2)}) copy-start(f32[4,4,128]{2,1,0:T(4,128)} %param.21) | copy-start | bytes 24580
  7.2 8.3 %copy-start.2 = (f32[8192]{0:T(1024)S(1)}, f32[8192]{0:T(1024)}, u32[]{:S(2)}) copy-start(f32[8192]{0:T(1024)} %param.18) | copy-start | bytes 98308
  7.2 97.6 %all-gather.3.cloned.1.call-start = ((), (), s32[]{:S(2)}) async-start(), calls=%async_computation | async-start | bytes 25952256 | tf_op jit(solution)/shard_map/all_gather | solution.py:131
  9.4 6.1 %copy-start.1 = (bf16[256,8192]{1,0:T(8,128)(2,1)S(1)}, bf16[256,8192]{1,0:T(8,128)(2,1)}, u32[]{:S(2)}) copy-start(bf16[256,8192]{1,0:T(8,128)(2,1)} %param.17) | copy-start | bytes 12582916
  125.1 8.3 %copy-start.3 = (s32[8]{0:T(128)S(1)}, s32[8]{0:T(128)}, u32[]{:S(2)}) copy-start(s32[8]{0:T(128)} %param.22) | copy-start | bytes 100
  128.4 5.4 %collective-permute-start = (f32[19,512]{1,0:T(8,128)S(1)}, f32[19,512]{1,0:T(8,128)S(1)}, u32[]{:S(2)}, u32[]{:S(2)}) collective-permute-start(f32[19,512]{1,0:T(8,128)S(1)} %get-tuple-element.27), channel_id=1, source_target_pairs={{0,1},{1,2},{2,3},{3,0},{4,5},{5,6},{6,7},{7,4},{8,9},{9,10},{10,1... | collective-permute-start | bytes 116744 | tf_op jit(solution)/shard_map/ppermute | solution.py:164
  129.9 4.1 %collective-permute-start.1 = (f32[19,512]{1,0:T(8,128)S(1)}, f32[19,512]{1,0:T(8,128)S(1)}, u32[]{:S(2)}, u32[]{:S(2)}) collective-permute-start(f32[19,512]{1,0:T(8,128)S(1)} %get-tuple-element.27), channel_id=1, source_target_pairs={{0,3},{1,0},{2,1},{3,2},{4,7},{5,4},{6,5},{7,6},{8,11},{9,8},{10,9... | collective-permute-start | bytes 116744 | tf_op jit(solution)/shard_map/ppermute | solution.py:164
  131.7 5.6 %collective-permute-start.2 = (f32[19,512]{1,0:T(8,128)S(1)}, f32[19,512]{1,0:T(8,128)S(1)}, u32[]{:S(2)}, u32[]{:S(2)}) collective-permute-start(f32[19,512]{1,0:T(8,128)S(1)} %get-tuple-element.27), channel_id=1, source_target_pairs={{0,2},{1,3},{2,0},{3,1},{4,6},{5,7},{6,4},{7,5},{8,10},{9,11},{10,... | collective-permute-start | bytes 116744 | tf_op jit(solution)/shard_map/ppermute | solution.py:164
Sparse Core Ops, SparseCore 0:
  10.3 94.5 all-gather.2

commit v15 on v6

--- a/solution.py
+++ b/solution.py
@@ -70,7 +70,10 @@
         act = g / (1.0 + jnp.exp(-g))
         col = jnp.sum(act * uacc[...] * head_ref[...], axis=1, keepdims=True)
         wide = jnp.broadcast_to(col, (col.shape[0], 128))
-        score_ref[...] = jnp.transpose(wide)[0 : score_ref.shape[0], :]
+        row = jnp.transpose(wide)[0:1, :]
+        width = score_ref.shape[1]
+        for r in range(score_ref.shape[0]):
+            score_ref[r : r + 1, :] = row[:, r * width : (r + 1) * width]
 
 
 def project_all(normed, tokens, gathered, head, kv_rows, d_rows, steps):
@@ -92,18 +95,18 @@
         ],
         out_specs=[
             pl.BlockSpec((n_norm, cols), lambda j: (0, 0)),
-            pl.BlockSpec((8, n_tok), lambda j: (0, 0)),
+            pl.BlockSpec((n_tok // (cols // 2), cols // 2), lambda j: (0, 0)),
         ],
         out_shape=[
             jax.ShapeDtypeStruct((n_norm, cols), jnp.float32),
-            jax.ShapeDtypeStruct((8, n_tok), jnp.float32),
+            jax.ShapeDtypeStruct((n_tok // (cols // 2), cols // 2), jnp.float32),
         ],
         scratch_shapes=[
             pltpu.VMEM((n_tok, cols), jnp.float32),
             pltpu.VMEM((n_tok, cols), jnp.float32),
         ],
     )(normed, gathered, tokens, gathered, gathered, head.reshape(1, cols))
-    return seg_kv, scores[0]
+    return seg_kv, scores
 
 
 def local(
@@ -165,7 +168,7 @@
             for k in range(1, n_seq)
         ]
     )
-    score_rows = partial_scores.shape[0] // width
+    score_rows = partial_scores.size // width
     scores_all = tail_all[:, :score_rows].reshape(n_seq, -1)
     summary_all = tail_all[:, score_rows:]
     own = lax.axis_index("seq")

time: 146 us -> 145 us (level)
  no operation moved by 1% of the time
where the time goes in v15:
time: 145 us
  waiting for transfers between devices  88.8 us (61%)
  Pallas kernels  20.3 us (14%)
  between operations  14.2 us (10%)
  other arithmetic  13.2 us (9%)
  starting transfers between devices  5.72 us (4%)
  local copies, waits for them, and re-layouts  1.92 us (1%)
    all_gather x1, waiting for transfers between devices, local(): gathered = lax.all_gather(block, 'fsdp', axis=0, tiled=False)  86.1 us
    pallas_call x1, Pallas kernels, project_all(): pl.pallas_call(fused_kernel, grid=(steps,), in_specs=[pl.BlockSpec((n_nor...  20.3 us
    ppermute x3, starting transfers between devices, local(): lax.ppermute(tail, 'seq', [(i, (i + k) % n_seq) for i in range(n_seq)])  5.68 us
    convert_element_type x1, other arithmetic, normalize_rows(): return (values * scale * norm_gain).astype(jnp.bfloat16)  3.16 us
    reduce_sum x1, other arithmetic, normalize_rows(): scale = lax.rsqrt(jnp.mean(values * values, axis=-1, keepdims=True) + eps)  3.1 us
  transfers between devices with their start and end apart: 4, of which 3 were waited for; matrix products, arithmetic and copies ran while one was open for 6% of the time, Pallas kernels for 0%

profile of v15, /device:TPU:0, one launch (start us, length us, event | category | flops | bytes accessed | tf_op | source)
XLA Modules:
  0.0 145.1 jit_solution(17450035405218177160)
XLA Ops:
  7.2 2.2 %pad_maximum_fusion = bf16[384,1024]{1,0:T(8,128)(2,1)} fusion(bf16[64,1024]{1,0:T(8,128)(2,1)} %param.15, bf16[64,1024]{1,0:T(8,128)(2,1)} %param.14, bf16[256,512]{1,0:T(8,128)(2,1)} %param.20, bf16[256,512]{1,0:T(8,128)(2,1)} %param.19), kind=kLoop, calls=%fused_computation.12 | loop fusion | flops 3145728 | bytes 1572864 | tf_op jit(solution)/shard_map/concatenate | solution.py:133
  9.4 1.0 fusion.19
  10.5 0.6 compare_reduce_fusion.1
  11.1 1.3 fusion.27
  12.4 3.1 %fusion.2 = f32[256]{0:T(256)S(1)} fusion(bf16[256,8192]{1,0:T(8,128)(2,1)} %param.17), kind=kLoop, calls=%fused_computation.4 | loop fusion | flops 6291200 | bytes 4195328 | tf_op jit(solution)/shard_map/reduce_sum | solution.py:20
  15.5 3.2 %fusion.4.x_ref = bf16[256,8192]{1,0:T(8,128)(2,1)} fusion(bf16[256,8192]{1,0:T(8,128)(2,1)S(1)} %copy-done.1, f32[8192]{0:T(1024)S(1)} %copy-done.2, f32[256]{0:T(256)S(1)} %add_rsqrt_fusion), kind=kLoop, calls=%fused_computation.6 | loop fusion | flops 8388608 | bytes 8422400 | tf_op jit(solution)/shard_map/convert_element_type | solution.py:21
  18.7 86.1 %all-gather.3.cloned.1.call-done = bf16[12288,1024]{1,0:T(8,128)(2,1)} async-done(((bf16[384,1024]{1,0:T(8,128)(2,1)}), bf16[12288,1024]{1,0:T(8,128)(2,1)}) %all-gather.3.cloned.1.call-update) | async-done | bytes 25165840 | tf_op jit(solution)/shard_map/all_gather | solution.py:134
  104.8 20.3 %shard_map.122 = (f32[256,1024]{1,0:T(8,128)}, f32[2,512]{1,0:T(2,128)}) custom-call(bf16[256,8192]{1,0:T(8,128)(2,1)} %fusion.4.x_ref, bf16[32,384,1024]{2,1,0:T(8,128)(2,1)} %bitcast.31, bf16[1024,2048]{1,0:T(8,128)(2,1)} %tok_ref.1, bf16[32,384,1024]{2,1,0:T(8,128)(2,1)} %bitcast.32, bf16[32,384,1024]{2,1,0:T(8,128)(2,1)} %bitcast.33, f32[1,1024]{1,0:T(1,128)} %bitcast.48), custom_call_target="tpu_custom_call" | custom-call | tf_op jit(solution)/shard_map/pallas_call | solution.py:85
  125.1 1.3 fusion.35
  126.4 0.2 reshape.113
  126.6 0.4 multiply_reduce_fusion.4
  127.0 0.2 reshape.115
  127.2 0.3 multiply_reduce_fusion.3
  127.6 1.5 %collective-permute-start = (f32[19,512]{1,0:T(8,128)S(1)}, f32[19,512]{1,0:T(8,128)S(1)}, u32[]{:S(2)}, u32[]{:S(2)}) collective-permute-start(f32[19,512]{1,0:T(8,128)S(1)} %get-tuple-element.27), channel_id=1, source_target_pairs={{0,1},{1,2},{2,3},{3,0},{4,5},{5,6},{6,7},{7,4},{8,9},{9,10},{10,1... | collective-permute-start | bytes 116744 | tf_op jit(solution)/shard_map/ppermute | solution.py:167
  129.1 2.7 %collective-permute-start.1 = (f32[19,512]{1,0:T(8,128)S(1)}, f32[19,512]{1,0:T(8,128)S(1)}, u32[]{:S(2)}, u32[]{:S(2)}) collective-permute-start(f32[19,512]{1,0:T(8,128)S(1)} %get-tuple-element.27), channel_id=1, source_target_pairs={{0,2},{1,3},{2,0},{3,1},{4,6},{5,7},{6,4},{7,5},{8,10},{9,11},{10,... | collective-permute-start | bytes 116744 | tf_op jit(solution)/shard_map/ppermute | solution.py:167
  131.8 1.5 %collective-permute-start.2 = (f32[19,512]{1,0:T(8,128)S(1)}, f32[19,512]{1,0:T(8,128)S(1)}, u32[]{:S(2)}, u32[]{:S(2)}) collective-permute-start(f32[19,512]{1,0:T(8,128)S(1)} %get-tuple-element.27), channel_id=1, source_target_pairs={{0,3},{1,0},{2,1},{3,2},{4,7},{5,4},{6,5},{7,6},{8,11},{9,8},{10,9... | collective-permute-start | bytes 116744 | tf_op jit(solution)/shard_map/ppermute | solution.py:167
  133.3 1.5 %collective-permute-done.1 = f32[19,512]{1,0:T(8,128)S(1)} collective-permute-done((f32[19,512]{1,0:T(8,128)S(1)}, f32[19,512]{1,0:T(8,128)S(1)}, u32[]{:S(2)}, u32[]{:S(2)}) %collective-permute-start.1) | collective-permute-done | bytes 38944 | tf_op jit(solution)/shard_map/ppermute | solution.py:167
  134.8 1.1 collective-permute-done.2
  136.1 0.2 multiply_reduce_fusion.1
  136.5 0.1 reduce_sum.96
  136.6 0.5 add_divide_fusion
  137.1 0.2 fusion.36
  137.3 0.2 multiply_reduce_fusion
  137.6 0.7 fusion.15
  (31 shorter events, 0.6 us)
Async XLA Ops:
  7.2 2.3 %copy-start = (f32[4,4,128]{2,1,0:T(4,128)S(1)}, f32[4,4,128]{2,1,0:T(4,128)}, u32[]{:S(2)}) copy-start(f32[4,4,128]{2,1,0:T(4,128)} %param.21) | copy-start | bytes 24580
  7.2 8.3 %copy-start.2 = (f32[8192]{0:T(1024)S(1)}, f32[8192]{0:T(1024)}, u32[]{:S(2)}) copy-start(f32[8192]{0:T(1024)} %param.18) | copy-start | bytes 98308
  7.2 97.6 %all-gather.3.cloned.1.call-start = ((), (), s32[]{:S(2)}) async-start(), calls=%async_computation | async-start | bytes 25952256 | tf_op jit(solution)/shard_map/all_gather | solution.py:134
  9.4 6.1 %copy-start.1 = (bf16[256,8192]{1,0:T(8,128)(2,1)S(1)}, bf16[256,8192]{1,0:T(8,128)(2,1)}, u32[]{:S(2)}) copy-start(bf16[256,8192]{1,0:T(8,128)(2,1)} %param.17) | copy-start | bytes 12582916
  125.1 2.5 %copy-start.3 = (f32[2,512]{1,0:T(2,128)S(1)}, f32[2,512]{1,0:T(2,128)}, u32[]{:S(2)}) copy-start(f32[2,512]{1,0:T(2,128)} %get-tuple-element.16) | copy-start | bytes 12292
  125.1 8.2 %copy-start.4 = (s32[8]{0:T(128)S(1)}, s32[8]{0:T(128)}, u32[]{:S(2)}) copy-start(s32[8]{0:T(128)} %param.22) | copy-start | bytes 100
  127.6 5.7 %collective-permute-start = (f32[19,512]{1,0:T(8,128)S(1)}, f32[19,512]{1,0:T(8,128)S(1)}, u32[]{:S(2)}, u32[]{:S(2)}) collective-permute-start(f32[19,512]{1,0:T(8,128)S(1)} %get-tuple-element.27), channel_id=1, source_target_pairs={{0,1},{1,2},{2,3},{3,0},{4,5},{5,6},{6,7},{7,4},{8,9},{9,10},{10,1... | collective-permute-start | bytes 116744 | tf_op jit(solution)/shard_map/ppermute | solution.py:167
  129.1 5.6 %collective-permute-start.1 = (f32[19,512]{1,0:T(8,128)S(1)}, f32[19,512]{1,0:T(8,128)S(1)}, u32[]{:S(2)}, u32[]{:S(2)}) collective-permute-start(f32[19,512]{1,0:T(8,128)S(1)} %get-tuple-element.27), channel_id=1, source_target_pairs={{0,2},{1,3},{2,0},{3,1},{4,6},{5,7},{6,4},{7,5},{8,10},{9,11},{10,... | collective-permute-start | bytes 116744 | tf_op jit(solution)/shard_map/ppermute | solution.py:167
  131.8 4.1 %collective-permute-start.2 = (f32[19,512]{1,0:T(8,128)S(1)}, f32[19,512]{1,0:T(8,128)S(1)}, u32[]{:S(2)}, u32[]{:S(2)}) collective-permute-start(f32[19,512]{1,0:T(8,128)S(1)} %get-tuple-element.27), channel_id=1, source_target_pairs={{0,3},{1,0},{2,1},{3,2},{4,7},{5,4},{6,5},{7,6},{8,11},{9,8},{10,9... | collective-permute-start | bytes 116744 | tf_op jit(solution)/shard_map/ppermute | solution.py:167
Sparse Core Ops, SparseCore 0:
  10.3 94.5 all-gather.2
